TPU v7x, 256 devices: a whole 4x4x8 slice. The times are simulated.
256 devices in a mesh: pipe: 8 (over z), seq: 8 (over y, core), mp: 4 (over x).
Axes of the slice: x: 4, y: 4, z: 8, core: 2. Of those that a mesh axis runs over, the one named last changes fastest.
Arguments:
- shared_fwd: bfloat16 [8, 2048, 3072], P('pipe', ('seq', 'mp')), may hold values from -7.5 to 7.5
- values_fwd: bfloat16 [8, 2048, 3072], P('pipe', ('seq', 'mp')), may hold values from -6 to 6
- shared_bwd: bfloat16 [8, 2048, 3072], P('pipe', ('seq', 'mp')), may hold values from -7.5 to 7.5
- values_bwd: bfloat16 [8, 2048, 3072], P('pipe', ('seq', 'mp')), may hold values from -6 to 6
- upstream_bwd: bfloat16 [8, 2048, 3072], P('pipe', ('seq', 'mp')), may hold values from -6 to 6
- cluster_order: int32 [8, 2, 2048], P('pipe'), may hold values from 0 to 2047, as said below
Outputs:
- forward_in: bfloat16 [8, 2048, 3072], P('pipe', ('seq', 'mp'))
- shared_grad_in: bfloat16 [8, 2048, 3072], P('pipe', ('seq', 'mp'))
- values_grad_in: bfloat16 [8, 2048, 3072], P('pipe', ('seq', 'mp'))
Inputs may be any that keep to these rules, and one draw needn't show every extreme that they name: cluster_order[l, b] is a permutation of the token positions for every layer l and micro-batch b. Cut the slots into blocks of 256 and the positions into ranges of 64: each range fills 0, 8 or 16 slots of each block, and some range fills 16 in some block.
All inputs are finite; a program needn't handle non-finite values.
Results may differ from a plain program's by a relative error of at most 0.007.
Values may be sent and summed in bfloat16 or wider, within the bound.
No kernel may reach another device: no remote copies, remote signals or barrier semaphores. Data moves between devices by JAX's collectives and lax.ppermute only.
A program may use at most 64 MiB of HBM per device.

v0:
```python
import math

import jax
import jax.numpy as jnp
from jax import lax
from jax.sharding import PartitionSpec as P

HEAD_DIM = 128
CLUSTER = 256


MASKED = -1e30


def shifted(block, axis, distance):
    devices = range(lax.axis_size(axis))
    route = [(i - distance, i) for i in devices if i - distance in devices]
    return lax.ppermute(block, axis, route)


def visible_mask(positions):
    count = positions.shape[1]
    earlier = positions[:, None, :] < positions[:, :, None]
    earliest = positions == jnp.min(positions, axis=1, keepdims=True)
    diagonal = (jnp.arange(count)[:, None] == jnp.arange(count)[None, :])[None]
    return earlier | diagonal & earliest[:, :, None]


def softmax_weights(shared, positions, score_scale):
    scores = (
        jnp.einsum("nqhd,nkhd->nhqk", shared, shared, preferred_element_type=jnp.float32)
        * score_scale
    )
    scores = jnp.where(visible_mask(positions)[:, None], scores, MASKED)
    largest = jnp.max(scores, axis=-1, keepdims=True)
    exponent = jnp.exp(scores - largest)
    return exponent / jnp.sum(exponent, axis=-1, keepdims=True)


def forward_block(shared, values, positions, score_scale):
    weights = softmax_weights(shared, positions, score_scale).astype(jnp.bfloat16)
    return jnp.einsum(
        "nhqk,nkhd->nqhd", weights, values, preferred_element_type=jnp.float32
    ).astype(jnp.bfloat16)


def backward_block(shared, values, upstream, positions, score_scale):
    weights = softmax_weights(shared, positions, score_scale)
    rounded = weights.astype(jnp.bfloat16)
    output_b = jnp.einsum("nhqk,nkhd->nqhd", rounded, values, preferred_element_type=jnp.float32)
    row_delta = jnp.sum(upstream.astype(jnp.float32) * output_b, axis=-1)
    value_grad = jnp.einsum(
        "nhqk,nqhd->nkhd", rounded, upstream, preferred_element_type=jnp.float32
    ).astype(jnp.bfloat16)
    prob_grad = jnp.einsum("nqhd,nkhd->nhqk", upstream, values, preferred_element_type=jnp.float32)
    score_grad = (
        weights * (prob_grad - jnp.transpose(row_delta, (0, 2, 1))[..., None]) * score_scale
    ).astype(jnp.bfloat16)
    shared_grad = jnp.einsum(
        "nhqk,nkhd->nqhd", score_grad, shared, preferred_element_type=jnp.float32
    )
    shared_grad = shared_grad + jnp.einsum(
        "nhqk,nqhd->nkhd", score_grad, shared, preferred_element_type=jnp.float32
    )
    return (shared_grad.astype(jnp.bfloat16), value_grad)


def route_plan(slot_tokens, seq_index, range_here, seq_count, group_count, tok_dev, slot_count):
    block_rows = slot_tokens.shape[0] // seq_count
    source = slot_tokens // tok_dev
    local_row = (slot_tokens - range_here * tok_dev).reshape(seq_count, block_rows)
    owned_here = (source == range_here).reshape(seq_count, block_rows)
    slot_rank = jnp.cumsum(owned_here.astype(jnp.int32), axis=1) - 1
    selected = owned_here[:, None, :] & (
        slot_rank[:, None, :] == jnp.arange(slot_count)[None, :, None]
    )
    send_rows = jnp.sum(jnp.where(selected, local_row[:, None, :], 0), axis=2)
    filled = jnp.any(selected, axis=2)
    send = filled[:, :, None] & (send_rows[:, :, None] == jnp.arange(tok_dev)[None, None, :])
    block_order = lax.dynamic_slice_in_dim(slot_tokens, seq_index * block_rows, block_rows)
    block_source = block_order // tok_dev
    indicator = (block_source[:, None] == jnp.arange(group_count)[None, :]).astype(jnp.int32)
    block_rank = jnp.sum(jnp.cumsum(indicator, axis=0) * indicator, axis=1) - 1
    gather = (block_source[:, None, None] == jnp.arange(group_count)[None, :, None]) & (
        block_rank[:, None, None] == jnp.arange(slot_count)[None, None, :]
    )
    return (
        send.astype(jnp.bfloat16),
        gather.astype(jnp.bfloat16),
        block_order,
    )


def per_device(shared_fwd, values_fwd, shared_bwd, values_bwd, upstream_bwd, cluster_order):
    seq_count = lax.axis_size("seq")
    mp_count = lax.axis_size("mp")
    seq_index = lax.axis_index("seq")
    mp_index = lax.axis_index("mp")
    tok_dev = shared_fwd.shape[1]
    features = shared_fwd.shape[2]
    group_features = features // mp_count
    heads_dev = group_features // HEAD_DIM
    group_count = seq_count * mp_count
    range_here = seq_index * mp_count + mp_index
    block_rows = cluster_order.shape[2] // seq_count
    slot_count = 2 * block_rows // group_count
    score_scale = 1.0 / math.sqrt(HEAD_DIM)
    axes = ("seq", "mp")
    plan_fwd = route_plan(
        cluster_order[0, 0], seq_index, range_here, seq_count, group_count, tok_dev, slot_count
    )
    plan_bwd = route_plan(
        cluster_order[0, 1], seq_index, range_here, seq_count, group_count, tok_dev, slot_count
    )

    def exchange(arrays, send):
        packed = [
            jnp.einsum(
                "skt,tmf->smkf",
                send,
                array[0].reshape(tok_dev, mp_count, group_features),
                preferred_element_type=jnp.bfloat16,
            )
            for array in arrays
        ]
        stacked = jnp.stack(packed, axis=2).reshape(
            group_count, len(arrays), slot_count, group_features
        )
        return lax.all_to_all(stacked, axes, split_axis=0, concat_axis=0, tiled=True)

    def gather_block(arrived, gather):
        rows = jnp.einsum("irk,rakf->aif", gather, arrived, preferred_element_type=jnp.bfloat16)
        return [row.reshape(1, block_rows, heads_dev, HEAD_DIM) for row in rows]

    def give_back(results, gather, send):
        flat = jnp.stack([r.reshape(block_rows, group_features) for r in results], axis=0)
        placed = jnp.einsum("irk,aif->rakf", gather, flat, preferred_element_type=jnp.bfloat16)
        arrived = lax.all_to_all(placed, axes, split_axis=0, concat_axis=0, tiled=True)
        arrived = arrived.reshape(seq_count, mp_count, len(results), slot_count, group_features)
        rows = jnp.einsum("skt,smakf->atmf", send, arrived, preferred_element_type=jnp.bfloat16)
        return [row.reshape(1, tok_dev, features) for row in rows]

    arrived_f = exchange((shared_fwd, values_fwd), plan_fwd[0])
    arrived_b = exchange((shared_bwd, values_bwd, upstream_bwd), plan_bwd[0])
    positions_f = plan_fwd[2].reshape(-1, CLUSTER)
    positions_b = plan_bwd[2].reshape(-1, CLUSTER)
    shared_f, values_f = gather_block(arrived_f, plan_fwd[1])
    attended = forward_block(shared_f, values_f, positions_f, score_scale)
    (forward_out,) = give_back((attended,), plan_fwd[1], plan_fwd[0])
    forward_in = shifted(forward_out, "pipe", 1)
    shared_b, values_b, upstream_b = gather_block(arrived_b, plan_bwd[1])
    shared_grad, value_grad = backward_block(shared_b, values_b, upstream_b, positions_b, score_scale)
    shared_out, values_out = give_back((shared_grad, value_grad), plan_bwd[1], plan_bwd[0])
    shared_grad_in, values_grad_in = shifted((shared_out, values_out), "pipe", -1)
    return (forward_in, shared_grad_in, values_grad_in)


def solution(mesh):
    in_specs = (
        P("pipe", ("seq", "mp"), None),
        P("pipe", ("seq", "mp"), None),
        P("pipe", ("seq", "mp"), None),
        P("pipe", ("seq", "mp"), None),
        P("pipe", ("seq", "mp"), None),
        P("pipe", None, None),
    )
    out_specs = (
        P("pipe", ("seq", "mp"), None),
        P("pipe", ("seq", "mp"), None),
        P("pipe", ("seq", "mp"), None),
    )
    return jax.shard_map(
        per_device, mesh=mesh, in_specs=in_specs, out_specs=out_specs, check_vma=False
    )
```

profile of v0, /device:TPU:96, one launch (start us, length us, event | category | flops | bytes accessed | tf_op | source)
XLA Modules:
  0.0 143.0 jit_solution(15337795594115509562)
XLA Ops:
  3.0 1.3 reshape_squeeze.15
  6.4 1.3 pad_maximum_fusion.1
  7.7 7.6 %all-to-all-start = ((bf16[32,2,16,768]{3,2,1,0:T(8,128)(2,1)}), bf16[32,2,16,768]{3,2,1,0:T(8,128)(2,1)}, u32[]{:S(2)}, u32[]{:S(2)}) async-start(bf16[32,2,16,768]{3,2,1,0:T(8,128)(2,1)} %pad_maximum_fusion.1), calls=%async_computation | async-start | bytes 3145728 | tf_op jit(solution)/shard_map/all_to_all | solution.py:129
  22.7 1.7 %pad_maximum_fusion = bf16[32,3,16,768]{3,2,1,0:T(8,128)(2,1)} fusion(bf16[32,1,16,768]{3,2,1,0:T(8,128)(2,1)S(1)} %bitcast.208, bf16[32,1,16,768]{3,2,1,0:T(8,128)(2,1)S(1)} %bitcast.207, bf16[32,1,16,768]{3,2,1,0:T(8,128)(2,1)S(1)} %bitcast.206), kind=kLoop, calls=%fused_computation.2 | loop fusion | flops 2359296 | bytes 4718592 | tf_op jit(solution)/shard_map/stack | solution.py:126
  24.6 13.1 %all-to-all-done = bf16[32,2,16,768]{3,2,1,0:T(8,128)(2,1)} async-done(((bf16[32,2,16,768]{3,2,1,0:T(8,128)(2,1)}), bf16[32,2,16,768]{3,2,1,0:T(8,128)(2,1)}, u32[]{:S(2)}, u32[]{:S(2)}) %all-to-all-start) | async-done | bytes 1572896 | tf_op jit(solution)/shard_map/all_to_all | solution.py:129
  37.8 4.3 %all-to-all-start.2 = ((bf16[32,3,16,768]{3,2,1,0:T(8,128)(2,1)}), bf16[32,3,16,768]{3,2,1,0:T(8,128)(2,1)S(1)}, u32[]{:S(2)}, u32[]{:S(2)}) async-start(bf16[32,3,16,768]{3,2,1,0:T(8,128)(2,1)} %pad_maximum_fusion), calls=%async_computation.2 | async-start | bytes 4718592 | tf_op jit(solution)/shard_map/all_to_all | solution.py:129
  42.3 2.0 %convolution_bitcast_fusion.3 = bf16[2,256,768]{1,2,0:T(8,128)(2,1)S(1)} fusion(bf16[32,2,16,768]{3,2,1,0:T(8,128)(2,1)} %all-to-all-done, pred[256,32,16,1]{0,1,2,3:T(32,128)(4,1)S(1)} %and_bitcast_fusion), kind=kOutput, calls=%fused_computation.15 | convolution fusion | flops 402653184 | bytes 2490368 | tf_op jit(solution)/shard_map/irk,rakf->aif/dot_general | solution.py:132
  44.4 1.9 %fusion.101 = (f32[6,256]{1,0:T(8,128)S(1)}, f32[6,256,256]{1,2,0:T(8,128)}) fusion(bf16[256,6,128]{0,2,1:T(8,128)(2,1)S(1)} %bitcast.224, pred[256,256]{0,1:T(8,128)(4,1)S(1)} %fusion.33), kind=kOutput, calls=%fused_computation.183 | convolution fusion | flops 102236416 | bytes 2037760 | tf_op jit(solution)/shard_map/sub | solution.py:36
  46.3 1.7 %convolution_convert_fusion.1 = bf16[6,128,256]{2,1,0:T(8,128)(2,1)S(1)} fusion(bf16[256,6,128]{0,2,1:T(8,128)(2,1)S(1)} %bitcast.223, f32[6,256,256]{1,2,0:T(8,128)} %get-tuple-element.19, f32[6,256]{1,0:T(8,128)S(1)} %get-tuple-element.18), kind=kOutput, calls=%fused_computation.21 | convolution fusion | flops 101646336 | bytes 2365440 | tf_op jit(solution)/shard_map/nhqk,nkhd->nqhd/dot_general | solution.py:42
  48.4 1.3 copy.176
  49.7 22.7 %all-to-all-done.2 = bf16[32,3,16,768]{3,2,1,0:T(8,128)(2,1)S(1)} async-done(((bf16[32,3,16,768]{3,2,1,0:T(8,128)(2,1)}), bf16[32,3,16,768]{3,2,1,0:T(8,128)(2,1)S(1)}, u32[]{:S(2)}, u32[]{:S(2)}) %all-to-all-start.2) | async-done | bytes 2359328 | tf_op jit(solution)/shard_map/all_to_all | solution.py:129
  72.4 5.0 %all-to-all-start.1 = ((bf16[32,1,16,768]{3,2,1,0:T(8,128)(2,1)}), bf16[32,1,16,768]{3,2,1,0:T(8,128)(2,1)S(1)}, u32[]{:S(2)}, u32[]{:S(2)}) async-start(bf16[32,1,16,768]{3,2,1,0:T(8,128)(2,1)} %copy.176), calls=%async_computation.1 | async-start | bytes 1572864 | tf_op jit(solution)/shard_map/all_to_all | solution.py:138
  78.4 1.9 %fusion.102 = (f32[6,256]{1,0:T(8,128)S(1)}, f32[6,256,256]{1,2,0:T(8,128)}) fusion(bf16[256,6,128]{0,2,1:T(8,128)(2,1)S(1)} %bitcast.203, pred[256,256]{0,1:T(8,128)(4,1)S(1)} %fusion.34), kind=kOutput, calls=%fused_computation.184 | convolution fusion | flops 102236416 | bytes 2037760 | tf_op jit(solution)/shard_map/sub | solution.py:36
  80.2 1.8 %fusion.8 = f32[256,6]{0,1:T(8,128)S(1)} fusion(bf16[256,6,128]{0,2,1:T(8,128)(2,1)S(1)} %bitcast.217, bf16[1,256,6,128]{1,3,2,0:T(8,128)(2,1)S(1)} %bitcast.214, f32[6,256,256]{1,2,0:T(8,128)} %get-tuple-element.21, f32[6,256]{1,0:T(8,128)S(1)} %get-tuple-element.20), kind=kOutput, calls=%fused_computation.22 | convolution fusion | flops 102038016 | bytes 2371584 | tf_op jit(solution)/shard_map/nhqk,nkhd->nqhd/dot_general | solution.py:50
  83.4 1.8 %convolution_convert_fusion = bf16[6,128,256]{2,1,0:T(8,128)(2,1)S(1)} fusion(bf16[256,6,128]{0,2,1:T(8,128)(2,1)S(1)} %bitcast.216, f32[6,256,256]{1,2,0:T(8,128)} %get-tuple-element.21, f32[6,256]{1,0:T(8,128)S(1)} %get-tuple-element.20), kind=kOutput, calls=%fused_computation.20 | convolution fusion | flops 101646336 | bytes 2365440 | tf_op jit(solution)/shard_map/nhqk,nqhd->nkhd/dot_general | solution.py:52
  86.0 2.0 %copy.201 = bf16[32,2,16,768]{3,2,1,0:T(8,128)(2,1)} copy(bf16[32,2,16,768]{3,0,2,1:T(8,128)(2,1)S(1)} %convolution_bitcast_fusion) | data formatting | bytes 3145728 | tf_op jit(solution)/shard_map/irk,aif->rakf/transpose | solution.py:137
  88.0 3.6 %all-to-all-done.1 = bf16[32,1,16,768]{3,2,1,0:T(8,128)(2,1)S(1)} async-done(((bf16[32,1,16,768]{3,2,1,0:T(8,128)(2,1)}), bf16[32,1,16,768]{3,2,1,0:T(8,128)(2,1)S(1)}, u32[]{:S(2)}, u32[]{:S(2)}) %all-to-all-start.1) | async-done | bytes 786464 | tf_op jit(solution)/shard_map/all_to_all | solution.py:138
  91.6 4.0 %all-to-all-start.3 = ((bf16[32,2,16,768]{3,2,1,0:T(8,128)(2,1)}), bf16[32,2,16,768]{3,2,1,0:T(8,128)(2,1)S(1)}, u32[]{:S(2)}, u32[]{:S(2)}) async-start(bf16[32,2,16,768]{3,2,1,0:T(8,128)(2,1)} %copy.201), calls=%async_computation.3 | async-start | bytes 3145728 | tf_op jit(solution)/shard_map/all_to_all | solution.py:138
  96.1 5.0 %collective-permute-start = (bf16[1,64,3072]{2,1,0:T(8,128)(2,1)S(1)}, bf16[1,64,3072]{2,1,0:T(8,128)(2,1)S(1)}, u32[]{:S(2)}, u32[]{:S(2)}) collective-permute-start(bf16[1,64,3072]{2,1,0:T(8,128)(2,1)S(1)} %bitcast.219), channel_id=1, source_target_pairs={{0,32},{32,64},{64,96},{96,128},{128,160},{160,192},{192,224},{1,3... | collective-permute-start | bytes 1179656 | tf_op jit(solution)/shard_map/ppermute | solution.py:18
  101.1 17.0 %all-to-all-done.3 = bf16[32,2,16,768]{3,2,1,0:T(8,128)(2,1)S(1)} async-done(((bf16[32,2,16,768]{3,2,1,0:T(8,128)(2,1)}), bf16[32,2,16,768]{3,2,1,0:T(8,128)(2,1)S(1)}, u32[]{:S(2)}, u32[]{:S(2)}) %all-to-all-start.3) | async-done | bytes 1572896 | tf_op jit(solution)/shard_map/all_to_all | solution.py:138
  118.8 2.0 %collective-permute-start.1 = (bf16[1,64,3072]{2,1,0:T(8,128)(2,1)S(1)}, bf16[1,64,3072]{2,1,0:T(8,128)(2,1)S(1)}, u32[]{:S(2)}, u32[]{:S(2)}) collective-permute-start(bf16[1,64,3072]{2,1,0:T(8,128)(2,1)S(1)} %bitcast.220), channel_id=1, source_target_pairs={{32,0},{64,32},{96,64},{128,96},{160,128},{192,160},{224,192},{33,... | collective-permute-start | bytes 1179656 | tf_op jit(solution)/shard_map/ppermute | solution.py:18
  120.9 2.0 %collective-permute-start.2 = (bf16[1,64,3072]{2,1,0:T(8,128)(2,1)S(1)}, bf16[1,64,3072]{2,1,0:T(8,128)(2,1)S(1)}, u32[]{:S(2)}, u32[]{:S(2)}) collective-permute-start(bf16[1,64,3072]{2,1,0:T(8,128)(2,1)S(1)} %bitcast.221), channel_id=1, source_target_pairs={{32,0},{64,32},{96,64},{128,96},{160,128},{192,160},{224,192},{33,... | collective-permute-start | bytes 1179656 | tf_op jit(solution)/shard_map/ppermute | solution.py:18
  122.9 11.0 %collective-permute-done.1 = bf16[1,64,3072]{2,1,0:T(8,128)(2,1)S(1)} collective-permute-done((bf16[1,64,3072]{2,1,0:T(8,128)(2,1)S(1)}, bf16[1,64,3072]{2,1,0:T(8,128)(2,1)S(1)}, u32[]{:S(2)}, u32[]{:S(2)}) %collective-permute-start.1) | collective-permute-done | bytes 393248 | tf_op jit(solution)/shard_map/ppermute | solution.py:18
  133.9 6.8 %collective-permute-done.2 = bf16[1,64,3072]{2,1,0:T(8,128)(2,1)S(1)} collective-permute-done((bf16[1,64,3072]{2,1,0:T(8,128)(2,1)S(1)}, bf16[1,64,3072]{2,1,0:T(8,128)(2,1)S(1)}, u32[]{:S(2)}, u32[]{:S(2)}) %collective-permute-start.2) | collective-permute-done | bytes 393248 | tf_op jit(solution)/shard_map/ppermute | solution.py:18
  (87 shorter events, 18.9 us)
Async XLA Ops:
  7.7 9.0 %copy-start = (bf16[1,64,3072]{2,1,0:T(8,128)(2,1)S(1)}, bf16[1,64,3072]{2,1,0:T(8,128)(2,1)}, u32[]{:S(2)}) copy-start(bf16[1,64,3072]{2,1,0:T(8,128)(2,1)} %param.8) | copy-start | bytes 1179652
  7.7 9.3 %copy-start.1 = (bf16[1,64,3072]{2,1,0:T(8,128)(2,1)S(1)}, bf16[1,64,3072]{2,1,0:T(8,128)(2,1)}, u32[]{:S(2)}) copy-start(bf16[1,64,3072]{2,1,0:T(8,128)(2,1)} %param.9) | copy-start | bytes 1179652
  7.7 30.1 %all-to-all-start = ((bf16[32,2,16,768]{3,2,1,0:T(8,128)(2,1)}), bf16[32,2,16,768]{3,2,1,0:T(8,128)(2,1)}, u32[]{:S(2)}, u32[]{:S(2)}) async-start(bf16[32,2,16,768]{3,2,1,0:T(8,128)(2,1)} %pad_maximum_fusion.1), calls=%async_computation | async-start | bytes 3145728 | tf_op jit(solution)/shard_map/all_to_all | solution.py:129
  17.0 1.1 copy-start.2
  37.8 34.6 %all-to-all-start.2 = ((bf16[32,3,16,768]{3,2,1,0:T(8,128)(2,1)}), bf16[32,3,16,768]{3,2,1,0:T(8,128)(2,1)S(1)}, u32[]{:S(2)}, u32[]{:S(2)}) async-start(bf16[32,3,16,768]{3,2,1,0:T(8,128)(2,1)} %pad_maximum_fusion), calls=%async_computation.2 | async-start | bytes 4718592 | tf_op jit(solution)/shard_map/all_to_all | solution.py:129
  72.4 19.2 %all-to-all-start.1 = ((bf16[32,1,16,768]{3,2,1,0:T(8,128)(2,1)}), bf16[32,1,16,768]{3,2,1,0:T(8,128)(2,1)S(1)}, u32[]{:S(2)}, u32[]{:S(2)}) async-start(bf16[32,1,16,768]{3,2,1,0:T(8,128)(2,1)} %copy.176), calls=%async_computation.1 | async-start | bytes 1572864 | tf_op jit(solution)/shard_map/all_to_all | solution.py:138
  80.2 1.9 %copy-start.3 = (f32[6,256,256]{1,2,0:T(8,128)S(1)}, f32[6,256,256]{1,2,0:T(8,128)}, u32[]{:S(2)}) copy-start(f32[6,256,256]{1,2,0:T(8,128)} %get-tuple-element.21) | copy-start | bytes 4718596
  91.6 26.6 %all-to-all-start.3 = ((bf16[32,2,16,768]{3,2,1,0:T(8,128)(2,1)}), bf16[32,2,16,768]{3,2,1,0:T(8,128)(2,1)S(1)}, u32[]{:S(2)}, u32[]{:S(2)}) async-start(bf16[32,2,16,768]{3,2,1,0:T(8,128)(2,1)} %copy.201), calls=%async_computation.3 | async-start | bytes 3145728 | tf_op jit(solution)/shard_map/all_to_all | solution.py:138
  96.1 26.8 %collective-permute-start = (bf16[1,64,3072]{2,1,0:T(8,128)(2,1)S(1)}, bf16[1,64,3072]{2,1,0:T(8,128)(2,1)S(1)}, u32[]{:S(2)}, u32[]{:S(2)}) collective-permute-start(bf16[1,64,3072]{2,1,0:T(8,128)(2,1)S(1)} %bitcast.219), channel_id=1, source_target_pairs={{0,32},{32,64},{64,96},{96,128},{128,160},{160,192},{192,224},{1,3... | collective-permute-start | bytes 1179656 | tf_op jit(solution)/shard_map/ppermute | solution.py:18
  118.8 15.1 %collective-permute-start.1 = (bf16[1,64,3072]{2,1,0:T(8,128)(2,1)S(1)}, bf16[1,64,3072]{2,1,0:T(8,128)(2,1)S(1)}, u32[]{:S(2)}, u32[]{:S(2)}) collective-permute-start(bf16[1,64,3072]{2,1,0:T(8,128)(2,1)S(1)} %bitcast.220), channel_id=1, source_target_pairs={{32,0},{64,32},{96,64},{128,96},{160,128},{192,160},{224,192},{33,... | collective-permute-start | bytes 1179656 | tf_op jit(solution)/shard_map/ppermute | solution.py:18
  120.9 19.9 %collective-permute-start.2 = (bf16[1,64,3072]{2,1,0:T(8,128)(2,1)S(1)}, bf16[1,64,3072]{2,1,0:T(8,128)(2,1)S(1)}, u32[]{:S(2)}, u32[]{:S(2)}) collective-permute-start(bf16[1,64,3072]{2,1,0:T(8,128)(2,1)S(1)} %bitcast.221), channel_id=1, source_target_pairs={{32,0},{64,32},{96,64},{128,96},{160,128},{192,160},{224,192},{33,... | collective-permute-start | bytes 1179656 | tf_op jit(solution)/shard_map/ppermute | solution.py:18
where the time goes:
time: 144 us; the launch traced here: 143 us
  waiting for transfers between devices  74.3 us (52%)
  starting transfers between devices  30 us (21%)
  matrix products  17 us (12%)
  local copies, waits for them, and re-layouts  11.4 us (8%)
  other arithmetic  9.17 us (6%)
    all_to_all x2, waiting for transfers between devices, exchange(): lax.all_to_all(stacked, axes, split_axis=0, concat_axis=0, tiled=True)  35.8 us
    all_to_all x2, waiting for transfers between devices, give_back(): lax.all_to_all(placed, axes, split_axis=0, concat_axis=0, tiled=True)  20.6 us
    ppermute x3, waiting for transfers between devices, shifted(): return lax.ppermute(block, axis, route)  17.8 us
    all_to_all x2, starting transfers between devices, exchange(): lax.all_to_all(stacked, axes, split_axis=0, concat_axis=0, tiled=True)  11.9 us
    ppermute x3, starting transfers between devices, shifted(): return lax.ppermute(block, axis, route)  9.07 us
    all_to_all x2, starting transfers between devices, give_back(): lax.all_to_all(placed, axes, split_axis=0, concat_axis=0, tiled=True)  9.04 us
    sub x2, matrix products, softmax_weights(): exponent = jnp.exp(scores - largest)  3.73 us
    another operation x5, local copies, waits for them, and re-layouts, exchange(): array[0].reshape(tok_dev, mp_count, group_features)  3.41 us
  transfers between devices with their start and end apart: 7, of which 6 were waited for; matrix products, arithmetic and copies ran while one was open for 20% of the time, Pallas kernels for 0%

commit v1 on v0

--- a/solution.py
+++ b/solution.py
@@ -140,18 +140,21 @@
         rows = jnp.einsum("skt,smakf->atmf", send, arrived, preferred_element_type=jnp.bfloat16)
         return [row.reshape(1, tok_dev, features) for row in rows]
 
-    arrived_f = exchange((shared_fwd, values_fwd), plan_fwd[0])
-    arrived_b = exchange((shared_bwd, values_bwd, upstream_bwd), plan_bwd[0])
     positions_f = plan_fwd[2].reshape(-1, CLUSTER)
     positions_b = plan_bwd[2].reshape(-1, CLUSTER)
+    arrived_b = exchange((shared_bwd, values_bwd, upstream_bwd), plan_bwd[0])
+    arrived_b, shared_fwd, values_fwd = lax.optimization_barrier((arrived_b, shared_fwd, values_fwd))
+    arrived_f = exchange((shared_fwd, values_fwd), plan_fwd[0])
+    shared_b, values_b, upstream_b = gather_block(arrived_b, plan_bwd[1])
+    shared_grad, value_grad = backward_block(shared_b, values_b, upstream_b, positions_b, score_scale)
+    shared_grad, value_grad, arrived_f = lax.optimization_barrier((shared_grad, value_grad, arrived_f))
+    shared_out, values_out = give_back((shared_grad, value_grad), plan_bwd[1], plan_bwd[0])
     shared_f, values_f = gather_block(arrived_f, plan_fwd[1])
     attended = forward_block(shared_f, values_f, positions_f, score_scale)
+    attended, shared_out, values_out = lax.optimization_barrier((attended, shared_out, values_out))
+    shared_grad_in, values_grad_in = shifted((shared_out, values_out), "pipe", -1)
     (forward_out,) = give_back((attended,), plan_fwd[1], plan_fwd[0])
     forward_in = shifted(forward_out, "pipe", 1)
-    shared_b, values_b, upstream_b = gather_block(arrived_b, plan_bwd[1])
-    shared_grad, value_grad = backward_block(shared_b, values_b, upstream_b, positions_b, score_scale)
-    shared_out, values_out = give_back((shared_grad, value_grad), plan_bwd[1], plan_bwd[0])
-    shared_grad_in, values_grad_in = shifted((shared_out, values_out), "pipe", -1)
     return (forward_in, shared_grad_in, values_grad_in)
 
 

time: 144 us -> 148 us (1.028)
  local copies, waits for them, and re-layouts: 11.4 us -> 15.1 us
  matrix products: 17 us -> 14.2 us
    ppermute x3, waiting for transfers between devices: 17.8 us -> 8.11 us  [shifted(): return lax.ppermute(block, axis, route)]
    all_to_all x2, waiting for transfers between devices: 20.6 us -> 27.8 us  [give_back(): lax.all_to_all(placed, axes, split_axis=0, concat_axis=0, tiled=True)]
    all_to_all x2, waiting for transfers between devices: 35.8 us -> 39.8 us  [exchange(): lax.all_to_all(stacked, axes, split_axis=0, concat_axis=0, tiled=True)]
    unnamed x12 -> x40, local copies, waits for them, and re-layouts: 2.36 us -> 3.87 us
  transfers between devices with their start and end apart: 7 -> 7, of which waited for: 6 -> 6; matrix products, arithmetic and copies ran while one was open for 20% -> 12% of each run, Pallas kernels for 0% -> 0%
where the time goes in v1:
time: 148 us; the launch traced here: 146 us
  waiting for transfers between devices  75.7 us (51%)
  starting transfers between devices  30.1 us (20%)
  local copies, waits for them, and re-layouts  15.1 us (10%)
  matrix products  14.2 us (10%)
  other arithmetic  9.89 us (7%)
    all_to_all x2, waiting for transfers between devices, exchange(): lax.all_to_all(stacked, axes, split_axis=0, concat_axis=0, tiled=True)  39.8 us
    all_to_all x2, waiting for transfers between devices, give_back(): lax.all_to_all(placed, axes, split_axis=0, concat_axis=0, tiled=True)  27.8 us
    all_to_all x2, starting transfers between devices, exchange(): lax.all_to_all(stacked, axes, split_axis=0, concat_axis=0, tiled=True)  12.3 us
    ppermute x3, starting transfers between devices, shifted(): return lax.ppermute(block, axis, route)  9.07 us
    all_to_all x2, starting transfers between devices, give_back(): lax.all_to_all(placed, axes, split_axis=0, concat_axis=0, tiled=True)  8.79 us
    ppermute x3, waiting for transfers between devices, shifted(): return lax.ppermute(block, axis, route)  8.11 us
    unnamed x40, local copies, waits for them, and re-layouts  3.87 us
    sub x2, matrix products, softmax_weights(): exponent = jnp.exp(scores - largest)  3.71 us
  transfers between devices with their start and end apart: 7, of which 6 were waited for; matrix products, arithmetic and copies ran while one was open for 12% of the time, Pallas kernels for 0%

profile of v1, /device:TPU:96, one launch (start us, length us, event | category | flops | bytes accessed | tf_op | source)
XLA Modules:
  0.0 146.3 jit_solution(7934049616116018385)
XLA Ops:
  1.6 1.3 reshape_squeeze.17
  4.3 1.3 reshape_squeeze.16
  7.2 1.7 %pad_maximum_fusion = bf16[32,3,16,768]{3,2,1,0:T(8,128)(2,1)} fusion(bf16[32,1,16,768]{3,2,1,0:T(8,128)(2,1)S(1)} %bitcast.199, bf16[32,1,16,768]{3,2,1,0:T(8,128)(2,1)S(1)} %bitcast.200, bf16[32,1,16,768]{3,2,1,0:T(8,128)(2,1)S(1)} %bitcast.201), kind=kLoop, calls=%fused_computation.2 | loop fusion | flops 2359296 | bytes 4718592 | tf_op jit(solution)/shard_map/stack | solution.py:126
  8.8 7.3 %all-to-all-start = ((bf16[32,3,16,768]{3,2,1,0:T(8,128)(2,1)}), bf16[32,3,16,768]{3,2,1,0:T(8,128)(2,1)S(1)}, u32[]{:S(2)}, u32[]{:S(2)}) async-start(bf16[32,3,16,768]{3,2,1,0:T(8,128)(2,1)} %pad_maximum_fusion), calls=%async_computation | async-start | bytes 4718592 | tf_op jit(solution)/shard_map/all_to_all | solution.py:129
  23.8 22.6 %all-to-all-done = bf16[32,3,16,768]{3,2,1,0:T(8,128)(2,1)S(1)} async-done(((bf16[32,3,16,768]{3,2,1,0:T(8,128)(2,1)}), bf16[32,3,16,768]{3,2,1,0:T(8,128)(2,1)S(1)}, u32[]{:S(2)}, u32[]{:S(2)}) %all-to-all-start) | async-done | bytes 2359328 | tf_op jit(solution)/shard_map/all_to_all | solution.py:129
  46.4 0.9 convolution_bitcast_fusion.1
  50.6 1.3 copy.193
  51.9 4.9 %all-to-all-start.1 = ((bf16[32,2,16,768]{3,2,1,0:T(8,128)(2,1)}), bf16[32,2,16,768]{3,2,1,0:T(8,128)(2,1)S(1)}, u32[]{:S(2)}, u32[]{:S(2)}) async-start(bf16[32,2,16,768]{3,2,1,0:T(8,128)(2,1)} %copy.193), calls=%async_computation.1 | async-start | bytes 3145728 | tf_op jit(solution)/shard_map/all_to_all | solution.py:129
  56.9 1.9 %fusion.101 = (f32[6,256]{1,0:T(8,128)S(1)}, f32[6,256,256]{1,2,0:T(8,128)}) fusion(bf16[256,6,128]{0,2,1:T(8,128)(2,1)S(1)} %bitcast.196, pred[256,256]{0,1:T(8,128)(4,1)S(1)} %copy-done.8), kind=kOutput, calls=%fused_computation.185 | convolution fusion | flops 102236416 | bytes 2037760 | tf_op jit(solution)/shard_map/sub | solution.py:36
  58.7 1.8 %fusion.8 = f32[256,6]{0,1:T(8,128)S(1)} fusion(bf16[256,6,128]{0,2,1:T(8,128)(2,1)S(1)} %bitcast.212, bf16[1,256,6,128]{1,3,2,0:T(8,128)(2,1)S(1)} %bitcast.209, f32[6,256,256]{1,2,0:T(8,128)} %get-tuple-element.37, f32[6,256]{1,0:T(8,128)S(1)} %get-tuple-element.36), kind=kOutput, calls=%fused_computation.24 | convolution fusion | flops 102038016 | bytes 2371584 | tf_op jit(solution)/shard_map/nhqk,nkhd->nqhd/dot_general | solution.py:50
  62.2 17.2 %all-to-all-done.1 = bf16[32,2,16,768]{3,2,1,0:T(8,128)(2,1)S(1)} async-done(((bf16[32,2,16,768]{3,2,1,0:T(8,128)(2,1)}), bf16[32,2,16,768]{3,2,1,0:T(8,128)(2,1)S(1)}, u32[]{:S(2)}, u32[]{:S(2)}) %all-to-all-start.1) | async-done | bytes 1572896 | tf_op jit(solution)/shard_map/all_to_all | solution.py:129
  80.3 2.0 %copy.201 = bf16[32,2,16,768]{3,2,1,0:T(8,128)(2,1)} copy(bf16[32,2,16,768]{3,0,2,1:T(8,128)(2,1)S(1)} %convolution_bitcast_fusion) | data formatting | bytes 3145728 | tf_op jit(solution)/shard_map/irk,aif->rakf/transpose | solution.py:137
  82.3 4.5 %all-to-all-start.2 = ((bf16[32,2,16,768]{3,2,1,0:T(8,128)(2,1)}), bf16[32,2,16,768]{3,2,1,0:T(8,128)(2,1)S(1)}, u32[]{:S(2)}, u32[]{:S(2)}) async-start(bf16[32,2,16,768]{3,2,1,0:T(8,128)(2,1)} %copy.201), calls=%async_computation.2 | async-start | bytes 3145728 | tf_op jit(solution)/shard_map/all_to_all | solution.py:138
  88.4 1.9 %fusion.102 = (f32[6,256]{1,0:T(8,128)S(1)}, f32[6,256,256]{1,2,0:T(8,128)}) fusion(bf16[256,6,128]{0,2,1:T(8,128)(2,1)S(1)} %bitcast.220, pred[256,256]{0,1:T(8,128)(4,1)S(1)} %copy-done.7), kind=kOutput, calls=%fused_computation.186 | convolution fusion | flops 102236416 | bytes 2037760 | tf_op jit(solution)/shard_map/sub | solution.py:36
  90.2 1.7 %fusion.11 = bf16[1,256,6,128]{1,3,2,0:T(8,128)(2,1)S(1)} fusion(bf16[256,6,128]{0,2,1:T(8,128)(2,1)S(1)} %bitcast.219, f32[6,256,256]{1,2,0:T(8,128)} %get-tuple-element.39, f32[6,256]{1,0:T(8,128)S(1)} %get-tuple-element.38), kind=kOutput, calls=%fused_computation.27 | convolution fusion | flops 101646336 | bytes 2365440 | tf_op jit(solution)/shard_map/nhqk,nkhd->nqhd/dot_general | solution.py:42
  91.9 17.4 %all-to-all-done.2 = bf16[32,2,16,768]{3,2,1,0:T(8,128)(2,1)S(1)} async-done(((bf16[32,2,16,768]{3,2,1,0:T(8,128)(2,1)}), bf16[32,2,16,768]{3,2,1,0:T(8,128)(2,1)S(1)}, u32[]{:S(2)}, u32[]{:S(2)}) %all-to-all-start.2) | async-done | bytes 1572896 | tf_op jit(solution)/shard_map/all_to_all | solution.py:138
  110.4 1.3 copy.206
  111.8 4.3 %all-to-all-start.3 = ((bf16[32,1,16,768]{3,2,1,0:T(8,128)(2,1)}), bf16[32,1,16,768]{3,2,1,0:T(8,128)(2,1)S(1)}, u32[]{:S(2)}, u32[]{:S(2)}) async-start(bf16[32,1,16,768]{3,2,1,0:T(8,128)(2,1)} %copy.206), calls=%async_computation.3 | async-start | bytes 1572864 | tf_op jit(solution)/shard_map/all_to_all | solution.py:138
  116.1 2.0 %collective-permute-start.1 = (bf16[1,64,3072]{2,1,0:T(8,128)(2,1)S(1)}, bf16[1,64,3072]{2,1,0:T(8,128)(2,1)S(1)}, u32[]{:S(2)}, u32[]{:S(2)}) collective-permute-start(bf16[1,64,3072]{2,1,0:T(8,128)(2,1)S(1)} %bitcast.215), channel_id=1, source_target_pairs={{32,0},{64,32},{96,64},{128,96},{160,128},{192,160},{224,192},{33,... | collective-permute-start | bytes 1179656 | tf_op jit(solution)/shard_map/ppermute | solution.py:18
  118.1 2.0 %collective-permute-start.2 = (bf16[1,64,3072]{2,1,0:T(8,128)(2,1)S(1)}, bf16[1,64,3072]{2,1,0:T(8,128)(2,1)S(1)}, u32[]{:S(2)}, u32[]{:S(2)}) collective-permute-start(bf16[1,64,3072]{2,1,0:T(8,128)(2,1)S(1)} %bitcast.214), channel_id=1, source_target_pairs={{32,0},{64,32},{96,64},{128,96},{160,128},{192,160},{224,192},{33,... | collective-permute-start | bytes 1179656 | tf_op jit(solution)/shard_map/ppermute | solution.py:18
  120.1 10.4 %all-to-all-done.3 = bf16[32,1,16,768]{3,2,1,0:T(8,128)(2,1)S(1)} async-done(((bf16[32,1,16,768]{3,2,1,0:T(8,128)(2,1)}), bf16[32,1,16,768]{3,2,1,0:T(8,128)(2,1)S(1)}, u32[]{:S(2)}, u32[]{:S(2)}) %all-to-all-start.3) | async-done | bytes 786464 | tf_op jit(solution)/shard_map/all_to_all | solution.py:138
  130.9 5.0 %collective-permute-start = (bf16[1,64,3072]{2,1,0:T(8,128)(2,1)S(1)}, bf16[1,64,3072]{2,1,0:T(8,128)(2,1)S(1)}, u32[]{:S(2)}, u32[]{:S(2)}) collective-permute-start(bf16[1,64,3072]{2,1,0:T(8,128)(2,1)S(1)} %bitcast.216), channel_id=1, source_target_pairs={{0,32},{32,64},{64,96},{96,128},{128,160},{160,192},{192,224},{1,3... | collective-permute-start | bytes 1179656 | tf_op jit(solution)/shard_map/ppermute | solution.py:18
  136.0 3.1 %collective-permute-done.2 = bf16[1,64,3072]{2,1,0:T(8,128)(2,1)S(1)} collective-permute-done((bf16[1,64,3072]{2,1,0:T(8,128)(2,1)S(1)}, bf16[1,64,3072]{2,1,0:T(8,128)(2,1)S(1)}, u32[]{:S(2)}, u32[]{:S(2)}) %collective-permute-start.2) | collective-permute-done | bytes 393248 | tf_op jit(solution)/shard_map/ppermute | solution.py:18
  139.1 5.0 %collective-permute-done = bf16[1,64,3072]{2,1,0:T(8,128)(2,1)S(1)} collective-permute-done((bf16[1,64,3072]{2,1,0:T(8,128)(2,1)S(1)}, bf16[1,64,3072]{2,1,0:T(8,128)(2,1)S(1)}, u32[]{:S(2)}, u32[]{:S(2)}) %collective-permute-start) | collective-permute-done | bytes 393248 | tf_op jit(solution)/shard_map/ppermute | solution.py:18
  (118 shorter events, 22.2 us)
Async XLA Ops:
  4.0 2.7 %copy-start.11 = (pred[8,16]{1,0:T(8,128)(4,1)}, pred[8,16]{1,0:T(8,128)(4,1)S(1)}, u32[]{:S(2)}) copy-start(pred[8,16]{1,0:T(8,128)(4,1)S(1)} %fusion.37) | copy-start | bytes 388
  4.3 2.2 %copy-start.1 = (bf16[1,64,3072]{2,1,0:T(8,128)(2,1)S(1)}, bf16[1,64,3072]{2,1,0:T(8,128)(2,1)}, u32[]{:S(2)}) copy-start(bf16[1,64,3072]{2,1,0:T(8,128)(2,1)} %param.8) | copy-start | bytes 1179652
  8.8 37.6 %all-to-all-start = ((bf16[32,3,16,768]{3,2,1,0:T(8,128)(2,1)}), bf16[32,3,16,768]{3,2,1,0:T(8,128)(2,1)S(1)}, u32[]{:S(2)}, u32[]{:S(2)}) async-start(bf16[32,3,16,768]{3,2,1,0:T(8,128)(2,1)} %pad_maximum_fusion), calls=%async_computation | async-start | bytes 4718592 | tf_op jit(solution)/shard_map/all_to_all | solution.py:129
  17.3 32.6 %copy-start.15 = (pred[8,16]{1,0:T(8,128)(4,1)}, pred[8,16]{1,0:T(8,128)(4,1)S(1)}, u32[]{:S(2)}) copy-start(pred[8,16]{1,0:T(8,128)(4,1)S(1)} %fusion.39) | copy-start | bytes 388
  17.5 32.4 %copy-start.5 = (s32[8,16]{1,0:T(8,128)}, s32[8,16]{1,0:T(8,128)S(1)}, u32[]{:S(2)}) copy-start(s32[8,16]{1,0:T(8,128)S(1)} %select_reduce_fusion) | copy-start | bytes 1540
  21.5 25.8 %copy-start.13 = (pred[256,16]{0,1:T(8,128)(4,1)}, pred[256,16]{0,1:T(8,128)(4,1)S(1)}, u32[]{:S(2)}) copy-start(pred[256,16]{0,1:T(8,128)(4,1)S(1)} %iota_compare_fusion.10) | copy-start | bytes 12292
  21.5 25.8 %copy-start.9 = (pred[256,32]{0,1:T(8,128)(4,1)}, pred[256,32]{0,1:T(8,128)(4,1)S(1)}, u32[]{:S(2)}) copy-start(pred[256,32]{0,1:T(8,128)(4,1)S(1)} %iota_compare_fusion.8) | copy-start | bytes 24580
  47.3 1.0 copy-start.2
  48.6 1.0 copy-start.3
  51.9 5.0 %copy-start.8 = (pred[256,256]{0,1:T(8,128)(4,1)S(1)}, pred[256,256]{0,1:T(8,128)(4,1)}, u32[]{:S(2)}) copy-start(pred[256,256]{0,1:T(8,128)(4,1)} %fusion.32) | copy-start | bytes 196612
  51.9 27.5 %all-to-all-start.1 = ((bf16[32,2,16,768]{3,2,1,0:T(8,128)(2,1)}), bf16[32,2,16,768]{3,2,1,0:T(8,128)(2,1)S(1)}, u32[]{:S(2)}, u32[]{:S(2)}) async-start(bf16[32,2,16,768]{3,2,1,0:T(8,128)(2,1)} %copy.193), calls=%async_computation.1 | async-start | bytes 3145728 | tf_op jit(solution)/shard_map/all_to_all | solution.py:129
  56.9 1.9 %copy-start = (bf16[1,256,768]{1,2,0:T(8,128)(2,1)S(1)}, bf16[1,256,768]{1,2,0:T(8,128)(2,1)}, u32[]{:S(2)}) copy-start(bf16[1,256,768]{1,2,0:T(8,128)(2,1)} %get-tuple-element.27) | copy-start | bytes 1179652
  58.7 1.9 %copy-start.17 = (f32[6,256,256]{1,2,0:T(8,128)S(1)}, f32[6,256,256]{1,2,0:T(8,128)}, u32[]{:S(2)}) copy-start(f32[6,256,256]{1,2,0:T(8,128)} %get-tuple-element.37) | copy-start | bytes 4718596
  62.2 17.6 %copy-start.10 = (pred[256,32]{0,1:T(8,128)(4,1)S(1)}, pred[256,32]{0,1:T(8,128)(4,1)}, u32[]{:S(2)}) copy-start(pred[256,32]{0,1:T(8,128)(4,1)} %copy-done.9) | copy-start | bytes 24580
  62.2 17.6 %copy-start.14 = (pred[256,16]{0,1:T(8,128)(4,1)S(1)}, pred[256,16]{0,1:T(8,128)(4,1)}, u32[]{:S(2)}) copy-start(pred[256,16]{0,1:T(8,128)(4,1)} %copy-done.13) | copy-start | bytes 12292
  82.3 4.5 %copy-start.4 = (pred[256,32,16,1]{0,1,2,3:T(32,128)(4,1)S(1)}, pred[256,32,16,1]{0,1,2,3:T(32,128)(4,1)}, u32[]{:S(2)}) copy-start(pred[256,32,16,1]{0,1,2,3:T(32,128)(4,1)} %and_bitcast_fusion) | copy-start | bytes 393220
  82.3 27.0 %all-to-all-start.2 = ((bf16[32,2,16,768]{3,2,1,0:T(8,128)(2,1)}), bf16[32,2,16,768]{3,2,1,0:T(8,128)(2,1)S(1)}, u32[]{:S(2)}, u32[]{:S(2)}) async-start(bf16[32,2,16,768]{3,2,1,0:T(8,128)(2,1)} %copy.201), calls=%async_computation.2 | async-start | bytes 3145728 | tf_op jit(solution)/shard_map/all_to_all | solution.py:138
  90.2 19.1 %copy-start.12 = (pred[8,16]{1,0:T(8,128)(4,1)S(1)}, pred[8,16]{1,0:T(8,128)(4,1)}, u32[]{:S(2)}) copy-start(pred[8,16]{1,0:T(8,128)(4,1)} %copy-done.11) | copy-start | bytes 388
  110.4 20.1 %copy-start.6 = (s32[8,16]{1,0:T(8,128)S(1)}, s32[8,16]{1,0:T(8,128)}, u32[]{:S(2)}) copy-start(s32[8,16]{1,0:T(8,128)} %copy-done.5) | copy-start | bytes 1540
  110.4 20.1 %copy-start.16 = (pred[8,16]{1,0:T(8,128)(4,1)S(1)}, pred[8,16]{1,0:T(8,128)(4,1)}, u32[]{:S(2)}) copy-start(pred[8,16]{1,0:T(8,128)(4,1)} %copy-done.15) | copy-start | bytes 388
  111.8 18.7 %all-to-all-start.3 = ((bf16[32,1,16,768]{3,2,1,0:T(8,128)(2,1)}), bf16[32,1,16,768]{3,2,1,0:T(8,128)(2,1)S(1)}, u32[]{:S(2)}, u32[]{:S(2)}) async-start(bf16[32,1,16,768]{3,2,1,0:T(8,128)(2,1)} %copy.206), calls=%async_computation.3 | async-start | bytes 1572864 | tf_op jit(solution)/shard_map/all_to_all | solution.py:138
  116.1 19.9 %collective-permute-start.1 = (bf16[1,64,3072]{2,1,0:T(8,128)(2,1)S(1)}, bf16[1,64,3072]{2,1,0:T(8,128)(2,1)S(1)}, u32[]{:S(2)}, u32[]{:S(2)}) collective-permute-start(bf16[1,64,3072]{2,1,0:T(8,128)(2,1)S(1)} %bitcast.215), channel_id=1, source_target_pairs={{32,0},{64,32},{96,64},{128,96},{160,128},{192,160},{224,192},{33,... | collective-permute-start | bytes 1179656 | tf_op jit(solution)/shard_map/ppermute | solution.py:18
  118.1 21.0 %collective-permute-start.2 = (bf16[1,64,3072]{2,1,0:T(8,128)(2,1)S(1)}, bf16[1,64,3072]{2,1,0:T(8,128)(2,1)S(1)}, u32[]{:S(2)}, u32[]{:S(2)}) collective-permute-start(bf16[1,64,3072]{2,1,0:T(8,128)(2,1)S(1)} %bitcast.214), channel_id=1, source_target_pairs={{32,0},{64,32},{96,64},{128,96},{160,128},{192,160},{224,192},{33,... | collective-permute-start | bytes 1179656 | tf_op jit(solution)/shard_map/ppermute | solution.py:18
  130.9 13.2 %collective-permute-start = (bf16[1,64,3072]{2,1,0:T(8,128)(2,1)S(1)}, bf16[1,64,3072]{2,1,0:T(8,128)(2,1)S(1)}, u32[]{:S(2)}, u32[]{:S(2)}) collective-permute-start(bf16[1,64,3072]{2,1,0:T(8,128)(2,1)S(1)} %bitcast.216), channel_id=1, source_target_pairs={{0,32},{32,64},{64,96},{96,128},{128,160},{160,192},{192,224},{1,3... | collective-permute-start | bytes 1179656 | tf_op jit(solution)/shard_map/ppermute | solution.py:18
  (1 other events, 0.8 us)

commit v2 on v1

--- a/solution.py
+++ b/solution.py
@@ -117,11 +117,11 @@
         packed = [
             jnp.einsum(
                 "skt,tmf->smkf",
-                send,
+                send[index],
                 array[0].reshape(tok_dev, mp_count, group_features),
                 preferred_element_type=jnp.bfloat16,
             )
-            for array in arrays
+            for index, array in enumerate(arrays)
         ]
         stacked = jnp.stack(packed, axis=2).reshape(
             group_count, len(arrays), slot_count, group_features
@@ -134,26 +134,28 @@
 
     def give_back(results, gather, send):
         flat = jnp.stack([r.reshape(block_rows, group_features) for r in results], axis=0)
-        placed = jnp.einsum("irk,aif->rakf", gather, flat, preferred_element_type=jnp.bfloat16)
+        placed = jnp.einsum("airk,aif->rakf", gather, flat, preferred_element_type=jnp.bfloat16)
         arrived = lax.all_to_all(placed, axes, split_axis=0, concat_axis=0, tiled=True)
         arrived = arrived.reshape(seq_count, mp_count, len(results), slot_count, group_features)
-        rows = jnp.einsum("skt,smakf->atmf", send, arrived, preferred_element_type=jnp.bfloat16)
+        rows = jnp.einsum("askt,smakf->atmf", send, arrived, preferred_element_type=jnp.bfloat16)
         return [row.reshape(1, tok_dev, features) for row in rows]
 
     positions_f = plan_fwd[2].reshape(-1, CLUSTER)
     positions_b = plan_bwd[2].reshape(-1, CLUSTER)
-    arrived_b = exchange((shared_bwd, values_bwd, upstream_bwd), plan_bwd[0])
-    arrived_b, shared_fwd, values_fwd = lax.optimization_barrier((arrived_b, shared_fwd, values_fwd))
-    arrived_f = exchange((shared_fwd, values_fwd), plan_fwd[0])
-    shared_b, values_b, upstream_b = gather_block(arrived_b, plan_bwd[1])
+    arrived = exchange(
+        (shared_bwd, values_bwd, upstream_bwd, shared_fwd, values_fwd),
+        jnp.stack([plan_bwd[0]] * 3 + [plan_fwd[0]] * 2),
+    )
+    shared_b, values_b, upstream_b = gather_block(arrived[:, :3], plan_bwd[1])
     shared_grad, value_grad = backward_block(shared_b, values_b, upstream_b, positions_b, score_scale)
-    shared_grad, value_grad, arrived_f = lax.optimization_barrier((shared_grad, value_grad, arrived_f))
-    shared_out, values_out = give_back((shared_grad, value_grad), plan_bwd[1], plan_bwd[0])
-    shared_f, values_f = gather_block(arrived_f, plan_fwd[1])
+    shared_f, values_f = gather_block(arrived[:, 3:], plan_fwd[1])
     attended = forward_block(shared_f, values_f, positions_f, score_scale)
-    attended, shared_out, values_out = lax.optimization_barrier((attended, shared_out, values_out))
+    shared_out, values_out, forward_out = give_back(
+        (shared_grad, value_grad, attended),
+        jnp.stack([plan_bwd[1]] * 2 + [plan_fwd[1]]),
+        jnp.stack([plan_bwd[0]] * 2 + [plan_fwd[0]]),
+    )
     shared_grad_in, values_grad_in = shifted((shared_out, values_out), "pipe", -1)
-    (forward_out,) = give_back((attended,), plan_fwd[1], plan_fwd[0])
     forward_in = shifted(forward_out, "pipe", 1)
     return (forward_in, shared_grad_in, values_grad_in)
 

time: 148 us -> 149 us (level)
  waiting for transfers between devices: 75.7 us -> 91.1 us
  starting transfers between devices: 30.1 us -> 21.8 us
  matrix products: 14.2 us -> 9.25 us
  other arithmetic: 9.89 us -> 6.37 us
  local copies, waits for them, and re-layouts: 15.1 us -> 18.1 us
    ppermute x3, waiting for transfers between devices: 8.11 us -> 17.9 us  [shifted(): return lax.ppermute(block, axis, route)]
    all_to_all x2 -> x1, starting transfers between devices: 12.3 us -> 7.62 us  [exchange(): lax.all_to_all(stacked, axes, split_axis=0, concat_axis=0, tiled=True)]
    all_to_all x2 -> x1, starting transfers between devices: 8.79 us -> 5.29 us  [give_back(): lax.all_to_all(placed, axes, split_axis=0, concat_axis=0, tiled=True)]
    all_to_all x2 -> x1, waiting for transfers between devices: 39.8 us -> 43.1 us  [exchange(): lax.all_to_all(stacked, axes, split_axis=0, concat_axis=0, tiled=True)]
    slice x1 -> x3, local copies, waits for them, and re-layouts: 0.21 us -> 3.55 us  [the longest x1 1.82 us: per_device(): shared_b, values_b, upstream_b = gather_block(arrived[:, :3], plan_bwd[1])]
    unnamed x40 -> x16, local copies, waits for them, and re-layouts: 3.87 us -> 6.3 us
    sub x2, matrix products: 3.71 us -> 1.43 us  [softmax_weights(): exponent = jnp.exp(scores - largest)]
    all_to_all x2 -> x1, waiting for transfers between devices: 27.8 us -> 30 us  [give_back(): lax.all_to_all(placed, axes, split_axis=0, concat_axis=0, tiled=True)]
  transfers between devices with their start and end apart: 7 -> 5, of which waited for: 6 -> 5; matrix products, arithmetic and copies ran while one was open for 12% -> 3% of each run, Pallas kernels for 0% -> 0%
where the time goes in v2:
time: 149 us; the launch traced here: 148 us
  waiting for transfers between devices  91.1 us (61%)
  starting transfers between devices  21.8 us (15%)
  local copies, waits for them, and re-layouts  18.1 us (12%)
  matrix products  9.25 us (6%)
  other arithmetic  6.37 us (4%)
    all_to_all x1, waiting for transfers between devices, exchange(): lax.all_to_all(stacked, axes, split_axis=0, concat_axis=0, tiled=True)  43.1 us
    all_to_all x1, waiting for transfers between devices, give_back(): lax.all_to_all(placed, axes, split_axis=0, concat_axis=0, tiled=True)  30 us
    ppermute x3, waiting for transfers between devices, shifted(): return lax.ppermute(block, axis, route)  17.9 us
    ppermute x3, starting transfers between devices, shifted(): return lax.ppermute(block, axis, route)  8.88 us
    all_to_all x1, starting transfers between devices, exchange(): lax.all_to_all(stacked, axes, split_axis=0, concat_axis=0, tiled=True)  7.62 us
    unnamed x16, local copies, waits for them, and re-layouts  6.3 us
    all_to_all x1, starting transfers between devices, give_back(): lax.all_to_all(placed, axes, split_axis=0, concat_axis=0, tiled=True)  5.29 us
  transfers between devices with their start and end apart: 5, of which 5 were waited for; matrix products, arithmetic and copies ran while one was open for 3% of the time, Pallas kernels for 0%

profile of v2, /device:TPU:96, one launch (start us, length us, event | category | flops | bytes accessed | tf_op | source)
XLA Modules:
  0.0 147.7 jit_solution(10335231402549920118)
XLA Ops:
  0.6 0.8 slice_reduce_fusion.4
  2.9 1.3 reshape_squeeze.15
  4.7 1.0 constant_dynamic-update-slice_fusion.4
  9.9 1.0 constant_dynamic-update-slice_fusion.3
  10.9 1.0 constant_dynamic-update-slice_fusion.2
  11.9 1.0 constant_dynamic-update-slice_fusion.1
  12.9 1.0 constant_dynamic-update-slice_fusion
  13.9 7.6 %all-to-all-start = ((bf16[32,5,16,768]{3,2,1,0:T(8,128)(2,1)}), bf16[32,5,16,768]{3,2,1,0:T(8,128)(2,1)}, u32[]{:S(2)}, u32[]{:S(2)}) async-start(bf16[32,5,16,768]{3,2,1,0:T(8,128)(2,1)} %constant_dynamic-update-slice_fusion), calls=%async_computation | async-start | bytes 7864320 | tf_op jit(solution)/shard_map/all_to_all | solution.py:129
  25.8 43.1 %all-to-all-done = bf16[32,5,16,768]{3,2,1,0:T(8,128)(2,1)} async-done(((bf16[32,5,16,768]{3,2,1,0:T(8,128)(2,1)}), bf16[32,5,16,768]{3,2,1,0:T(8,128)(2,1)}, u32[]{:S(2)}, u32[]{:S(2)}) %all-to-all-start) | async-done | bytes 3932192 | tf_op jit(solution)/shard_map/all_to_all | solution.py:129
  69.0 1.8 %slice.50 = bf16[32,3,16,768]{3,2,1,0:T(8,128)(2,1)S(1)} slice(bf16[32,5,16,768]{3,2,1,0:T(8,128)(2,1)} %all-to-all-done), slice={[0:32], [0:3], [0:16], [0:768]} | slice | bytes 4718592 | tf_op jit(solution)/shard_map/slice | solution.py:149
  70.8 1.1 fusion.20
  74.9 1.5 %slice.52 = bf16[32,2,16,768]{3,2,1,0:T(8,128)(2,1)S(1)} slice(bf16[32,5,16,768]{3,2,1,0:T(8,128)(2,1)} %all-to-all-done), slice={[0:32], [3:5], [0:16], [0:768]} | slice | bytes 3145728 | tf_op jit(solution)/shard_map/slice | solution.py:151
  76.4 1.3 fusion.23
  78.9 0.8 convolution_bitcast_fusion
  79.7 2.7 %copy.194 = bf16[32,3,16,768]{3,2,1,0:T(8,128)(2,1)} copy(bf16[32,3,16,768]{3,0,2,1:T(8,128)(2,1)S(1)} %convolution_bitcast_fusion) | data formatting | bytes 4718592 | tf_op jit(solution)/shard_map/airk,aif->rakf/transpose | solution.py:137
  82.4 5.3 %all-to-all-start.1 = ((bf16[32,3,16,768]{3,2,1,0:T(8,128)(2,1)}), bf16[32,3,16,768]{3,2,1,0:T(8,128)(2,1)S(1)}, u32[]{:S(2)}, u32[]{:S(2)}) async-start(bf16[32,3,16,768]{3,2,1,0:T(8,128)(2,1)} %copy.194), calls=%async_computation.1 | async-start | bytes 4718592 | tf_op jit(solution)/shard_map/all_to_all | solution.py:138
  87.9 30.0 %all-to-all-done.1 = bf16[32,3,16,768]{3,2,1,0:T(8,128)(2,1)S(1)} async-done(((bf16[32,3,16,768]{3,2,1,0:T(8,128)(2,1)}), bf16[32,3,16,768]{3,2,1,0:T(8,128)(2,1)S(1)}, u32[]{:S(2)}, u32[]{:S(2)}) %all-to-all-start.1) | async-done | bytes 2359328 | tf_op jit(solution)/shard_map/all_to_all | solution.py:138
  118.6 5.0 %collective-permute-start = (bf16[1,64,3072]{2,1,0:T(8,128)(2,1)S(1)}, bf16[1,64,3072]{2,1,0:T(8,128)(2,1)S(1)}, u32[]{:S(2)}, u32[]{:S(2)}) collective-permute-start(bf16[1,64,3072]{2,1,0:T(8,128)(2,1)S(1)} %bitcast.197), channel_id=1, source_target_pairs={{0,32},{32,64},{64,96},{96,128},{128,160},{160,192},{192,224},{1,3... | collective-permute-start | bytes 1179656 | tf_op jit(solution)/shard_map/ppermute | solution.py:18
  123.7 1.9 %collective-permute-start.1 = (bf16[1,64,3072]{2,1,0:T(8,128)(2,1)S(1)}, bf16[1,64,3072]{2,1,0:T(8,128)(2,1)S(1)}, u32[]{:S(2)}, u32[]{:S(2)}) collective-permute-start(bf16[1,64,3072]{2,1,0:T(8,128)(2,1)S(1)} %bitcast.199), channel_id=1, source_target_pairs={{32,0},{64,32},{96,64},{128,96},{160,128},{192,160},{224,192},{33,... | collective-permute-start | bytes 1179656 | tf_op jit(solution)/shard_map/ppermute | solution.py:18
  125.7 1.9 %collective-permute-start.2 = (bf16[1,64,3072]{2,1,0:T(8,128)(2,1)S(1)}, bf16[1,64,3072]{2,1,0:T(8,128)(2,1)S(1)}, u32[]{:S(2)}, u32[]{:S(2)}) collective-permute-start(bf16[1,64,3072]{2,1,0:T(8,128)(2,1)S(1)} %bitcast.200), channel_id=1, source_target_pairs={{32,0},{64,32},{96,64},{128,96},{160,128},{192,160},{224,192},{33,... | collective-permute-start | bytes 1179656 | tf_op jit(solution)/shard_map/ppermute | solution.py:18
  127.6 4.1 %collective-permute-done = bf16[1,64,3072]{2,1,0:T(8,128)(2,1)S(1)} collective-permute-done((bf16[1,64,3072]{2,1,0:T(8,128)(2,1)S(1)}, bf16[1,64,3072]{2,1,0:T(8,128)(2,1)S(1)}, u32[]{:S(2)}, u32[]{:S(2)}) %collective-permute-start) | collective-permute-done | bytes 393248 | tf_op jit(solution)/shard_map/ppermute | solution.py:18
  131.7 7.1 %collective-permute-done.1 = bf16[1,64,3072]{2,1,0:T(8,128)(2,1)S(1)} collective-permute-done((bf16[1,64,3072]{2,1,0:T(8,128)(2,1)S(1)}, bf16[1,64,3072]{2,1,0:T(8,128)(2,1)S(1)}, u32[]{:S(2)}, u32[]{:S(2)}) %collective-permute-start.1) | collective-permute-done | bytes 393248 | tf_op jit(solution)/shard_map/ppermute | solution.py:18
  138.8 6.7 %collective-permute-done.2 = bf16[1,64,3072]{2,1,0:T(8,128)(2,1)S(1)} collective-permute-done((bf16[1,64,3072]{2,1,0:T(8,128)(2,1)S(1)}, bf16[1,64,3072]{2,1,0:T(8,128)(2,1)S(1)}, u32[]{:S(2)}, u32[]{:S(2)}) %collective-permute-start.2) | collective-permute-done | bytes 393248 | tf_op jit(solution)/shard_map/ppermute | solution.py:18
  145.5 0.7 copy.272
  (87 shorter events, 16.7 us)
Async XLA Ops:
  4.2 1.4 copy-start
  4.7 1.7 %copy-start.1 = (bf16[1,64,3072]{2,1,0:T(8,128)(2,1)S(1)}, bf16[1,64,3072]{2,1,0:T(8,128)(2,1)}, u32[]{:S(2)}) copy-start(bf16[1,64,3072]{2,1,0:T(8,128)(2,1)} %param.10) | copy-start | bytes 1179652
  5.9 2.5 %copy-start.2 = (bf16[1,64,3072]{2,1,0:T(8,128)(2,1)S(1)}, bf16[1,64,3072]{2,1,0:T(8,128)(2,1)}, u32[]{:S(2)}) copy-start(bf16[1,64,3072]{2,1,0:T(8,128)(2,1)} %param.6) | copy-start | bytes 1179652
  6.4 2.4 %copy-start.3 = (bf16[1,64,3072]{2,1,0:T(8,128)(2,1)S(1)}, bf16[1,64,3072]{2,1,0:T(8,128)(2,1)}, u32[]{:S(2)}) copy-start(bf16[1,64,3072]{2,1,0:T(8,128)(2,1)} %param.7) | copy-start | bytes 1179652
  13.9 55.1 %all-to-all-start = ((bf16[32,5,16,768]{3,2,1,0:T(8,128)(2,1)}), bf16[32,5,16,768]{3,2,1,0:T(8,128)(2,1)}, u32[]{:S(2)}, u32[]{:S(2)}) async-start(bf16[32,5,16,768]{3,2,1,0:T(8,128)(2,1)} %constant_dynamic-update-slice_fusion), calls=%async_computation | async-start | bytes 7864320 | tf_op jit(solution)/shard_map/all_to_all | solution.py:129
  82.4 35.5 %all-to-all-start.1 = ((bf16[32,3,16,768]{3,2,1,0:T(8,128)(2,1)}), bf16[32,3,16,768]{3,2,1,0:T(8,128)(2,1)S(1)}, u32[]{:S(2)}, u32[]{:S(2)}) async-start(bf16[32,3,16,768]{3,2,1,0:T(8,128)(2,1)} %copy.194), calls=%async_computation.1 | async-start | bytes 4718592 | tf_op jit(solution)/shard_map/all_to_all | solution.py:138
  118.6 13.1 %collective-permute-start = (bf16[1,64,3072]{2,1,0:T(8,128)(2,1)S(1)}, bf16[1,64,3072]{2,1,0:T(8,128)(2,1)S(1)}, u32[]{:S(2)}, u32[]{:S(2)}) collective-permute-start(bf16[1,64,3072]{2,1,0:T(8,128)(2,1)S(1)} %bitcast.197), channel_id=1, source_target_pairs={{0,32},{32,64},{64,96},{96,128},{128,160},{160,192},{192,224},{1,3... | collective-permute-start | bytes 1179656 | tf_op jit(solution)/shard_map/ppermute | solution.py:18
  123.7 15.1 %collective-permute-start.1 = (bf16[1,64,3072]{2,1,0:T(8,128)(2,1)S(1)}, bf16[1,64,3072]{2,1,0:T(8,128)(2,1)S(1)}, u32[]{:S(2)}, u32[]{:S(2)}) collective-permute-start(bf16[1,64,3072]{2,1,0:T(8,128)(2,1)S(1)} %bitcast.199), channel_id=1, source_target_pairs={{32,0},{64,32},{96,64},{128,96},{160,128},{192,160},{224,192},{33,... | collective-permute-start | bytes 1179656 | tf_op jit(solution)/shard_map/ppermute | solution.py:18
  125.7 19.8 %collective-permute-start.2 = (bf16[1,64,3072]{2,1,0:T(8,128)(2,1)S(1)}, bf16[1,64,3072]{2,1,0:T(8,128)(2,1)S(1)}, u32[]{:S(2)}, u32[]{:S(2)}) collective-permute-start(bf16[1,64,3072]{2,1,0:T(8,128)(2,1)S(1)} %bitcast.200), channel_id=1, source_target_pairs={{32,0},{64,32},{96,64},{128,96},{160,128},{192,160},{224,192},{33,... | collective-permute-start | bytes 1179656 | tf_op jit(solution)/shard_map/ppermute | solution.py:18

commit v3 on v2

--- a/solution.py
+++ b/solution.py
@@ -106,12 +106,16 @@
     slot_count = 2 * block_rows // group_count
     score_scale = 1.0 / math.sqrt(HEAD_DIM)
     axes = ("seq", "mp")
-    plan_fwd = route_plan(
-        cluster_order[0, 0], seq_index, range_here, seq_count, group_count, tok_dev, slot_count
-    )
-    plan_bwd = route_plan(
-        cluster_order[0, 1], seq_index, range_here, seq_count, group_count, tok_dev, slot_count
-    )
+    order_fwd = cluster_order[0, 0]
+    order_bwd = cluster_order[0, 1]
+    order_prev_fwd = shifted(order_fwd, "pipe", 1)
+    order_next_bwd = shifted(order_bwd, "pipe", -1)
+
+    def plan(order):
+        return route_plan(order, seq_index, range_here, seq_count, group_count, tok_dev, slot_count)
+
+    own_f, own_b = plan(order_fwd), plan(order_bwd)
+    back_f, back_b = plan(order_prev_fwd), plan(order_next_bwd)
 
     def exchange(arrays, send):
         packed = [
@@ -128,35 +132,31 @@
         )
         return lax.all_to_all(stacked, axes, split_axis=0, concat_axis=0, tiled=True)
 
-    def gather_block(arrived, gather):
-        rows = jnp.einsum("irk,rakf->aif", gather, arrived, preferred_element_type=jnp.bfloat16)
-        return [row.reshape(1, block_rows, heads_dev, HEAD_DIM) for row in rows]
-
     def give_back(results, gather, send):
-        flat = jnp.stack([r.reshape(block_rows, group_features) for r in results], axis=0)
-        placed = jnp.einsum("airk,aif->rakf", gather, flat, preferred_element_type=jnp.bfloat16)
+        placed = jnp.einsum("airk,aif->rakf", gather, results, preferred_element_type=jnp.bfloat16)
         arrived = lax.all_to_all(placed, axes, split_axis=0, concat_axis=0, tiled=True)
-        arrived = arrived.reshape(seq_count, mp_count, len(results), slot_count, group_features)
+        arrived = arrived.reshape(seq_count, mp_count, results.shape[0], slot_count, group_features)
         rows = jnp.einsum("askt,smakf->atmf", send, arrived, preferred_element_type=jnp.bfloat16)
         return [row.reshape(1, tok_dev, features) for row in rows]
 
-    positions_f = plan_fwd[2].reshape(-1, CLUSTER)
-    positions_b = plan_bwd[2].reshape(-1, CLUSTER)
-    arrived = exchange(
-        (shared_bwd, values_bwd, upstream_bwd, shared_fwd, values_fwd),
-        jnp.stack([plan_bwd[0]] * 3 + [plan_fwd[0]] * 2),
+    positions_f = own_f[2].reshape(-1, CLUSTER)
+    positions_b = own_b[2].reshape(-1, CLUSTER)
+    send_in = jnp.stack([own_b[0]] * 3 + [own_f[0]] * 2)
+    gather_in = jnp.stack([own_b[1]] * 3 + [own_f[1]] * 2)
+    arrived = exchange((shared_bwd, values_bwd, upstream_bwd, shared_fwd, values_fwd), send_in)
+    rows = jnp.einsum("airk,rakf->aif", gather_in, arrived, preferred_element_type=jnp.bfloat16)
+    rows = rows.reshape(5, 1, block_rows, heads_dev, HEAD_DIM)
+    shared_grad, value_grad = backward_block(rows[0], rows[1], rows[2], positions_b, score_scale)
+    moved_b = shifted(
+        jnp.stack([shared_grad, value_grad]).reshape(2, block_rows, group_features), "pipe", -1
     )
-    shared_b, values_b, upstream_b = gather_block(arrived[:, :3], plan_bwd[1])
-    shared_grad, value_grad = backward_block(shared_b, values_b, upstream_b, positions_b, score_scale)
-    shared_f, values_f = gather_block(arrived[:, 3:], plan_fwd[1])
-    attended = forward_block(shared_f, values_f, positions_f, score_scale)
-    shared_out, values_out, forward_out = give_back(
-        (shared_grad, value_grad, attended),
-        jnp.stack([plan_bwd[1]] * 2 + [plan_fwd[1]]),
-        jnp.stack([plan_bwd[0]] * 2 + [plan_fwd[0]]),
+    attended = forward_block(rows[3], rows[4], positions_f, score_scale)
+    moved_f = shifted(attended.reshape(1, block_rows, group_features), "pipe", 1)
+    shared_grad_in, values_grad_in, forward_in = give_back(
+        jnp.concatenate([moved_b, moved_f]),
+        jnp.stack([back_b[1]] * 2 + [back_f[1]]),
+        jnp.stack([back_b[0]] * 2 + [back_f[0]]),
     )
-    shared_grad_in, values_grad_in = shifted((shared_out, values_out), "pipe", -1)
-    forward_in = shifted(forward_out, "pipe", 1)
     return (forward_in, shared_grad_in, values_grad_in)
 
 

time: 149 us -> 146 us (0.980)
  waiting for transfers between devices: 91.1 us -> 68.3 us
  matrix products: 9.25 us -> 17.1 us
  other arithmetic: 6.37 us -> 14 us
  starting transfers between devices: 21.8 us -> 27.8 us
    all_to_all x1, waiting for transfers between devices: 43.1 us -> 30.7 us  [exchange(): lax.all_to_all(stacked, axes, split_axis=0, concat_axis=0, tiled=True)]
    ppermute x3 -> x4, waiting for transfers between devices: 17.9 us -> 10.5 us  [shifted(): return lax.ppermute(block, axis, route)]
    ppermute x3 -> x4, starting transfers between devices: 8.88 us -> 14.3 us  [shifted(): return lax.ppermute(block, axis, route)]
    all_to_all x1, waiting for transfers between devices: 30 us -> 27.2 us  [give_back(): lax.all_to_all(placed, axes, split_axis=0, concat_axis=0, tiled=True)]
    another operation x8 -> x18, other arithmetic: 2.5 us -> 5.16 us
    dot_general x3 -> x2, matrix products: 3.13 us -> 5.77 us  [the longest x1 3.86 us: per_device(): jnp.einsum('airk,rakf->aif', gather_in, arrived, preferred_element_type=j...]
    slice x4 -> x7, local copies, waits for them, and re-layouts: 4.4 us -> 1.9 us  [the longest x1 0.84 us: per_device(): order_fwd = cluster_order[0, 0]]
    sub x2, matrix products: 1.43 us -> 3.72 us  [softmax_weights(): exponent = jnp.exp(scores - largest)]
  transfers between devices with their start and end apart: 5 -> 6, of which waited for: 5 -> 4; matrix products, arithmetic and copies ran while one was open for 3% -> 11% of each run, Pallas kernels for 0% -> 0%
where the time goes in v3:
time: 146 us
  waiting for transfers between devices  68.3 us (47%)
  starting transfers between devices  27.8 us (19%)
  local copies, waits for them, and re-layouts  17.1 us (12%)
  matrix products  17.1 us (12%)
  other arithmetic  14 us (10%)
    all_to_all x1, waiting for transfers between devices, exchange(): lax.all_to_all(stacked, axes, split_axis=0, concat_axis=0, tiled=True)  30.7 us
    all_to_all x1, waiting for transfers between devices, give_back(): lax.all_to_all(placed, axes, split_axis=0, concat_axis=0, tiled=True)  27.2 us
    ppermute x4, starting transfers between devices, shifted(): return lax.ppermute(block, axis, route)  14.3 us
    ppermute x4, waiting for transfers between devices, shifted(): return lax.ppermute(block, axis, route)  10.5 us
    all_to_all x1, starting transfers between devices, exchange(): lax.all_to_all(stacked, axes, split_axis=0, concat_axis=0, tiled=True)  7.44 us
    all_to_all x1, starting transfers between devices, give_back(): lax.all_to_all(placed, axes, split_axis=0, concat_axis=0, tiled=True)  6.05 us
    another operation x16, other arithmetic  5.01 us
    unnamed x25, local copies, waits for them, and re-layouts  4.57 us
  transfers between devices with their start and end apart: 6, of which 4 were waited for; matrix products, arithmetic and copies ran while one was open for 11% of the time, Pallas kernels for 0%

profile of v3, /device:TPU:96, one launch (start us, length us, event | category | flops | bytes accessed | tf_op | source)
XLA Modules:
  0.0 145.7 jit_solution(17676980683753674222)
XLA Ops:
  0.6 0.8 slice_reduce_fusion.8
  2.9 1.3 reshape_squeeze.15
  4.7 1.0 constant_dynamic-update-slice_fusion.4
  9.9 1.0 constant_dynamic-update-slice_fusion.3
  10.9 1.0 constant_dynamic-update-slice_fusion.2
  11.9 1.0 constant_dynamic-update-slice_fusion.1
  12.9 1.0 constant_dynamic-update-slice_fusion
  13.9 7.4 %all-to-all-start = ((bf16[32,5,16,768]{3,2,1,0:T(8,128)(2,1)}), bf16[32,5,16,768]{3,2,1,0:T(8,128)(2,1)}, u32[]{:S(2)}, u32[]{:S(2)}) async-start(bf16[32,5,16,768]{3,2,1,0:T(8,128)(2,1)} %constant_dynamic-update-slice_fusion), calls=%async_computation | async-start | bytes 7864320 | tf_op jit(solution)/shard_map/all_to_all | solution.py:133
  21.3 2.0 %collective-permute-start = (s32[2048]{0:T(1024)S(1)}, s32[2048]{0:T(1024)S(1)}, u32[]{:S(2)}, u32[]{:S(2)}) collective-permute-start(s32[2048]{0:T(1024)S(1)} %bitcast.234), channel_id=1, source_target_pairs={{32,0},{64,32},{96,64},{128,96},{160,128},{192,160},{224,192},{33,... | collective-permute-start | bytes 24584 | tf_op jit(solution)/shard_map/ppermute | solution.py:18
  23.3 5.2 %collective-permute-start.1 = (s32[2048]{0:T(1024)S(1)}, s32[2048]{0:T(1024)S(1)}, u32[]{:S(2)}, u32[]{:S(2)}) collective-permute-start(s32[2048]{0:T(1024)S(1)} %bitcast.232), channel_id=1, source_target_pairs={{0,32},{32,64},{64,96},{96,128},{128,160},{160,192},{192,224},{1,3... | collective-permute-start | bytes 24584 | tf_op jit(solution)/shard_map/ppermute | solution.py:18
  38.3 30.7 %all-to-all-done = bf16[32,5,16,768]{3,2,1,0:T(8,128)(2,1)} async-done(((bf16[32,5,16,768]{3,2,1,0:T(8,128)(2,1)}), bf16[32,5,16,768]{3,2,1,0:T(8,128)(2,1)}, u32[]{:S(2)}, u32[]{:S(2)}) %all-to-all-start) | async-done | bytes 3932192 | tf_op jit(solution)/shard_map/all_to_all | solution.py:133
  69.0 3.9 %fusion.8 = bf16[5,256,768]{2,1,0:T(8,128)(2,1)S(1)} fusion(pred[5,256,32,16]{1,2,3,0:T(8,128)(4,1)S(1)} %and_dynamic-update-slice_fusion.4, bf16[32,5,16,768]{3,2,1,0:T(8,128)(2,1)} %all-to-all-done), kind=kOutput, calls=%fused_computation.9 | convolution fusion | flops 1006632960 | bytes 6553600 | tf_op jit(solution)/shard_map/airk,rakf->aif/dot_general | solution.py:147
  74.3 1.9 %fusion.129 = (f32[6,256]{1,0:T(8,128)S(1)}, f32[6,256,256]{1,2,0:T(8,128)}) fusion(bf16[256,6,128]{0,2,1:T(8,128)(2,1)S(1)} %bitcast.210, pred[256,256]{0,1:T(8,128)(4,1)S(1)} %copy-done.6), kind=kOutput, calls=%fused_computation.258 | convolution fusion | flops 102236416 | bytes 2037760 | tf_op jit(solution)/shard_map/sub | solution.py:36
  76.2 1.9 %convolution_convert_fusion.1 = bf16[6,128,256]{2,1,0:T(8,128)(2,1)S(1)} fusion(bf16[256,6,128]{0,2,1:T(8,128)(2,1)S(1)} %bitcast.225, f32[6,256,256]{1,2,0:T(8,128)} %get-tuple-element.27, f32[6,256]{1,0:T(8,128)S(1)} %get-tuple-element.26), kind=kOutput, calls=%fused_computation.27 | convolution fusion | flops 101646336 | bytes 2365440 | tf_op jit(solution)/shard_map/nhqk,nqhd->nkhd/dot_general | solution.py:52
  80.0 2.0 %collective-permute-start.2 = (bf16[2,256,768]{2,1,0:T(8,128)(2,1)S(1)}, bf16[2,256,768]{2,1,0:T(8,128)(2,1)}, u32[]{:S(2)}, u32[]{:S(2)}) collective-permute-start(bf16[2,256,768]{2,1,0:T(8,128)(2,1)S(1)} %pad_maximum_fusion), channel_id=1, source_target_pairs={{32,0},{64,32},{96,64},{128,96},{160,128},{192,160},{224,192},{33,... | collective-permute-start | bytes 2359304 | tf_op jit(solution)/shard_map/ppermute | solution.py:18
  82.2 1.9 %fusion.128 = (f32[6,256]{1,0:T(8,128)S(1)}, f32[6,256,256]{1,2,0:T(8,128)}) fusion(bf16[256,6,128]{0,2,1:T(8,128)(2,1)S(1)} %bitcast.228, pred[256,256]{0,1:T(8,128)(4,1)S(1)} %copy-done.5), kind=kOutput, calls=%fused_computation.257 | convolution fusion | flops 102236416 | bytes 2037760 | tf_op jit(solution)/shard_map/sub | solution.py:36
  84.3 1.7 %convolution_convert_fusion = bf16[6,128,256]{2,1,0:T(8,128)(2,1)S(1)} fusion(bf16[256,6,128]{0,2,1:T(8,128)(2,1)S(1)} %bitcast.229, f32[6,256,256]{1,2,0:T(8,128)} %get-tuple-element.25, f32[6,256]{1,0:T(8,128)S(1)} %get-tuple-element.24), kind=kOutput, calls=%fused_computation.26 | convolution fusion | flops 101646336 | bytes 2365440 | tf_op jit(solution)/shard_map/nhqk,nkhd->nqhd/dot_general | solution.py:42
  86.2 5.0 %collective-permute-start.3 = (bf16[1,256,768]{2,1,0:T(8,128)(2,1)S(1)}, bf16[1,256,768]{2,1,0:T(8,128)(2,1)S(1)}, u32[]{:S(2)}, u32[]{:S(2)}) collective-permute-start(bf16[1,256,768]{2,1,0:T(8,128)(2,1)S(1)} %copy.234), channel_id=1, source_target_pairs={{0,32},{32,64},{64,96},{96,128},{128,160},{160,192},{192,224},{1,3... | collective-permute-start | bytes 1179656 | tf_op jit(solution)/shard_map/ppermute | solution.py:18
  91.4 7.3 %collective-permute-done.3 = bf16[1,256,768]{2,1,0:T(8,128)(2,1)S(1)} collective-permute-done((bf16[1,256,768]{2,1,0:T(8,128)(2,1)S(1)}, bf16[1,256,768]{2,1,0:T(8,128)(2,1)S(1)}, u32[]{:S(2)}, u32[]{:S(2)}) %collective-permute-start.3) | collective-permute-done | bytes 393248 | tf_op jit(solution)/shard_map/ppermute | solution.py:18
  98.7 3.2 %collective-permute-done.2 = bf16[2,256,768]{2,1,0:T(8,128)(2,1)} collective-permute-done((bf16[2,256,768]{2,1,0:T(8,128)(2,1)S(1)}, bf16[2,256,768]{2,1,0:T(8,128)(2,1)}, u32[]{:S(2)}, u32[]{:S(2)}) %collective-permute-start.2) | collective-permute-done | bytes 786464 | tf_op jit(solution)/shard_map/ppermute | solution.py:18
  101.8 1.9 %convolution_bitcast_fusion = bf16[32,3,16,768]{3,0,2,1:T(8,128)(2,1)S(1)} fusion(pred[1,256,32,16]{1,2,3,0:T(32,128)(4,1)S(1)} %broadcast_and_fusion, pred[1,256,32,16]{1,2,3,0:T(32,128)(4,1)S(1)} %copy-done.4, bf16[1,256,768]{2,1,0:T(8,128)(2,1)S(1)} %collective-permute-done.3, bf16[2,256,768]{2,1,0:T(8,128)(2,1)} %collective-permute-done.2), kind=kOutput, calls=%fused_computation.8 | convolution fusion | flops 607125504 | bytes 3801088 | tf_op jit(solution)/shard_map/airk,aif->rakf/dot_general | solution.py:136
  103.8 2.7 %copy.237 = bf16[32,3,16,768]{3,2,1,0:T(8,128)(2,1)} copy(bf16[32,3,16,768]{3,0,2,1:T(8,128)(2,1)S(1)} %convolution_bitcast_fusion) | data formatting | bytes 4718592 | tf_op jit(solution)/shard_map/airk,aif->rakf/transpose | solution.py:136
  106.5 6.1 %all-to-all-start.1 = ((bf16[32,3,16,768]{3,2,1,0:T(8,128)(2,1)}), bf16[32,3,16,768]{3,2,1,0:T(8,128)(2,1)S(1)}, u32[]{:S(2)}, u32[]{:S(2)}) async-start(bf16[32,3,16,768]{3,2,1,0:T(8,128)(2,1)} %copy.237), calls=%async_computation.1 | async-start | bytes 4718592 | tf_op jit(solution)/shard_map/all_to_all | solution.py:137
  115.6 27.2 %all-to-all-done.1 = bf16[32,3,16,768]{3,2,1,0:T(8,128)(2,1)S(1)} async-done(((bf16[32,3,16,768]{3,2,1,0:T(8,128)(2,1)}), bf16[32,3,16,768]{3,2,1,0:T(8,128)(2,1)S(1)}, u32[]{:S(2)}, u32[]{:S(2)}) %all-to-all-start.1) | async-done | bytes 2359328 | tf_op jit(solution)/shard_map/all_to_all | solution.py:137
  (148 shorter events, 25.4 us)
Async XLA Ops:
  4.2 1.4 copy-start
  4.7 1.7 %copy-start.1 = (bf16[1,64,3072]{2,1,0:T(8,128)(2,1)S(1)}, bf16[1,64,3072]{2,1,0:T(8,128)(2,1)}, u32[]{:S(2)}) copy-start(bf16[1,64,3072]{2,1,0:T(8,128)(2,1)} %param.10) | copy-start | bytes 1179652
  5.9 2.6 %copy-start.2 = (bf16[1,64,3072]{2,1,0:T(8,128)(2,1)S(1)}, bf16[1,64,3072]{2,1,0:T(8,128)(2,1)}, u32[]{:S(2)}) copy-start(bf16[1,64,3072]{2,1,0:T(8,128)(2,1)} %param.6) | copy-start | bytes 1179652
  6.4 2.4 %copy-start.3 = (bf16[1,64,3072]{2,1,0:T(8,128)(2,1)S(1)}, bf16[1,64,3072]{2,1,0:T(8,128)(2,1)}, u32[]{:S(2)}) copy-start(bf16[1,64,3072]{2,1,0:T(8,128)(2,1)} %param.7) | copy-start | bytes 1179652
  13.9 55.1 %all-to-all-start = ((bf16[32,5,16,768]{3,2,1,0:T(8,128)(2,1)}), bf16[32,5,16,768]{3,2,1,0:T(8,128)(2,1)}, u32[]{:S(2)}, u32[]{:S(2)}) async-start(bf16[32,5,16,768]{3,2,1,0:T(8,128)(2,1)} %constant_dynamic-update-slice_fusion), calls=%async_computation | async-start | bytes 7864320 | tf_op jit(solution)/shard_map/all_to_all | solution.py:133
  21.3 13.1 %collective-permute-start = (s32[2048]{0:T(1024)S(1)}, s32[2048]{0:T(1024)S(1)}, u32[]{:S(2)}, u32[]{:S(2)}) collective-permute-start(s32[2048]{0:T(1024)S(1)} %bitcast.234), channel_id=1, source_target_pairs={{32,0},{64,32},{96,64},{128,96},{160,128},{192,160},{224,192},{33,... | collective-permute-start | bytes 24584 | tf_op jit(solution)/shard_map/ppermute | solution.py:18
  23.3 11.1 %collective-permute-start.1 = (s32[2048]{0:T(1024)S(1)}, s32[2048]{0:T(1024)S(1)}, u32[]{:S(2)}, u32[]{:S(2)}) collective-permute-start(s32[2048]{0:T(1024)S(1)} %bitcast.232), channel_id=1, source_target_pairs={{0,32},{32,64},{64,96},{96,128},{128,160},{160,192},{192,224},{1,3... | collective-permute-start | bytes 24584 | tf_op jit(solution)/shard_map/ppermute | solution.py:18
  73.5 0.8 copy-start.6
  76.2 1.9 %copy-start.9 = (f32[6,256,256]{1,2,0:T(8,128)S(1)}, f32[6,256,256]{1,2,0:T(8,128)}, u32[]{:S(2)}) copy-start(f32[6,256,256]{1,2,0:T(8,128)} %get-tuple-element.27) | copy-start | bytes 4718596
  79.7 2.5 %copy-start.5 = (pred[256,256]{0,1:T(8,128)(4,1)S(1)}, pred[256,256]{0,1:T(8,128)(4,1)}, u32[]{:S(2)}) copy-start(pred[256,256]{0,1:T(8,128)(4,1)} %fusion.45) | copy-start | bytes 196612
  80.0 21.8 %collective-permute-start.2 = (bf16[2,256,768]{2,1,0:T(8,128)(2,1)S(1)}, bf16[2,256,768]{2,1,0:T(8,128)(2,1)}, u32[]{:S(2)}, u32[]{:S(2)}) collective-permute-start(bf16[2,256,768]{2,1,0:T(8,128)(2,1)S(1)} %pad_maximum_fusion), channel_id=1, source_target_pairs={{32,0},{64,32},{96,64},{128,96},{160,128},{192,160},{224,192},{33,... | collective-permute-start | bytes 2359304 | tf_op jit(solution)/shard_map/ppermute | solution.py:18
  84.3 7.0 %copy-start.8 = (s32[256]{0:T(256)S(1)}, s32[256]{0:T(256)}, u32[]{:S(2)}) copy-start(s32[256]{0:T(256)} %broadcast_add_fusion) | copy-start | bytes 3076
  84.3 7.0 %copy-start.7 = (pred[256,32]{0,1:T(8,128)(4,1)S(1)}, pred[256,32]{0,1:T(8,128)(4,1)}, u32[]{:S(2)}) copy-start(pred[256,32]{0,1:T(8,128)(4,1)} %iota_compare_fusion.10) | copy-start | bytes 24580
  84.3 17.6 %copy-start.4 = (pred[1,256,32,16]{1,2,3,0:T(32,128)(4,1)S(1)}, pred[1,256,32,16]{1,2,3,0:T(32,128)(4,1)}, u32[]{:S(2)}) copy-start(pred[1,256,32,16]{1,2,3,0:T(32,128)(4,1)} %broadcast_and_fusion.1) | copy-start | bytes 393220
  86.2 12.5 %collective-permute-start.3 = (bf16[1,256,768]{2,1,0:T(8,128)(2,1)S(1)}, bf16[1,256,768]{2,1,0:T(8,128)(2,1)S(1)}, u32[]{:S(2)}, u32[]{:S(2)}) collective-permute-start(bf16[1,256,768]{2,1,0:T(8,128)(2,1)S(1)} %copy.234), channel_id=1, source_target_pairs={{0,32},{32,64},{64,96},{96,128},{128,160},{160,192},{192,224},{1,3... | collective-permute-start | bytes 1179656 | tf_op jit(solution)/shard_map/ppermute | solution.py:18
  106.5 36.3 %all-to-all-start.1 = ((bf16[32,3,16,768]{3,2,1,0:T(8,128)(2,1)}), bf16[32,3,16,768]{3,2,1,0:T(8,128)(2,1)S(1)}, u32[]{:S(2)}, u32[]{:S(2)}) async-start(bf16[32,3,16,768]{3,2,1,0:T(8,128)(2,1)} %copy.237), calls=%async_computation.1 | async-start | bytes 4718592 | tf_op jit(solution)/shard_map/all_to_all | solution.py:137

commit v4 on v3

--- a/solution.py
+++ b/solution.py
@@ -91,6 +91,72 @@
     )
 
 
+def unit_plan(slot_tokens, seq_index, range_here, seq_count, group_count, tok_dev):
+    block_rows = slot_tokens.shape[0] // seq_count
+    unit = 8
+    source = (slot_tokens // tok_dev).reshape(seq_count, block_rows)
+    member = (source[:, :, None] == jnp.arange(group_count)[None, None, :]).astype(jnp.int32)
+    before = jnp.cumsum(member, axis=1) - member
+    slot_rank = jnp.sum(before * member, axis=2)
+    second = slot_rank // unit
+    place = slot_rank % unit
+    units = jnp.sum(member, axis=1) // unit
+    empty = (units == 0).astype(jnp.int32)
+    double = (units == 2).astype(jnp.int32)
+    empty_rank = jnp.cumsum(empty, axis=0) - empty
+    double_rank = jnp.cumsum(double, axis=0) - double
+    match = (
+        (double[:, None, :] == 1)
+        & (empty[None, :, :] == 1)
+        & (double_rank[:, None, :] == empty_rank[None, :, :])
+    ).astype(jnp.int32)
+    blocks = jnp.arange(seq_count)
+    carrier = jnp.sum(match * blocks[None, :, None], axis=1)
+    owner = jnp.sum(match * blocks[:, None, None], axis=0)
+    overfull = jnp.any(jnp.sum(empty, axis=1) > 1)
+    block_of = jnp.broadcast_to(blocks[:, None], (seq_count, block_rows))
+    mine = source == range_here
+    carrier_slot = jnp.sum(member * carrier[:, None, :], axis=2)
+    target = jnp.where(second == 0, block_of, carrier_slot)
+    code = jnp.where(mine, target * unit + place, -1).reshape(-1)
+    local = (slot_tokens - range_here * tok_dev)
+    token_hit = (local[:, None] == jnp.arange(tok_dev)[None, :]) & mine.reshape(-1)[:, None]
+    token_code = jnp.sum(jnp.where(token_hit, code[:, None], 0), axis=0)
+    send = (token_code[None, :] == jnp.arange(seq_count * unit)[:, None]).reshape(
+        seq_count, unit, tok_dev
+    )
+    src_here = lax.dynamic_index_in_dim(source, seq_index, keepdims=False)
+    second_here = lax.dynamic_index_in_dim(second, seq_index, keepdims=False)
+    place_here = lax.dynamic_index_in_dim(place, seq_index, keepdims=False)
+    carrier_rows = lax.dynamic_index_in_dim(carrier_slot, seq_index, keepdims=False)
+    empty_here = lax.dynamic_index_in_dim(empty, seq_index, keepdims=False)
+    owner_here = lax.dynamic_index_in_dim(owner, seq_index, keepdims=False)
+    at_place = place_here[:, None] == jnp.arange(unit)[None, :]
+    first_pick = (
+        (second_here == 0)[:, None, None]
+        & (src_here[:, None, None] == jnp.arange(group_count)[None, :, None])
+        & at_place[:, None, :]
+    )
+    second_pick = (
+        (second_here == 1)[:, None, None]
+        & (carrier_rows[:, None, None] == blocks[None, :, None])
+        & at_place[:, None, :]
+    )
+    foreign = empty_here == 1
+    spare = ((second_here == 1)[None, :] & at_place.T)
+    relay = foreign[:, None] & (owner_here[:, None] == blocks[None, :])
+    bf = jnp.bfloat16
+    return dict(
+        send=send.astype(bf),
+        first=first_pick.astype(bf),
+        second=second_pick.astype(bf),
+        foreign=foreign.astype(bf),
+        spare=spare.astype(bf),
+        relay=relay.astype(bf),
+        overfull=overfull,
+    )
+
+
 def per_device(shared_fwd, values_fwd, shared_bwd, values_bwd, upstream_bwd, cluster_order):
     seq_count = lax.axis_size("seq")
     mp_count = lax.axis_size("mp")
@@ -104,6 +170,7 @@
     range_here = seq_index * mp_count + mp_index
     block_rows = cluster_order.shape[2] // seq_count
     slot_count = 2 * block_rows // group_count
+    unit = slot_count // 2
     score_scale = 1.0 / math.sqrt(HEAD_DIM)
     axes = ("seq", "mp")
     order_fwd = cluster_order[0, 0]
@@ -114,10 +181,22 @@
     def plan(order):
         return route_plan(order, seq_index, range_here, seq_count, group_count, tok_dev, slot_count)
 
+    def uplan(order):
+        return unit_plan(order, seq_index, range_here, seq_count, group_count, tok_dev)
+
     own_f, own_b = plan(order_fwd), plan(order_bwd)
     back_f, back_b = plan(order_prev_fwd), plan(order_next_bwd)
-
-    def exchange(arrays, send):
+    uown_f, uown_b = uplan(order_fwd), uplan(order_bwd)
+    uback_f, uback_b = uplan(order_prev_fwd), uplan(order_next_bwd)
+    overfull = (uown_f["overfull"] | uown_b["overfull"]).astype(jnp.int32)
+    fast = lax.psum(overfull, "pipe") == 0
+
+    def stacked(plans, key, counts):
+        return jnp.stack([p[key] for p, n in zip(plans, counts) for _ in range(n)])
+
+    inputs = (shared_bwd, values_bwd, upstream_bwd, shared_fwd, values_fwd)
+
+    def pack(arrays, send, rows):
         packed = [
             jnp.einsum(
                 "skt,tmf->smkf",
@@ -127,24 +206,73 @@
             )
             for index, array in enumerate(arrays)
         ]
-        stacked = jnp.stack(packed, axis=2).reshape(
-            group_count, len(arrays), slot_count, group_features
-        )
-        return lax.all_to_all(stacked, axes, split_axis=0, concat_axis=0, tiled=True)
-
-    def give_back(results, gather, send):
+        return jnp.stack(packed, axis=2).reshape(group_count, len(arrays), rows, group_features)
+
+    def padded_in(arrays):
+        send = stacked((own_b, own_f), 0, (3, 2))
+        gather = stacked((own_b, own_f), 1, (3, 2))
+        arrived = lax.all_to_all(
+            pack(arrays, send, slot_count), axes, split_axis=0, concat_axis=0, tiled=True
+        )
+        return jnp.einsum("airk,rakf->aif", gather, arrived, preferred_element_type=jnp.bfloat16)
+
+    def unit_in(arrays):
+        plans = (uown_b, uown_f)
+        counts = (3, 2)
+        arrived = lax.all_to_all(
+            pack(arrays, stacked(plans, "send", counts), unit),
+            axes, split_axis=0, concat_axis=0, tiled=True,
+        )
+        spare = jnp.einsum(
+            "ar,rapf->apf", stacked(plans, "foreign", counts), arrived,
+            preferred_element_type=jnp.bfloat16,
+        )
+        spares = lax.all_gather(spare, "seq", axis=0, tiled=False)
+        first = jnp.einsum(
+            "airp,rapf->aif", stacked(plans, "first", counts), arrived,
+            preferred_element_type=jnp.float32,
+        )
+        second = jnp.einsum(
+            "aibp,bapf->aif", stacked(plans, "second", counts), spares,
+            preferred_element_type=jnp.float32,
+        )
+        return (first + second).astype(jnp.bfloat16)
+
+    def padded_out(results):
+        gather = stacked((back_b, back_f), 1, (2, 1))
+        send = stacked((back_b, back_f), 0, (2, 1))
         placed = jnp.einsum("airk,aif->rakf", gather, results, preferred_element_type=jnp.bfloat16)
         arrived = lax.all_to_all(placed, axes, split_axis=0, concat_axis=0, tiled=True)
         arrived = arrived.reshape(seq_count, mp_count, results.shape[0], slot_count, group_features)
-        rows = jnp.einsum("askt,smakf->atmf", send, arrived, preferred_element_type=jnp.bfloat16)
-        return [row.reshape(1, tok_dev, features) for row in rows]
+        return jnp.einsum("askt,smakf->atmf", send, arrived, preferred_element_type=jnp.bfloat16)
+
+    def unit_out(results):
+        plans = (uback_b, uback_f)
+        counts = (2, 1)
+        spare = jnp.einsum(
+            "api,aif->apf", stacked(plans, "spare", counts), results,
+            preferred_element_type=jnp.bfloat16,
+        )
+        spares = lax.all_gather(spare, "seq", axis=0, tiled=False)
+        first = jnp.einsum(
+            "airp,aif->rapf", stacked(plans, "first", counts), results,
+            preferred_element_type=jnp.float32,
+        )
+        relayed = jnp.einsum(
+            "arb,bapf->rapf", stacked(plans, "relay", counts), spares,
+            preferred_element_type=jnp.float32,
+        )
+        placed = (first + relayed).astype(jnp.bfloat16)
+        arrived = lax.all_to_all(placed, axes, split_axis=0, concat_axis=0, tiled=True)
+        arrived = arrived.reshape(seq_count, mp_count, results.shape[0], unit, group_features)
+        return jnp.einsum(
+            "adpt,dmapf->atmf", stacked(plans, "send", counts), arrived,
+            preferred_element_type=jnp.bfloat16,
+        )
 
     positions_f = own_f[2].reshape(-1, CLUSTER)
     positions_b = own_b[2].reshape(-1, CLUSTER)
-    send_in = jnp.stack([own_b[0]] * 3 + [own_f[0]] * 2)
-    gather_in = jnp.stack([own_b[1]] * 3 + [own_f[1]] * 2)
-    arrived = exchange((shared_bwd, values_bwd, upstream_bwd, shared_fwd, values_fwd), send_in)
-    rows = jnp.einsum("airk,rakf->aif", gather_in, arrived, preferred_element_type=jnp.bfloat16)
+    rows = lax.cond(fast, unit_in, padded_in, inputs)
     rows = rows.reshape(5, 1, block_rows, heads_dev, HEAD_DIM)
     shared_grad, value_grad = backward_block(rows[0], rows[1], rows[2], positions_b, score_scale)
     moved_b = shifted(
@@ -152,12 +280,9 @@
     )
     attended = forward_block(rows[3], rows[4], positions_f, score_scale)
     moved_f = shifted(attended.reshape(1, block_rows, group_features), "pipe", 1)
-    shared_grad_in, values_grad_in, forward_in = give_back(
-        jnp.concatenate([moved_b, moved_f]),
-        jnp.stack([back_b[1]] * 2 + [back_f[1]]),
-        jnp.stack([back_b[0]] * 2 + [back_f[0]]),
-    )
-    return (forward_in, shared_grad_in, values_grad_in)
+    outs = lax.cond(fast, unit_out, padded_out, jnp.concatenate([moved_b, moved_f]))
+    outs = [row.reshape(1, tok_dev, features) for row in outs]
+    return (outs[2], outs[0], outs[1])
 
 
 def solution(mesh):

time: 146 us -> 222 us (1.52); the launches traced: 146 us -> 219 us
  blocking collectives: 0 us -> 61.9 us
  other arithmetic: 14 us -> 51.6 us
  waiting for transfers between devices: 68.3 us -> 37.4 us
  starting transfers between devices: 27.8 us -> 20.6 us
  local copies, waits for them, and re-layouts: 17.1 us -> 23.8 us
  between operations: 1.29 us -> 3.98 us
    all_to_all x2 -> x1, waiting for transfers between devices: 57.9 us -> 25.5 us  [unit_in(): lax.all_to_all(pack(arrays, stacked(plans, 'send', counts), unit), axes,...]
    all_gather x0 -> x2, blocking collectives: none -> 26 us  [the longest x1 13.1 us: unit_in(): spares = lax.all_gather(spare, 'seq', axis=0, tiled=False)]
    all_to_all x0 -> x1, blocking collectives: none -> 23.2 us  [unit_out(): lax.all_to_all(placed, axes, split_axis=0, concat_axis=0, tiled=True)]
    another operation x17 -> x32, other arithmetic: 5.09 us -> 24 us
    psum x0 -> x1, blocking collectives: none -> 12.7 us  [per_device(): fast = lax.psum(overfull, 'pipe') == 0]
    all_to_all x2 -> x1, starting transfers between devices: 13.5 us -> 7.45 us  [unit_in(): lax.all_to_all(pack(arrays, stacked(plans, 'send', counts), unit), axes,...]
    convert_element_type x1 -> x26, other arithmetic: 0.19 us -> 5.28 us  [the longest x2 1.23 us: unit_plan(): second_pick.astype(bf)]
    reduce_sum x0 -> x16, other arithmetic: none -> 5.09 us  [the longest x2 2.59 us: unit_plan(): owner = jnp.sum(match * blocks[:, None, None], axis=0)]
  transfers between devices with their start and end apart: 6 -> 5, of which waited for: 4 -> 2; matrix products, arithmetic and copies ran while one was open for 11% -> 18% of each run, Pallas kernels for 0% -> 0%
where the time goes in v4:
time: 222 us; the launch traced here: 219 us
  blocking collectives  61.9 us (28%)
  other arithmetic  51.6 us (23%)
  waiting for transfers between devices  37.4 us (17%)
  local copies, waits for them, and re-layouts  23.8 us (11%)
  starting transfers between devices  20.6 us (9%)
  matrix products  18.8 us (8%)
  between operations  3.98 us (2%)
    all_to_all x1, waiting for transfers between devices, unit_in(): lax.all_to_all(pack(arrays, stacked(plans, 'send', counts), unit), axes,...  25.5 us
    another operation x24, other arithmetic  23.8 us
    all_to_all x1, blocking collectives, unit_out(): lax.all_to_all(placed, axes, split_axis=0, concat_axis=0, tiled=True)  23.2 us
    ppermute x4, starting transfers between devices, shifted(): return lax.ppermute(block, axis, route)  13.1 us
    all_gather x1, blocking collectives, unit_in(): spares = lax.all_gather(spare, 'seq', axis=0, tiled=False)  13.1 us
    all_gather x1, blocking collectives, unit_out(): spares = lax.all_gather(spare, 'seq', axis=0, tiled=False)  12.9 us
    psum x1, blocking collectives, per_device(): fast = lax.psum(overfull, 'pipe') == 0  12.7 us
    ppermute x4, waiting for transfers between devices, shifted(): return lax.ppermute(block, axis, route)  11.9 us
  transfers between devices with their start and end apart: 5, of which 2 were waited for; matrix products, arithmetic and copies ran while one was open for 18% of the time, Pallas kernels for 0%

profile of v4, /device:TPU:96, one launch (start us, length us, event | category | flops | bytes accessed | tf_op | source)
XLA Modules:
  0.0 218.6 jit_solution(13842314808909976742)
XLA Ops:
  1.5 2.0 collective-permute-start
  3.5 5.0 %collective-permute-start.1 = (s32[2048]{0:T(1024)S(1)}, s32[2048]{0:T(1024)S(1)}, u32[]{:S(2)}, u32[]{:S(2)}) collective-permute-start(s32[2048]{0:T(1024)S(1)} %bitcast.436), channel_id=1, source_target_pairs={{0,32},{32,64},{64,96},{96,128},{128,160},{160,192},{192,224},{1,3... | collective-permute-start | bytes 24584 | tf_op jit(solution)/shard_map/ppermute | solution.py:18
  11.1 4.6 %reduce-window.110 = s32[8,32,2,128]{3,1,2,0:T(8,128)S(1)} reduce-window(s32[8,32,2,128]{3,1,2,0:T(8,128)S(1)} %fusion.102, s32[]{:T(128)} %constant.299.clone.1), window={size=1x1x1x128 pad=0_0x0_0x0_0x127_0}, to_apply=%region_43.44 | reduce-window | flops 8323072 | bytes 524292 | tf_op jit(solution)/shard_map/reduce-window.18
  17.1 4.6 %reduce-window.106 = s32[8,32,2,128]{3,1,2,0:T(8,128)S(1)} reduce-window(s32[8,32,2,128]{3,1,2,0:T(8,128)S(1)} %fusion.101, s32[]{:T(128)} %constant.299.clone.1), window={size=1x1x1x128 pad=0_0x0_0x0_0x127_0}, to_apply=%region_35.36 | reduce-window | flops 8323072 | bytes 524292 | tf_op jit(solution)/shard_map/reduce-window.16
  35.4 12.7 %psum.7 = s32[]{:T(128)} all-reduce(s32[]{:T(128)S(6)} %convert_element_type.334), channel_id=1, replica_groups=mesh['pipe'=8,'seq'=8,'mp'=4] {'pipe'}, use_global_device_ids=true, to_apply=%region_6.7 | all-reduce | flops 1 | bytes 8 | tf_op jit(solution)/shard_map/psum | solution.py:192
  54.8 4.6 %reduce-window.114 = s32[8,32,2,128]{3,1,2,0:T(8,128)S(1)} reduce-window(s32[8,32,2,128]{3,1,2,0:T(8,128)S(1)} %fusion.105, s32[]{:T(128)} %constant.299.clone.1), window={size=1x1x1x128 pad=0_0x0_0x0_0x127_0}, to_apply=%region_60.61 | reduce-window | flops 8323072 | bytes 524292 | tf_op jit(solution)/shard_map/reduce-window.20
  59.9 4.6 %reduce-window.116 = s32[8,32,2,128]{3,1,2,0:T(8,128)S(1)} reduce-window(s32[8,32,2,128]{3,1,2,0:T(8,128)S(1)} %fusion.106, s32[]{:T(128)} %constant.299.clone.1), window={size=1x1x1x128 pad=0_0x0_0x0_0x127_0}, to_apply=%region_63.64 | reduce-window | flops 8323072 | bytes 524292 | tf_op jit(solution)/shard_map/reduce-window.22
  78.0 61.6 %conditional.2 = (bf16[5,256,768]{2,1,0:T(8,128)(2,1)}) conditional(s32[]{:T(128)} %convert_element_type.335, (bf16[256,32,16]{0,1,2:T(8,128)(2,1)S(1)}, bf16[256,32,16]{0,1,2:T(8,128)(2,1)S(1)}, bf16[1,64,3072]{2,1,0:T(8,128)(2,1)S(1)}, bf16[8,16,64]{2,1,0:T(8,128)(2,1)S(1)}, bf16[1,64,3072]{2,1,0:T(8,128)(2,1)S(1)}, ...), branch_computations={%region_51.52_spmd, %region_52.53_spmd} | conditional | flops 1258291200 | bytes 56770656 | solution.py:275
  89.4 7.4 %all-to-all-start.2 = ((bf16[32,5,8,768]{3,2,1,0:T(8,128)(2,1)}), bf16[32,5,8,768]{3,2,1,0:T(8,128)(2,1)S(1)}, u32[]{:S(2)}, u32[]{:S(2)}) async-start(bf16[32,5,8,768]{3,2,1,0:T(8,128)(2,1)} %copy.312), calls=%async_computation.2 | async-start | bytes 3932160 | tf_op jit(solution)/shard_map/cond/branch_1_fun/all_to_all | solution.py:222
  97.7 25.5 %all-to-all-done.2 = bf16[32,5,8,768]{3,2,1,0:T(8,128)(2,1)S(1)} async-done(((bf16[32,5,8,768]{3,2,1,0:T(8,128)(2,1)}), bf16[32,5,8,768]{3,2,1,0:T(8,128)(2,1)S(1)}, u32[]{:S(2)}, u32[]{:S(2)}) %all-to-all-start.2) | async-done | bytes 1966112 | tf_op jit(solution)/shard_map/cond/branch_1_fun/all_to_all | solution.py:222
  123.7 13.1 %all-gather = bf16[40,8,768]{2,1,0:T(8,128)(2,1)S(1)} all-gather(bf16[5,8,768]{2,1,0:T(8,128)(2,1)S(1)} %bitcast.435), channel_id=2, replica_groups=mesh['pipe'=8,'seq'=8,'mp'=4] {'seq'}, dimensions={0}, use_global_device_ids=true | all-gather | bytes 552960 | tf_op jit(solution)/shard_map/cond/branch_1_fun/all_gather | solution.py:230
  137.5 2.1 fusion.15
  139.6 1.6 fusion.229
  142.1 1.9 fusion.231
  143.9 1.7 convolution_convert_fusion
  145.8 2.2 %collective-permute-start.3 = (bf16[1,256,768]{2,1,0:T(8,128)(2,1)S(1)}, bf16[1,256,768]{2,1,0:T(8,128)(2,1)S(1)}, u32[]{:S(2)}, u32[]{:S(2)}) collective-permute-start(bf16[1,256,768]{2,1,0:T(8,128)(2,1)S(1)} %copy.362), channel_id=1, source_target_pairs={{0,32},{32,64},{64,96},{96,128},{128,160},{160,192},{192,224},{1,3... | collective-permute-start | bytes 1179656 | tf_op jit(solution)/shard_map/ppermute | solution.py:18
  148.6 1.9 fusion.230
  150.5 1.9 convolution_convert_fusion.1
  154.4 3.8 %collective-permute-start.2 = (bf16[2,256,768]{2,1,0:T(8,128)(2,1)S(1)}, bf16[2,256,768]{2,1,0:T(8,128)(2,1)S(1)}, u32[]{:S(2)}, u32[]{:S(2)}) collective-permute-start(bf16[2,256,768]{2,1,0:T(8,128)(2,1)S(1)} %pad_maximum_fusion), channel_id=1, source_target_pairs={{32,0},{64,32},{96,64},{128,96},{160,128},{192,160},{224,192},{33,... | collective-permute-start | bytes 2359304 | tf_op jit(solution)/shard_map/ppermute | solution.py:18
  165.1 11.9 %collective-permute-done.2 = bf16[2,256,768]{2,1,0:T(8,128)(2,1)S(1)} collective-permute-done((bf16[2,256,768]{2,1,0:T(8,128)(2,1)S(1)}, bf16[2,256,768]{2,1,0:T(8,128)(2,1)S(1)}, u32[]{:S(2)}, u32[]{:S(2)}) %collective-permute-start.2) | collective-permute-done | bytes 786464 | tf_op jit(solution)/shard_map/ppermute | solution.py:18
  177.2 39.0 %conditional.3 = (bf16[3,64,4,768]{3,1,2,0:T(8,128)(2,1)S(1)}) conditional(s32[]{:T(128)} %convert_element_type.335, (bf16[8,16,64]{2,1,0:T(8,128)(2,1)S(1)}, bf16[8,16,64]{2,1,0:T(8,128)(2,1)S(1)}, bf16[256,32,16]{0,2,1:T(8,128)(2,1)S(1)}, bf16[256,32,16]{0,2,1:T(8,128)(2,1)S(1)}, bf16[3,256,768]{2,1,0:T(8,128)(2,1)S(1)}) %tuple.22, ...), branch_computations={%region_80.81_spmd, %region_81.82_spmd} | conditional | flops 755908608 | bytes 17072136 | solution.py:283
  177.4 12.9 %all-gather.1 = bf16[24,8,768]{2,1,0:T(8,128)(2,1)S(1)} all-gather(bf16[3,8,768]{2,1,0:T(8,128)(2,1)S(1)} %fusion.63), channel_id=3, replica_groups=mesh['pipe'=8,'seq'=8,'mp'=4] {'seq'}, dimensions={0}, use_global_device_ids=true | all-gather | bytes 331776 | tf_op jit(solution)/shard_map/cond/branch_1_fun/all_gather | solution.py:256
  190.8 1.5 fusion.49
  192.5 23.2 %all_to_all.17 = bf16[32,3,8,768]{3,2,1,0:T(8,128)(2,1)S(1)} all-to-all(bf16[32,3,8,768]{3,2,1,0:T(8,128)(2,1)S(1)} %copy.319), channel_id=1, replica_groups=mesh['pipe'=8,'seq'=8,'mp'=4] {'seq','mp'}, dimensions={0} | all-to-all | bytes 2359296 | tf_op jit(solution)/shard_map/cond/branch_1_fun/all_to_all | solution.py:266
  (362 shorter events, 63.1 us)
Async XLA Ops:
  1.5 49.1 %collective-permute-start = (s32[2048]{0:T(1024)S(1)}, s32[2048]{0:T(1024)S(1)}, u32[]{:S(2)}, u32[]{:S(2)}) collective-permute-start(s32[2048]{0:T(1024)S(1)} %bitcast.440), channel_id=1, source_target_pairs={{32,0},{64,32},{96,64},{128,96},{160,128},{192,160},{224,192},{33,... | collective-permute-start | bytes 24584 | tf_op jit(solution)/shard_map/ppermute | solution.py:18
  3.5 47.4 %collective-permute-start.1 = (s32[2048]{0:T(1024)S(1)}, s32[2048]{0:T(1024)S(1)}, u32[]{:S(2)}, u32[]{:S(2)}) collective-permute-start(s32[2048]{0:T(1024)S(1)} %bitcast.436), channel_id=1, source_target_pairs={{0,32},{32,64},{64,96},{96,128},{128,160},{160,192},{192,224},{1,3... | collective-permute-start | bytes 24584 | tf_op jit(solution)/shard_map/ppermute | solution.py:18
  59.6 18.4 %copy-start = (bf16[1,64,3072]{2,1,0:T(8,128)(2,1)S(1)}, bf16[1,64,3072]{2,1,0:T(8,128)(2,1)}, u32[]{:S(2)}) copy-start(bf16[1,64,3072]{2,1,0:T(8,128)(2,1)} %param.12) | copy-start | bytes 1179652
  59.6 18.4 %copy-start.1 = (bf16[1,64,3072]{2,1,0:T(8,128)(2,1)S(1)}, bf16[1,64,3072]{2,1,0:T(8,128)(2,1)}, u32[]{:S(2)}) copy-start(bf16[1,64,3072]{2,1,0:T(8,128)(2,1)} %param.13) | copy-start | bytes 1179652
  59.6 18.4 %copy-start.2 = (bf16[1,64,3072]{2,1,0:T(8,128)(2,1)S(1)}, bf16[1,64,3072]{2,1,0:T(8,128)(2,1)}, u32[]{:S(2)}) copy-start(bf16[1,64,3072]{2,1,0:T(8,128)(2,1)} %param.14) | copy-start | bytes 1179652
  59.6 18.4 %copy-start.3 = (bf16[1,64,3072]{2,1,0:T(8,128)(2,1)S(1)}, bf16[1,64,3072]{2,1,0:T(8,128)(2,1)}, u32[]{:S(2)}) copy-start(bf16[1,64,3072]{2,1,0:T(8,128)(2,1)} %param.10) | copy-start | bytes 1179652
  59.8 17.0 %copy-start.29 = (s32[8,8]{1,0:T(8,128)S(1)}, s32[8,8]{1,0:T(8,128)}, u32[]{:S(2)}) copy-start(s32[8,8]{1,0:T(8,128)} %multiply_add_fusion) | copy-start | bytes 772
  89.4 7.5 %copy-start.40 = (s32[1,32]{1,0:T(1,128)S(1)}, s32[1,32]{1,0:T(1,128)}, u32[]{:S(2)}) copy-start(s32[1,32]{1,0:T(1,128)} %get-tuple-element.288) | copy-start | bytes 388 | tf_op jit(solution)/shard_map/cond
  89.4 8.2 %copy-start.13 = (bf16[256,8,8]{0,2,1:T(8,128)(2,1)S(1)}, bf16[256,8,8]{0,2,1:T(8,128)(2,1)}, u32[]{:S(2)}) copy-start(bf16[256,8,8]{0,2,1:T(8,128)(2,1)} %get-tuple-element.97) | copy-start | bytes 98308 | tf_op jit(solution)/shard_map/cond
  89.4 33.9 %all-to-all-start.2 = ((bf16[32,5,8,768]{3,2,1,0:T(8,128)(2,1)}), bf16[32,5,8,768]{3,2,1,0:T(8,128)(2,1)S(1)}, u32[]{:S(2)}, u32[]{:S(2)}) async-start(bf16[32,5,8,768]{3,2,1,0:T(8,128)(2,1)} %copy.312), calls=%async_computation.2 | async-start | bytes 3932160 | tf_op jit(solution)/shard_map/cond/branch_1_fun/all_to_all | solution.py:222
  145.8 31.3 %collective-permute-start.3 = (bf16[1,256,768]{2,1,0:T(8,128)(2,1)S(1)}, bf16[1,256,768]{2,1,0:T(8,128)(2,1)S(1)}, u32[]{:S(2)}, u32[]{:S(2)}) collective-permute-start(bf16[1,256,768]{2,1,0:T(8,128)(2,1)S(1)} %copy.362), channel_id=1, source_target_pairs={{0,32},{32,64},{64,96},{96,128},{128,160},{160,192},{192,224},{1,3... | collective-permute-start | bytes 1179656 | tf_op jit(solution)/shard_map/ppermute | solution.py:18
  154.1 9.7 %copy-start.35 = (s32[1,256]{1,0:T(1,128)S(1)}, s32[1,256]{1,0:T(1,128)}, u32[]{:S(2)}) copy-start(s32[1,256]{1,0:T(1,128)} %get-tuple-element.267) | copy-start | bytes 3076
  154.1 9.7 %copy-start.38 = (pred[256]{0:T(512)(128)(4,1)S(1)}, pred[256]{0:T(512)(128)(4,1)}, u32[]{:S(2)}) copy-start(pred[256]{0:T(512)(128)(4,1)} %get-tuple-element.146) | copy-start | bytes 772
  154.1 9.8 %copy-start.32 = (pred[256,8]{0,1:T(8,128)(4,1)S(1)}, pred[256,8]{0,1:T(8,128)(4,1)}, u32[]{:S(2)}) copy-start(pred[256,8]{0,1:T(8,128)(4,1)} %iota_compare_fusion.39) | copy-start | bytes 6148
  154.1 9.8 %copy-start.34 = (s32[1,256]{1,0:T(1,128)S(1)}, s32[1,256]{1,0:T(1,128)}, u32[]{:S(2)}) copy-start(s32[1,256]{1,0:T(1,128)} %get-tuple-element.268) | copy-start | bytes 3076
  154.1 9.8 %copy-start.39 = (pred[256]{0:T(512)(128)(4,1)S(1)}, pred[256]{0:T(512)(128)(4,1)}, u32[]{:S(2)}) copy-start(pred[256]{0:T(512)(128)(4,1)} %get-tuple-element.148) | copy-start | bytes 772
  154.1 9.8 %copy-start.33 = (pred[256,8]{0,1:T(8,128)(4,1)S(1)}, pred[256,8]{0,1:T(8,128)(4,1)}, u32[]{:S(2)}) copy-start(pred[256,8]{0,1:T(8,128)(4,1)} %iota_compare_fusion.40) | copy-start | bytes 6148
  154.1 10.8 %copy-start.37 = (pred[32]{0:T(512)(128)(4,1)S(1)}, pred[32]{0:T(512)(128)(4,1)}, u32[]{:S(2)}) copy-start(pred[32]{0:T(512)(128)(4,1)} %get-tuple-element.270) | copy-start | bytes 100
  154.3 10.7 %copy-start.36 = (pred[32]{0:T(512)(128)(4,1)S(1)}, pred[32]{0:T(512)(128)(4,1)}, u32[]{:S(2)}) copy-start(pred[32]{0:T(512)(128)(4,1)} %get-tuple-element.269) | copy-start | bytes 100
  154.4 22.6 %collective-permute-start.2 = (bf16[2,256,768]{2,1,0:T(8,128)(2,1)S(1)}, bf16[2,256,768]{2,1,0:T(8,128)(2,1)S(1)}, u32[]{:S(2)}, u32[]{:S(2)}) collective-permute-start(bf16[2,256,768]{2,1,0:T(8,128)(2,1)S(1)} %pad_maximum_fusion), channel_id=1, source_target_pairs={{32,0},{64,32},{96,64},{128,96},{160,128},{192,160},{224,192},{33,... | collective-permute-start | bytes 2359304 | tf_op jit(solution)/shard_map/ppermute | solution.py:18
  164.0 13.2 %copy-start.15 = (bf16[8,8,64]{2,1,0:T(8,128)(2,1)S(1)}, bf16[8,8,64]{2,1,0:T(8,128)(2,1)}, u32[]{:S(2)}) copy-start(bf16[8,8,64]{2,1,0:T(8,128)(2,1)} %get-tuple-element.225) | copy-start | bytes 24580
  164.0 13.2 %copy-start.16 = (bf16[8,8,64]{2,1,0:T(8,128)(2,1)S(1)}, bf16[8,8,64]{2,1,0:T(8,128)(2,1)}, u32[]{:S(2)}) copy-start(bf16[8,8,64]{2,1,0:T(8,128)(2,1)} %get-tuple-element.227) | copy-start | bytes 24580
  164.0 13.2 %copy-start.27 = (bf16[8,256]{1,0:T(8,128)(2,1)S(1)}, bf16[8,256]{1,0:T(8,128)(2,1)}, u32[]{:S(2)}) copy-start(bf16[8,256]{1,0:T(8,128)(2,1)} %fusion.186) | copy-start | bytes 12292
  164.0 13.2 %copy-start.28 = (bf16[8,256]{1,0:T(8,128)(2,1)S(1)}, bf16[8,256]{1,0:T(8,128)(2,1)}, u32[]{:S(2)}) copy-start(bf16[8,256]{1,0:T(8,128)(2,1)} %fusion.184) | copy-start | bytes 12292
  (21 other events, 72.9 us)

commit v5 on v4

--- a/solution.py
+++ b/solution.py
@@ -96,7 +96,10 @@
     unit = 8
     source = (slot_tokens // tok_dev).reshape(seq_count, block_rows)
     member = (source[:, :, None] == jnp.arange(group_count)[None, None, :]).astype(jnp.int32)
-    before = jnp.cumsum(member, axis=1) - member
+    earlier = (jnp.arange(block_rows)[None, :] < jnp.arange(block_rows)[:, None]).astype(jnp.bfloat16)
+    before = jnp.einsum(
+        "ij,bjr->bir", earlier, member.astype(jnp.bfloat16), preferred_element_type=jnp.float32
+    ).astype(jnp.int32)
     slot_rank = jnp.sum(before * member, axis=2)
     second = slot_rank // unit
     place = slot_rank % unit
@@ -184,12 +187,14 @@
     def uplan(order):
         return unit_plan(order, seq_index, range_here, seq_count, group_count, tok_dev)
 
-    own_f, own_b = plan(order_fwd), plan(order_bwd)
-    back_f, back_b = plan(order_prev_fwd), plan(order_next_bwd)
-    uown_f, uown_b = uplan(order_fwd), uplan(order_bwd)
-    uback_f, uback_b = uplan(order_prev_fwd), uplan(order_next_bwd)
-    overfull = (uown_f["overfull"] | uown_b["overfull"]).astype(jnp.int32)
-    fast = lax.psum(overfull, "pipe") == 0
+    def overfull(order):
+        source = (order // tok_dev).reshape(seq_count, block_rows)
+        member = source[:, :, None] == jnp.arange(group_count)[None, None, :]
+        units = jnp.sum(member.astype(jnp.int32), axis=1) // (slot_count // 2)
+        return jnp.any(jnp.sum((units == 0).astype(jnp.int32), axis=1) > 1)
+
+    fast_in = ~(overfull(order_fwd) | overfull(order_bwd))
+    fast_out = ~(overfull(order_prev_fwd) | overfull(order_next_bwd))
 
     def stacked(plans, key, counts):
         return jnp.stack([p[key] for p, n in zip(plans, counts) for _ in range(n)])
@@ -209,6 +214,7 @@
         return jnp.stack(packed, axis=2).reshape(group_count, len(arrays), rows, group_features)
 
     def padded_in(arrays):
+        own_f, own_b = plan(order_fwd), plan(order_bwd)
         send = stacked((own_b, own_f), 0, (3, 2))
         gather = stacked((own_b, own_f), 1, (3, 2))
         arrived = lax.all_to_all(
@@ -217,7 +223,7 @@
         return jnp.einsum("airk,rakf->aif", gather, arrived, preferred_element_type=jnp.bfloat16)
 
     def unit_in(arrays):
-        plans = (uown_b, uown_f)
+        plans = (uplan(order_bwd), uplan(order_fwd))
         counts = (3, 2)
         arrived = lax.all_to_all(
             pack(arrays, stacked(plans, "send", counts), unit),
@@ -239,6 +245,7 @@
         return (first + second).astype(jnp.bfloat16)
 
     def padded_out(results):
+        back_f, back_b = plan(order_prev_fwd), plan(order_next_bwd)
         gather = stacked((back_b, back_f), 1, (2, 1))
         send = stacked((back_b, back_f), 0, (2, 1))
         placed = jnp.einsum("airk,aif->rakf", gather, results, preferred_element_type=jnp.bfloat16)
@@ -247,7 +254,7 @@
         return jnp.einsum("askt,smakf->atmf", send, arrived, preferred_element_type=jnp.bfloat16)
 
     def unit_out(results):
-        plans = (uback_b, uback_f)
+        plans = (uplan(order_next_bwd), uplan(order_prev_fwd))
         counts = (2, 1)
         spare = jnp.einsum(
             "api,aif->apf", stacked(plans, "spare", counts), results,
@@ -270,9 +277,9 @@
             preferred_element_type=jnp.bfloat16,
         )
 
-    positions_f = own_f[2].reshape(-1, CLUSTER)
-    positions_b = own_b[2].reshape(-1, CLUSTER)
-    rows = lax.cond(fast, unit_in, padded_in, inputs)
+    positions_f = lax.dynamic_slice_in_dim(order_fwd, seq_index * block_rows, block_rows)[None]
+    positions_b = lax.dynamic_slice_in_dim(order_bwd, seq_index * block_rows, block_rows)[None]
+    rows = lax.cond(fast_in, unit_in, padded_in, inputs)
     rows = rows.reshape(5, 1, block_rows, heads_dev, HEAD_DIM)
     shared_grad, value_grad = backward_block(rows[0], rows[1], rows[2], positions_b, score_scale)
     moved_b = shifted(
@@ -280,7 +287,7 @@
     )
     attended = forward_block(rows[3], rows[4], positions_f, score_scale)
     moved_f = shifted(attended.reshape(1, block_rows, group_features), "pipe", 1)
-    outs = lax.cond(fast, unit_out, padded_out, jnp.concatenate([moved_b, moved_f]))
+    outs = lax.cond(fast_out, unit_out, padded_out, jnp.concatenate([moved_b, moved_f]))
     outs = [row.reshape(1, tok_dev, features) for row in outs]
     return (outs[2], outs[0], outs[1])
 

time: 222 us -> 160 us (0.72); the launches traced: 219 us -> 159 us
  other arithmetic: 51.6 us -> 11.3 us
  blocking collectives: 61.9 us -> 26.2 us
  waiting for transfers between devices: 37.4 us -> 61.2 us
  local copies, waits for them, and re-layouts: 23.8 us -> 15.1 us
  starting transfers between devices: 20.6 us -> 25.8 us
  matrix products: 18.8 us -> 14.8 us
    another operation x24 -> x2, other arithmetic: 23.8 us -> 0.06 us  [stacked(): return jnp.stack([p[key] for p, n in zip(plans, counts) for _ in range(n)])]
    all_to_all x1 -> x0, blocking collectives: 23.2 us -> none  [unit_out(): lax.all_to_all(placed, axes, split_axis=0, concat_axis=0, tiled=True)]
    all_to_all x0 -> x1, waiting for transfers between devices: none -> 17.5 us  [unit_out(): lax.all_to_all(placed, axes, split_axis=0, concat_axis=0, tiled=True)]
    psum x1 -> x0, blocking collectives: 12.7 us -> none  [per_device(): fast = lax.psum(overfull, 'pipe') == 0]
    convert_element_type x34 -> x0, other arithmetic: 6.52 us -> none  [the longest x2 1.23 us: unit_plan(): second_pick.astype(bf)]
    ppermute x4, waiting for transfers between devices: 11.9 us -> 18 us  [shifted(): return lax.ppermute(block, axis, route)]
    all_to_all x0 -> x1, starting transfers between devices: none -> 4.47 us  [unit_out(): lax.all_to_all(placed, axes, split_axis=0, concat_axis=0, tiled=True)]
    another operation x32 -> x0, local copies, waits for them, and re-layouts: 3.17 us -> none
  transfers between devices with their start and end apart: 5 -> 6, of which waited for: 2 -> 3; matrix products, arithmetic and copies ran while one was open for 18% -> 19% of each run, Pallas kernels for 0% -> 0%
where the time goes in v5:
time: 160 us; the launch traced here: 159 us
  waiting for transfers between devices  61.2 us (38%)
  blocking collectives  26.2 us (16%)
  starting transfers between devices  25.8 us (16%)
  local copies, waits for them, and re-layouts  15.1 us (9%)
  matrix products  14.8 us (9%)
  other arithmetic  11.3 us (7%)
  between operations  3.58 us (2%)
    all_to_all x1, waiting for transfers between devices, unit_in(): lax.all_to_all(pack(arrays, stacked(plans, 'send', counts), unit), axes,...  25.7 us
    ppermute x4, waiting for transfers between devices, shifted(): return lax.ppermute(block, axis, route)  18 us
    all_to_all x1, waiting for transfers between devices, unit_out(): lax.all_to_all(placed, axes, split_axis=0, concat_axis=0, tiled=True)  17.5 us
    ppermute x4, starting transfers between devices, shifted(): return lax.ppermute(block, axis, route)  14 us
    all_gather x1, blocking collectives, unit_out(): spares = lax.all_gather(spare, 'seq', axis=0, tiled=False)  13.1 us
    all_gather x1, blocking collectives, unit_in(): spares = lax.all_gather(spare, 'seq', axis=0, tiled=False)  13.1 us
    all_to_all x1, starting transfers between devices, unit_in(): lax.all_to_all(pack(arrays, stacked(plans, 'send', counts), unit), axes,...  7.31 us
    all_to_all x1, starting transfers between devices, unit_out(): lax.all_to_all(placed, axes, split_axis=0, concat_axis=0, tiled=True)  4.47 us
  transfers between devices with their start and end apart: 6, of which 3 were waited for; matrix products, arithmetic and copies ran while one was open for 19% of the time, Pallas kernels for 0%

profile of v5, /device:TPU:96, one launch (start us, length us, event | category | flops | bytes accessed | tf_op | source)
XLA Modules:
  0.0 159.4 jit_solution(12290429536943335254)
XLA Ops:
  0.6 1.4 slice_reduce_fusion.8
  2.0 5.0 %collective-permute-start = (s32[2048]{0:T(1024)}, s32[2048]{0:T(1024)S(1)}, u32[]{:S(2)}, u32[]{:S(2)}) collective-permute-start(s32[2048]{0:T(1024)} %bitcast.117), channel_id=1, source_target_pairs={{0,32},{32,64},{64,96},{96,128},{128,160},{160,192},{192,224},{1,3... | collective-permute-start | bytes 24584 | tf_op jit(solution)/shard_map/ppermute | solution.py:18
  7.1 1.9 %collective-permute-start.1 = (s32[2048]{0:T(1024)}, s32[2048]{0:T(1024)S(1)}, u32[]{:S(2)}, u32[]{:S(2)}) collective-permute-start(s32[2048]{0:T(1024)} %bitcast.118), channel_id=1, source_target_pairs={{32,0},{64,32},{96,64},{128,96},{160,128},{192,160},{224,192},{33,... | collective-permute-start | bytes 24584 | tf_op jit(solution)/shard_map/ppermute | solution.py:18
  9.0 2.0 %fusion.298 = (s32[]{:T(128)}, s32[1,1,256]{2,1,0:T(1,128)S(1)}, s32[]{:T(128)}, s32[1,1,256]{2,1,0:T(1,128)}) fusion(s32[1,1,2048]{2,1,0:T(1,128)} %get-tuple-element.214, s32[]{:T(128)S(6)} %select_n.361, s32[1,1,2048]{2,1,0:T(1,128)} %get-tuple-element.213), kind=kLoop, calls=%fused_computation.694 | loop fusion | flops 510 | bytes 4108 | tf_op jit(solution)/shard_map/reduce_min | solution.py:24
  15.2 59.3 %conditional.2 = (bf16[5,256,768]{2,1,0:T(8,128)(2,1)S(1)}) conditional(s32[]{:T(128)} %convert_element_type.466, (s32[]{:T(128)}, s32[2048]{0:T(1024)}, s32[2048]{0:T(1024)}, s32[]{:T(128)}, bf16[1,64,3072]{2,1,0:T(8,128)(2,1)}, /*index=5*/bf16[1,64,3072]{2,1,0:T(8,128)(2,1)}, bf16[1,64,3072]{2,1,0:T(8,128)(2,1)}, ...), branch_computations={%region_12.27_spmd, %region_27.42_spmd} | conditional | flops 1262300416 | bytes 43633984 | solution.py:282
  24.5 0.9 constant_dynamic-update-slice_fusion.5
  25.4 7.3 %all-to-all-start = ((bf16[32,5,8,768]{3,2,1,0:T(8,128)(2,1)}), bf16[32,5,8,768]{3,2,1,0:T(8,128)(2,1)S(1)}, u32[]{:S(2)}, u32[]{:S(2)}) async-start(bf16[32,5,8,768]{3,2,1,0:T(8,128)(2,1)} %constant_dynamic-update-slice_fusion.5), calls=%async_computation | async-start | bytes 3932160 | tf_op jit(solution)/shard_map/cond/branch_1_fun/all_to_all | solution.py:228
  33.4 25.7 %all-to-all-done = bf16[32,5,8,768]{3,2,1,0:T(8,128)(2,1)S(1)} async-done(((bf16[32,5,8,768]{3,2,1,0:T(8,128)(2,1)}), bf16[32,5,8,768]{3,2,1,0:T(8,128)(2,1)S(1)}, u32[]{:S(2)}, u32[]{:S(2)}) %all-to-all-start) | async-done | bytes 1966112 | tf_op jit(solution)/shard_map/cond/branch_1_fun/all_to_all | solution.py:228
  59.6 13.1 %all-gather = bf16[40,8,768]{2,1,0:T(8,128)(2,1)S(1)} all-gather(bf16[5,8,768]{2,1,0:T(8,128)(2,1)S(1)} %bitcast.410), channel_id=2, replica_groups=mesh['pipe'=8,'seq'=8,'mp'=4] {'seq'}, dimensions={0}, use_global_device_ids=true | all-gather | bytes 552960 | tf_op jit(solution)/shard_map/cond/branch_1_fun/all_gather | solution.py:236
  75.3 1.2 copy.315
  76.7 1.9 %fusion.302 = (f32[6,256]{1,0:T(8,128)S(1)}, f32[6,256,256]{1,2,0:T(8,128)}) fusion(bf16[256,6,128]{0,2,1:T(8,128)(2,1)S(1)} %bitcast.408, pred[256,256]{0,1:T(8,128)(4,1)S(1)} %copy-done.9), kind=kOutput, calls=%fused_computation.698 | convolution fusion | flops 102236416 | bytes 2037760 | tf_op jit(solution)/shard_map/sub | solution.py:36
  78.6 1.7 %convolution_convert_fusion.4 = bf16[6,128,256]{2,1,0:T(8,128)(2,1)S(1)} fusion(bf16[256,6,128]{0,2,1:T(8,128)(2,1)S(1)} %bitcast.407, f32[6,256,256]{1,2,0:T(8,128)} %get-tuple-element.218, f32[6,256]{1,0:T(8,128)S(1)} %get-tuple-element.217), kind=kOutput, calls=%fused_computation.586 | convolution fusion | flops 101646336 | bytes 2365440 | tf_op jit(solution)/shard_map/nhqk,nkhd->nqhd/dot_general | solution.py:42
  80.5 5.1 %collective-permute-start.3 = (bf16[1,256,768]{2,1,0:T(8,128)(2,1)S(1)}, bf16[1,256,768]{2,1,0:T(8,128)(2,1)}, u32[]{:S(2)}, u32[]{:S(2)}) collective-permute-start(bf16[1,256,768]{2,1,0:T(8,128)(2,1)S(1)} %copy.280), channel_id=1, source_target_pairs={{0,32},{32,64},{64,96},{96,128},{128,160},{160,192},{192,224},{1,3... | collective-permute-start | bytes 1179656 | tf_op jit(solution)/shard_map/ppermute | solution.py:18
  86.9 1.3 fusion.301
  88.3 1.2 convolution_convert_fusion.5
  91.3 1.9 %collective-permute-start.2 = (bf16[2,256,768]{2,1,0:T(8,128)(2,1)S(1)}, bf16[2,256,768]{2,1,0:T(8,128)(2,1)S(1)}, u32[]{:S(2)}, u32[]{:S(2)}) collective-permute-start(bf16[2,256,768]{2,1,0:T(8,128)(2,1)S(1)} %pad_maximum_fusion), channel_id=1, source_target_pairs={{32,0},{64,32},{96,64},{128,96},{160,128},{192,160},{224,192},{33,... | collective-permute-start | bytes 2359304 | tf_op jit(solution)/shard_map/ppermute | solution.py:18
  96.0 18.0 %collective-permute-done.2 = bf16[2,256,768]{2,1,0:T(8,128)(2,1)S(1)} collective-permute-done((bf16[2,256,768]{2,1,0:T(8,128)(2,1)S(1)}, bf16[2,256,768]{2,1,0:T(8,128)(2,1)S(1)}, u32[]{:S(2)}, u32[]{:S(2)}) %collective-permute-start.2) | collective-permute-done | bytes 786464 | tf_op jit(solution)/shard_map/ppermute | solution.py:18
  114.0 1.0 constant_dynamic-update-slice_fusion.10
  115.0 41.9 %conditional.3 = (bf16[3,64,4,768]{3,1,2,0:T(8,128)(2,1)S(1)}) conditional(s32[]{:T(128)} %convert_element_type.461, (s32[2048]{0:T(1024)S(1)}, s32[]{:T(128)}, s32[2048]{0:T(1024)S(1)}, s32[]{:T(128)}, bf16[3,256,768]{2,1,0:T(8,128)(2,1)S(1)}) %tuple.22, (s32[]{:T(128)}, s32[2048]{0:T(1024)S(1)}, s32[2048]{0:T(1024)S(1)}, s32[]{:T(128)}, ...), branch_computations={%region_49.64_spmd, %region_64.81_spmd} | conditional | flops 759377088 | bytes 20034894 | solution.py:290
  116.7 13.1 %all-gather.1 = bf16[24,8,768]{2,1,0:T(8,128)(2,1)S(1)} all-gather(bf16[3,8,768]{2,1,0:T(8,128)(2,1)S(1)} %fusion.204), channel_id=3, replica_groups=mesh['pipe'=8,'seq'=8,'mp'=4] {'seq'}, dimensions={0}, use_global_device_ids=true | all-gather | bytes 331776 | tf_op jit(solution)/shard_map/cond/branch_1_fun/all_gather | solution.py:263
  130.7 1.5 fusion.175
  132.2 1.1 copy.259
  133.3 4.5 %all-to-all-start.1 = ((bf16[32,3,8,768]{3,2,1,0:T(8,128)(2,1)}), bf16[32,3,8,768]{3,2,1,0:T(8,128)(2,1)S(1)}, u32[]{:S(2)}, u32[]{:S(2)}) async-start(bf16[32,3,8,768]{3,2,1,0:T(8,128)(2,1)} %copy.259), calls=%async_computation.1 | async-start | bytes 2359296 | tf_op jit(solution)/shard_map/cond/branch_1_fun/all_to_all | solution.py:273
  138.7 17.5 %all-to-all-done.1 = bf16[32,3,8,768]{3,2,1,0:T(8,128)(2,1)S(1)} async-done(((bf16[32,3,8,768]{3,2,1,0:T(8,128)(2,1)}), bf16[32,3,8,768]{3,2,1,0:T(8,128)(2,1)S(1)}, u32[]{:S(2)}, u32[]{:S(2)}) %all-to-all-start.1) | async-done | bytes 1179680 | tf_op jit(solution)/shard_map/cond/branch_1_fun/all_to_all | solution.py:273
  (194 shorter events, 25.9 us)
Async XLA Ops:
  2.0 91.2 %collective-permute-start = (s32[2048]{0:T(1024)}, s32[2048]{0:T(1024)S(1)}, u32[]{:S(2)}, u32[]{:S(2)}) collective-permute-start(s32[2048]{0:T(1024)} %bitcast.117), channel_id=1, source_target_pairs={{0,32},{32,64},{64,96},{96,128},{128,160},{160,192},{192,224},{1,3... | collective-permute-start | bytes 24584 | tf_op jit(solution)/shard_map/ppermute | solution.py:18
  7.1 86.2 %collective-permute-start.1 = (s32[2048]{0:T(1024)}, s32[2048]{0:T(1024)S(1)}, u32[]{:S(2)}, u32[]{:S(2)}) collective-permute-start(s32[2048]{0:T(1024)} %bitcast.118), channel_id=1, source_target_pairs={{32,0},{64,32},{96,64},{128,96},{160,128},{192,160},{224,192},{33,... | collective-permute-start | bytes 24584 | tf_op jit(solution)/shard_map/ppermute | solution.py:18
  15.4 2.4 %copy-start = (bf16[1,64,3072]{2,1,0:T(8,128)(2,1)S(1)}, bf16[1,64,3072]{2,1,0:T(8,128)(2,1)}, u32[]{:S(2)}) copy-start(bf16[1,64,3072]{2,1,0:T(8,128)(2,1)} %get-tuple-element.75) | copy-start | bytes 1179652 | tf_op jit(solution)/shard_map/cond
  16.9 2.5 %copy-start.2 = (bf16[1,64,3072]{2,1,0:T(8,128)(2,1)S(1)}, bf16[1,64,3072]{2,1,0:T(8,128)(2,1)}, u32[]{:S(2)}) copy-start(bf16[1,64,3072]{2,1,0:T(8,128)(2,1)} %get-tuple-element.76) | copy-start | bytes 1179652 | tf_op jit(solution)/shard_map/cond
  18.3 1.7 %copy-start.4 = (bf16[1,64,3072]{2,1,0:T(8,128)(2,1)S(1)}, bf16[1,64,3072]{2,1,0:T(8,128)(2,1)}, u32[]{:S(2)}) copy-start(bf16[1,64,3072]{2,1,0:T(8,128)(2,1)} %get-tuple-element.77) | copy-start | bytes 1179652 | tf_op jit(solution)/shard_map/cond
  19.4 1.2 copy-start.6
  19.7 1.2 copy-start.8
  25.4 33.8 %all-to-all-start = ((bf16[32,5,8,768]{3,2,1,0:T(8,128)(2,1)}), bf16[32,5,8,768]{3,2,1,0:T(8,128)(2,1)S(1)}, u32[]{:S(2)}, u32[]{:S(2)}) async-start(bf16[32,5,8,768]{3,2,1,0:T(8,128)(2,1)} %constant_dynamic-update-slice_fusion.5), calls=%async_computation | async-start | bytes 3932160 | tf_op jit(solution)/shard_map/cond/branch_1_fun/all_to_all | solution.py:228
  75.3 1.4 copy-start.9
  78.6 7.0 %copy-start.10 = (s32[1,1,256]{2,1,0:T(1,128)S(1)}, s32[1,1,256]{2,1,0:T(1,128)}, u32[]{:S(2)}) copy-start(s32[1,1,256]{2,1,0:T(1,128)} %get-tuple-element.220) | copy-start | bytes 3076
  80.5 33.5 %collective-permute-start.3 = (bf16[1,256,768]{2,1,0:T(8,128)(2,1)S(1)}, bf16[1,256,768]{2,1,0:T(8,128)(2,1)}, u32[]{:S(2)}, u32[]{:S(2)}) collective-permute-start(bf16[1,256,768]{2,1,0:T(8,128)(2,1)S(1)} %copy.280), channel_id=1, source_target_pairs={{0,32},{32,64},{64,96},{96,128},{128,160},{160,192},{192,224},{1,3... | collective-permute-start | bytes 1179656 | tf_op jit(solution)/shard_map/ppermute | solution.py:18
  88.3 1.2 copy-start.11
  91.3 22.6 %collective-permute-start.2 = (bf16[2,256,768]{2,1,0:T(8,128)(2,1)S(1)}, bf16[2,256,768]{2,1,0:T(8,128)(2,1)S(1)}, u32[]{:S(2)}, u32[]{:S(2)}) collective-permute-start(bf16[2,256,768]{2,1,0:T(8,128)(2,1)S(1)} %pad_maximum_fusion), channel_id=1, source_target_pairs={{32,0},{64,32},{96,64},{128,96},{160,128},{192,160},{224,192},{33,... | collective-permute-start | bytes 2359304 | tf_op jit(solution)/shard_map/ppermute | solution.py:18
  133.3 22.8 %all-to-all-start.1 = ((bf16[32,3,8,768]{3,2,1,0:T(8,128)(2,1)}), bf16[32,3,8,768]{3,2,1,0:T(8,128)(2,1)S(1)}, u32[]{:S(2)}, u32[]{:S(2)}) async-start(bf16[32,3,8,768]{3,2,1,0:T(8,128)(2,1)} %copy.259), calls=%async_computation.1 | async-start | bytes 2359296 | tf_op jit(solution)/shard_map/cond/branch_1_fun/all_to_all | solution.py:273

commit v6 on v5

--- a/solution.py
+++ b/solution.py
@@ -148,6 +148,14 @@
     foreign = empty_here == 1
     spare = ((second_here == 1)[None, :] & at_place.T)
     relay = foreign[:, None] & (owner_here[:, None] == blocks[None, :])
+    forward_to = jnp.sum(relay.astype(jnp.int32) * blocks[None, :])
+    double_here = lax.dynamic_index_in_dim(double, seq_index, keepdims=False)
+    carrier_here = lax.dynamic_index_in_dim(carrier, seq_index, keepdims=False)
+    return_to = jnp.sum(double_here * carrier_here)
+    has_foreign = jnp.any(foreign)
+    has_spare = jnp.any(double_here == 1)
+    to_owner = (blocks == forward_to) & has_foreign
+    to_carrier = (blocks == return_to) & has_spare
     bf = jnp.bfloat16
     return dict(
         send=send.astype(bf),
@@ -156,6 +164,8 @@
         foreign=foreign.astype(bf),
         spare=spare.astype(bf),
         relay=relay.astype(bf),
+        to_owner=to_owner.astype(bf),
+        to_carrier=to_carrier.astype(bf),
         overfull=overfull,
     )
 
@@ -194,7 +204,10 @@
         return jnp.any(jnp.sum((units == 0).astype(jnp.int32), axis=1) > 1)
 
     fast_in = ~(overfull(order_fwd) | overfull(order_bwd))
-    fast_out = ~(overfull(order_prev_fwd) | overfull(order_next_bwd))
+    pipe_index = lax.axis_index("pipe")
+    first_plane = pipe_index == 0
+    last_plane = pipe_index == lax.axis_size("pipe") - 1
+    fast_out = ~((overfull(order_prev_fwd) & ~first_plane) | (overfull(order_next_bwd) & ~last_plane))
 
     def stacked(plans, key, counts):
         return jnp.stack([p[key] for p, n in zip(plans, counts) for _ in range(n)])
@@ -233,7 +246,11 @@
             "ar,rapf->apf", stacked(plans, "foreign", counts), arrived,
             preferred_element_type=jnp.bfloat16,
         )
-        spares = lax.all_gather(spare, "seq", axis=0, tiled=False)
+        spare = jnp.einsum(
+            "ab,apf->bapf", stacked(plans, "to_owner", counts), spare,
+            preferred_element_type=jnp.bfloat16,
+        )
+        spares = lax.all_to_all(spare, "seq", split_axis=0, concat_axis=0, tiled=True)
         first = jnp.einsum(
             "airp,rapf->aif", stacked(plans, "first", counts), arrived,
             preferred_element_type=jnp.float32,
@@ -260,7 +277,11 @@
             "api,aif->apf", stacked(plans, "spare", counts), results,
             preferred_element_type=jnp.bfloat16,
         )
-        spares = lax.all_gather(spare, "seq", axis=0, tiled=False)
+        spare = jnp.einsum(
+            "ab,apf->bapf", stacked(plans, "to_carrier", counts), spare,
+            preferred_element_type=jnp.bfloat16,
+        )
+        spares = lax.all_to_all(spare, "seq", split_axis=0, concat_axis=0, tiled=True)
         first = jnp.einsum(
             "airp,aif->rapf", stacked(plans, "first", counts), results,
             preferred_element_type=jnp.float32,
@@ -285,7 +306,8 @@
     moved_b = shifted(
         jnp.stack([shared_grad, value_grad]).reshape(2, block_rows, group_features), "pipe", -1
     )
-    attended = forward_block(rows[3], rows[4], positions_f, score_scale)
+    moved_b, rows_f = lax.optimization_barrier((moved_b, rows[3:]))
+    attended = forward_block(rows_f[0], rows_f[1], positions_f, score_scale)
     moved_f = shifted(attended.reshape(1, block_rows, group_features), "pipe", 1)
     outs = lax.cond(fast_out, unit_out, padded_out, jnp.concatenate([moved_b, moved_f]))
     outs = [row.reshape(1, tok_dev, features) for row in outs]

time: 160 us -> 171 us (1.069)
  blocking collectives: 26.2 us -> 0 us
  waiting for transfers between devices: 61.2 us -> 76.2 us
  other arithmetic: 11.3 us -> 22.9 us
  starting transfers between devices: 25.8 us -> 31.1 us
  matrix products: 14.8 us -> 18.8 us
    all_gather x2 -> x0, blocking collectives: 26.2 us -> none  [the longest x1 13.1 us: unit_out(): spares = lax.all_gather(spare, 'seq', axis=0, tiled=False)]
    all_to_all x0 -> x2, waiting for transfers between devices: none -> 14.5 us  [the longest x1 7.3 us: unit_in(): lax.all_to_all(spare, 'seq', split_axis=0, concat_axis=0, tiled=True)]
    all_to_all x0 -> x2, starting transfers between devices: none -> 7.3 us  [the longest x1 3.68 us: unit_out(): lax.all_to_all(spare, 'seq', split_axis=0, concat_axis=0, tiled=True)]
    and x0 -> x4, other arithmetic: none -> 5.05 us  [the longest x2 2.54 us: unit_plan(): to_carrier = (blocks == return_to) & has_spare]
    ppermute x4, waiting for transfers between devices: 18 us -> 23 us  [shifted(): return lax.ppermute(block, axis, route)]
    all_to_all x1, waiting for transfers between devices: 25.7 us -> 21.1 us  [unit_in(): lax.all_to_all(pack(arrays, stacked(plans, 'send', counts), unit), axes,...]
    reduce_or x0 -> x4, other arithmetic: none -> 2.68 us  [the longest x2 1.35 us: unit_plan(): has_spare = jnp.any(double_here == 1)]
    dot_general x1, matrix products: 0.72 us -> 2.83 us  [unit_in(): jnp.einsum('aibp,bapf->aif', stacked(plans, 'second', counts), spares, pr...]
  transfers between devices with their start and end apart: 6 -> 8, of which waited for: 3 -> 6; matrix products, arithmetic and copies ran while one was open for 19% -> 21% of each run, Pallas kernels for 0% -> 0%
where the time goes in v6:
time: 171 us; the launch traced here: 170 us
  waiting for transfers between devices  76.2 us (45%)
  starting transfers between devices  31.1 us (18%)
  other arithmetic  22.9 us (13%)
  matrix products  18.8 us (11%)
  local copies, waits for them, and re-layouts  15.8 us (9%)
  between operations  3.54 us (2%)
    ppermute x4, waiting for transfers between devices, shifted(): return lax.ppermute(block, axis, route)  23 us
    all_to_all x1, waiting for transfers between devices, unit_in(): lax.all_to_all(pack(arrays, stacked(plans, 'send', counts), unit), axes,...  21.1 us
    all_to_all x1, waiting for transfers between devices, unit_out(): lax.all_to_all(placed, axes, split_axis=0, concat_axis=0, tiled=True)  17.5 us
    ppermute x4, starting transfers between devices, shifted(): return lax.ppermute(block, axis, route)  12.5 us
    all_to_all x1, starting transfers between devices, unit_in(): lax.all_to_all(pack(arrays, stacked(plans, 'send', counts), unit), axes,...  7.3 us
    all_to_all x1, waiting for transfers between devices, unit_in(): lax.all_to_all(spare, 'seq', split_axis=0, concat_axis=0, tiled=True)  7.3 us
    all_to_all x1, waiting for transfers between devices, unit_out(): lax.all_to_all(spare, 'seq', split_axis=0, concat_axis=0, tiled=True)  7.23 us
    all_to_all x1, starting transfers between devices, unit_out(): lax.all_to_all(placed, axes, split_axis=0, concat_axis=0, tiled=True)  3.96 us
  transfers between devices with their start and end apart: 8, of which 6 were waited for; matrix products, arithmetic and copies ran while one was open for 21% of the time, Pallas kernels for 0%

profile of v6, /device:TPU:96, one launch (start us, length us, event | category | flops | bytes accessed | tf_op | source)
XLA Modules:
  0.0 169.7 jit_solution(7783384748690626460)
XLA Ops:
  0.6 1.4 slice_reduce_fusion.8
  2.0 5.0 %collective-permute-start = (s32[2048]{0:T(1024)}, s32[2048]{0:T(1024)S(1)}, u32[]{:S(2)}, u32[]{:S(2)}) collective-permute-start(s32[2048]{0:T(1024)} %bitcast.121), channel_id=1, source_target_pairs={{0,32},{32,64},{64,96},{96,128},{128,160},{160,192},{192,224},{1,3... | collective-permute-start | bytes 24584 | tf_op jit(solution)/shard_map/ppermute | solution.py:18
  7.1 1.9 %collective-permute-start.1 = (s32[2048]{0:T(1024)}, s32[2048]{0:T(1024)S(1)}, u32[]{:S(2)}, u32[]{:S(2)}) collective-permute-start(s32[2048]{0:T(1024)} %bitcast.122), channel_id=1, source_target_pairs={{32,0},{64,32},{96,64},{128,96},{160,128},{192,160},{224,192},{33,... | collective-permute-start | bytes 24584 | tf_op jit(solution)/shard_map/ppermute | solution.py:18
  9.0 1.4 fusion.314
  14.0 62.6 %conditional.2 = (bf16[5,256,768]{2,1,0:T(8,128)(2,1)S(1)}) conditional(s32[]{:T(128)} %convert_element_type.500, (s32[]{:T(128)}, s32[2048]{0:T(1024)}, s32[2048]{0:T(1024)}, s32[]{:T(128)}, bf16[1,64,3072]{2,1,0:T(8,128)(2,1)}, /*index=5*/bf16[1,64,3072]{2,1,0:T(8,128)(2,1)}, bf16[1,64,3072]{2,1,0:T(8,128)(2,1)}, ...), branch_computations={%region_12.27_spmd, %region_27.48_spmd} | conditional | flops 1262300416 | bytes 43633984 | solution.py:303
  24.9 7.3 %all-to-all-start = ((bf16[32,5,8,768]{3,2,1,0:T(8,128)(2,1)}), bf16[32,5,8,768]{3,2,1,0:T(8,128)(2,1)S(1)}, u32[]{:S(2)}, u32[]{:S(2)}) async-start(bf16[32,5,8,768]{3,2,1,0:T(8,128)(2,1)} %constant_dynamic-update-slice_fusion.5), calls=%async_computation | async-start | bytes 3932160 | tf_op jit(solution)/shard_map/cond/branch_1_fun/all_to_all | solution.py:241
  37.5 21.1 %all-to-all-done = bf16[32,5,8,768]{3,2,1,0:T(8,128)(2,1)S(1)} async-done(((bf16[32,5,8,768]{3,2,1,0:T(8,128)(2,1)}), bf16[32,5,8,768]{3,2,1,0:T(8,128)(2,1)S(1)}, u32[]{:S(2)}, u32[]{:S(2)}) %all-to-all-start) | async-done | bytes 1966112 | tf_op jit(solution)/shard_map/cond/branch_1_fun/all_to_all | solution.py:241
  60.0 3.6 %all-to-all-start.1 = ((bf16[8,5,8,768]{3,2,1,0:T(8,128)(2,1)}), bf16[8,5,8,768]{3,2,1,0:T(8,128)(2,1)S(1)}, u32[]{:S(2)}, u32[]{:S(2)}) async-start(bf16[8,5,8,768]{3,2,1,0:T(8,128)(2,1)} %multiply_bitcast_fusion), calls=%async_computation.1 | async-start | bytes 983040 | tf_op jit(solution)/shard_map/cond/branch_1_fun/all_to_all | solution.py:253
  63.6 2.7 %fusion.58 = f32[5,256,768,1]{2,1,3,0:T(8,128)} fusion(pred[5,256,32,8]{1,2,3,0:T(8,128)(4,1)S(1)} %and_dynamic-update-slice_fusion.9, bf16[32,5,8,768]{3,2,1,0:T(8,128)(2,1)S(1)} %all-to-all-done), kind=kOutput, calls=%fused_computation.106 | convolution fusion | flops 503316480 | bytes 6225920 | tf_op jit(solution)/shard_map/cond/branch_1_fun/airp,rapf->aif/dot_general | solution.py:254
  66.2 7.3 %all-to-all-done.1 = bf16[8,5,8,768]{3,2,1,0:T(8,128)(2,1)S(1)} async-done(((bf16[8,5,8,768]{3,2,1,0:T(8,128)(2,1)}), bf16[8,5,8,768]{3,2,1,0:T(8,128)(2,1)S(1)}, u32[]{:S(2)}, u32[]{:S(2)}) %all-to-all-start.1) | async-done | bytes 491552 | tf_op jit(solution)/shard_map/cond/branch_1_fun/all_to_all | solution.py:253
  73.5 2.8 %fusion.55 = bf16[5,256,768]{2,1,0:T(8,128)(2,1)S(1)} fusion(f32[5,256,768,1]{2,1,3,0:T(8,128)} %fusion.58, pred[5,256,8,8]{1,3,2,0:T(8,128)(4,1)S(1)} %and_dynamic-update-slice_fusion.14, bf16[8,5,8,768]{3,2,1,0:T(8,128)(2,1)S(1)} %all-to-all-done.1), kind=kOutput, calls=%fused_computation.103 | convolution fusion | flops 127795200 | bytes 6471680 | tf_op jit(solution)/shard_map/cond/branch_1_fun/aibp,bapf->aif/dot_general | solution.py:258
  80.3 1.8 %fusion.268 = f32[256,6]{0,1:T(8,128)S(1)} fusion(bf16[256,6,128]{0,2,1:T(8,128)(2,1)S(1)} %bitcast.417, bf16[1,256,6,128]{1,3,2,0:T(8,128)(2,1)S(1)} %bitcast.421, f32[6,256,256]{1,2,0:T(8,128)} %copy-done.10, f32[6,256]{1,0:T(8,128)S(1)} %get-tuple-element.243), kind=kOutput, calls=%fused_computation.623 | convolution fusion | flops 102038016 | bytes 2371584 | tf_op jit(solution)/shard_map/nhqk,nkhd->nqhd/dot_general | solution.py:50
  83.7 1.9 %collective-permute-start.2 = (bf16[2,256,768]{2,1,0:T(8,128)(2,1)S(1)}, bf16[2,256,768]{2,1,0:T(8,128)(2,1)S(1)}, u32[]{:S(2)}, u32[]{:S(2)}) collective-permute-start(bf16[2,256,768]{2,1,0:T(8,128)(2,1)S(1)} %pad_maximum_fusion), channel_id=1, source_target_pairs={{32,0},{64,32},{96,64},{128,96},{160,128},{192,160},{224,192},{33,... | collective-permute-start | bytes 2359304 | tf_op jit(solution)/shard_map/ppermute | solution.py:18
  88.5 17.6 %collective-permute-done.2 = bf16[2,256,768]{2,1,0:T(8,128)(2,1)S(1)} collective-permute-done((bf16[2,256,768]{2,1,0:T(8,128)(2,1)S(1)}, bf16[2,256,768]{2,1,0:T(8,128)(2,1)S(1)}, u32[]{:S(2)}, u32[]{:S(2)}) %collective-permute-start.2) | collective-permute-done | bytes 786464 | tf_op jit(solution)/shard_map/ppermute | solution.py:18
  106.5 1.8 %fusion.318 = (f32[6,256]{1,0:T(8,128)S(1)}, f32[6,256,256]{1,2,0:T(8,128)}) fusion(pred[256,256]{0,1:T(8,128)(4,1)S(1)} %fusion.273, bf16[2,1,256,6,128]{4,2,3,1,0:T(8,128)(2,1)S(1)} %copy.272), kind=kOutput, calls=%fused_computation.737 | convolution fusion | flops 102236416 | bytes 2037760 | tf_op jit(solution)/shard_map/sub | solution.py:36
  108.3 1.7 convolution_convert_fusion.4
  110.1 3.6 %collective-permute-start.3 = (bf16[1,256,768]{2,1,0:T(8,128)(2,1)S(1)}, bf16[1,256,768]{2,1,0:T(8,128)(2,1)S(1)}, u32[]{:S(2)}, u32[]{:S(2)}) collective-permute-start(bf16[1,256,768]{2,1,0:T(8,128)(2,1)S(1)} %copy.274), channel_id=1, source_target_pairs={{0,32},{32,64},{64,96},{96,128},{128,160},{160,192},{192,224},{1,3... | collective-permute-start | bytes 1179656 | tf_op jit(solution)/shard_map/ppermute | solution.py:18
  116.6 5.5 %collective-permute-done.3 = bf16[1,256,768]{2,1,0:T(8,128)(2,1)S(1)} collective-permute-done((bf16[1,256,768]{2,1,0:T(8,128)(2,1)S(1)}, bf16[1,256,768]{2,1,0:T(8,128)(2,1)S(1)}, u32[]{:S(2)}, u32[]{:S(2)}) %collective-permute-start.3) | collective-permute-done | bytes 393248 | tf_op jit(solution)/shard_map/ppermute | solution.py:18
  122.1 45.3 %conditional.3 = (bf16[3,64,4,768]{3,1,2,0:T(8,128)(2,1)S(1)}) conditional(s32[]{:T(128)} %convert_element_type.495, (s32[2048]{0:T(1024)S(1)}, s32[]{:T(128)}, s32[2048]{0:T(1024)S(1)}, s32[]{:T(128)}, bf16[3,256,768]{2,1,0:T(8,128)(2,1)S(1)}) %tuple.24, (s32[]{:T(128)}, s32[2048]{0:T(1024)S(1)}, s32[2048]{0:T(1024)S(1)}, s32[]{:T(128)}, ...), branch_computations={%region_55.70_spmd, %region_70.91_spmd} | conditional | flops 759377088 | bytes 20034894 | solution.py:312
  129.8 3.7 %all-to-all-start.2 = ((bf16[8,3,8,768]{3,2,1,0:T(8,128)(2,1)}), bf16[8,3,8,768]{3,2,1,0:T(8,128)(2,1)S(1)}, u32[]{:S(2)}, u32[]{:S(2)}) async-start(bf16[8,3,8,768]{3,2,1,0:T(8,128)(2,1)} %multiply_bitcast_fusion.1), calls=%async_computation.2 | async-start | bytes 589824 | tf_op jit(solution)/shard_map/cond/branch_1_fun/all_to_all | solution.py:284
  133.8 7.2 %all-to-all-done.2 = bf16[8,3,8,768]{3,2,1,0:T(8,128)(2,1)S(1)} async-done(((bf16[8,3,8,768]{3,2,1,0:T(8,128)(2,1)}), bf16[8,3,8,768]{3,2,1,0:T(8,128)(2,1)S(1)}, u32[]{:S(2)}, u32[]{:S(2)}) %all-to-all-start.2) | async-done | bytes 294944 | tf_op jit(solution)/shard_map/cond/branch_1_fun/all_to_all | solution.py:284
  141.5 1.5 fusion.181
  144.2 4.0 %all-to-all-start.3 = ((bf16[32,3,8,768]{3,2,1,0:T(8,128)(2,1)}), bf16[32,3,8,768]{3,2,1,0:T(8,128)(2,1)S(1)}, u32[]{:S(2)}, u32[]{:S(2)}) async-start(bf16[32,3,8,768]{3,2,1,0:T(8,128)(2,1)} %copy.254), calls=%async_computation.3 | async-start | bytes 2359296 | tf_op jit(solution)/shard_map/cond/branch_1_fun/all_to_all | solution.py:294
  149.0 17.5 %all-to-all-done.3 = bf16[32,3,8,768]{3,2,1,0:T(8,128)(2,1)S(1)} async-done(((bf16[32,3,8,768]{3,2,1,0:T(8,128)(2,1)}), bf16[32,3,8,768]{3,2,1,0:T(8,128)(2,1)S(1)}, u32[]{:S(2)}, u32[]{:S(2)}) %all-to-all-start.3) | async-done | bytes 1179680 | tf_op jit(solution)/shard_map/cond/branch_1_fun/all_to_all | solution.py:294
  (209 shorter events, 42.3 us)
Async XLA Ops:
  2.0 85.8 %collective-permute-start = (s32[2048]{0:T(1024)}, s32[2048]{0:T(1024)S(1)}, u32[]{:S(2)}, u32[]{:S(2)}) collective-permute-start(s32[2048]{0:T(1024)} %bitcast.121), channel_id=1, source_target_pairs={{0,32},{32,64},{64,96},{96,128},{128,160},{160,192},{192,224},{1,3... | collective-permute-start | bytes 24584 | tf_op jit(solution)/shard_map/ppermute | solution.py:18
  7.1 80.9 %collective-permute-start.1 = (s32[2048]{0:T(1024)}, s32[2048]{0:T(1024)S(1)}, u32[]{:S(2)}, u32[]{:S(2)}) collective-permute-start(s32[2048]{0:T(1024)} %bitcast.122), channel_id=1, source_target_pairs={{32,0},{64,32},{96,64},{128,96},{160,128},{192,160},{224,192},{33,... | collective-permute-start | bytes 24584 | tf_op jit(solution)/shard_map/ppermute | solution.py:18
  14.2 3.0 %copy-start.1 = (bf16[1,64,3072]{2,1,0:T(8,128)(2,1)S(1)}, bf16[1,64,3072]{2,1,0:T(8,128)(2,1)}, u32[]{:S(2)}) copy-start(bf16[1,64,3072]{2,1,0:T(8,128)(2,1)} %get-tuple-element.75) | copy-start | bytes 1179652 | tf_op jit(solution)/shard_map/cond
  16.4 2.7 %copy-start.3 = (bf16[1,64,3072]{2,1,0:T(8,128)(2,1)S(1)}, bf16[1,64,3072]{2,1,0:T(8,128)(2,1)}, u32[]{:S(2)}) copy-start(bf16[1,64,3072]{2,1,0:T(8,128)(2,1)} %get-tuple-element.76) | copy-start | bytes 1179652 | tf_op jit(solution)/shard_map/cond
  18.0 1.7 %copy-start.5 = (bf16[1,64,3072]{2,1,0:T(8,128)(2,1)S(1)}, bf16[1,64,3072]{2,1,0:T(8,128)(2,1)}, u32[]{:S(2)}) copy-start(bf16[1,64,3072]{2,1,0:T(8,128)(2,1)} %get-tuple-element.77) | copy-start | bytes 1179652 | tf_op jit(solution)/shard_map/cond
  19.1 1.2 copy-start.7
  19.3 1.2 copy-start.9
  24.9 33.8 %all-to-all-start = ((bf16[32,5,8,768]{3,2,1,0:T(8,128)(2,1)}), bf16[32,5,8,768]{3,2,1,0:T(8,128)(2,1)S(1)}, u32[]{:S(2)}, u32[]{:S(2)}) async-start(bf16[32,5,8,768]{3,2,1,0:T(8,128)(2,1)} %constant_dynamic-update-slice_fusion.5), calls=%async_computation | async-start | bytes 3932160 | tf_op jit(solution)/shard_map/cond/branch_1_fun/all_to_all | solution.py:241
  60.0 13.6 %all-to-all-start.1 = ((bf16[8,5,8,768]{3,2,1,0:T(8,128)(2,1)}), bf16[8,5,8,768]{3,2,1,0:T(8,128)(2,1)S(1)}, u32[]{:S(2)}, u32[]{:S(2)}) async-start(bf16[8,5,8,768]{3,2,1,0:T(8,128)(2,1)} %multiply_bitcast_fusion), calls=%async_computation.1 | async-start | bytes 983040 | tf_op jit(solution)/shard_map/cond/branch_1_fun/all_to_all | solution.py:253
  76.6 1.3 copy-start
  79.1 1.1 copy-start.10
  80.3 1.9 %copy-start.11 = (f32[6,256,256]{1,2,0:T(8,128)S(1)}, f32[6,256,256]{1,2,0:T(8,128)}, u32[]{:S(2)}) copy-start(f32[6,256,256]{1,2,0:T(8,128)} %copy-done.10) | copy-start | bytes 4718596
  83.7 22.4 %collective-permute-start.2 = (bf16[2,256,768]{2,1,0:T(8,128)(2,1)S(1)}, bf16[2,256,768]{2,1,0:T(8,128)(2,1)S(1)}, u32[]{:S(2)}, u32[]{:S(2)}) collective-permute-start(bf16[2,256,768]{2,1,0:T(8,128)(2,1)S(1)} %pad_maximum_fusion), channel_id=1, source_target_pairs={{32,0},{64,32},{96,64},{128,96},{160,128},{192,160},{224,192},{33,... | collective-permute-start | bytes 2359304 | tf_op jit(solution)/shard_map/ppermute | solution.py:18
  110.1 11.9 %collective-permute-start.3 = (bf16[1,256,768]{2,1,0:T(8,128)(2,1)S(1)}, bf16[1,256,768]{2,1,0:T(8,128)(2,1)S(1)}, u32[]{:S(2)}, u32[]{:S(2)}) collective-permute-start(bf16[1,256,768]{2,1,0:T(8,128)(2,1)S(1)} %copy.274), channel_id=1, source_target_pairs={{0,32},{32,64},{64,96},{96,128},{128,160},{160,192},{192,224},{1,3... | collective-permute-start | bytes 1179656 | tf_op jit(solution)/shard_map/ppermute | solution.py:18
  129.8 11.2 %all-to-all-start.2 = ((bf16[8,3,8,768]{3,2,1,0:T(8,128)(2,1)}), bf16[8,3,8,768]{3,2,1,0:T(8,128)(2,1)S(1)}, u32[]{:S(2)}, u32[]{:S(2)}) async-start(bf16[8,3,8,768]{3,2,1,0:T(8,128)(2,1)} %multiply_bitcast_fusion.1), calls=%async_computation.2 | async-start | bytes 589824 | tf_op jit(solution)/shard_map/cond/branch_1_fun/all_to_all | solution.py:284
  144.2 22.3 %all-to-all-start.3 = ((bf16[32,3,8,768]{3,2,1,0:T(8,128)(2,1)}), bf16[32,3,8,768]{3,2,1,0:T(8,128)(2,1)S(1)}, u32[]{:S(2)}, u32[]{:S(2)}) async-start(bf16[32,3,8,768]{3,2,1,0:T(8,128)(2,1)} %copy.254), calls=%async_computation.3 | async-start | bytes 2359296 | tf_op jit(solution)/shard_map/cond/branch_1_fun/all_to_all | solution.py:294

commit v7 on v3

--- a/solution.py
+++ b/solution.py
@@ -106,31 +106,38 @@
     slot_count = 2 * block_rows // group_count
     score_scale = 1.0 / math.sqrt(HEAD_DIM)
     axes = ("seq", "mp")
+    pipe_index = lax.axis_index("pipe")
+    last_plane = pipe_index == lax.axis_size("pipe") - 1
     order_fwd = cluster_order[0, 0]
-    order_bwd = cluster_order[0, 1]
+    order_next_bwd, shared_bwd, values_bwd, upstream_bwd = shifted(
+        (cluster_order[0, 1], shared_bwd, values_bwd, upstream_bwd), "pipe", -1
+    )
     order_prev_fwd = shifted(order_fwd, "pipe", 1)
-    order_next_bwd = shifted(order_bwd, "pipe", -1)
 
     def plan(order):
         return route_plan(order, seq_index, range_here, seq_count, group_count, tok_dev, slot_count)
 
-    own_f, own_b = plan(order_fwd), plan(order_bwd)
-    back_f, back_b = plan(order_prev_fwd), plan(order_next_bwd)
+    own_f, next_b, prev_f = plan(order_fwd), plan(order_next_bwd), plan(order_prev_fwd)
 
     def exchange(arrays, send):
         packed = [
             jnp.einsum(
                 "skt,tmf->smkf",
-                send[index],
+                send,
                 array[0].reshape(tok_dev, mp_count, group_features),
                 preferred_element_type=jnp.bfloat16,
             )
-            for index, array in enumerate(arrays)
+            for array in arrays
         ]
         stacked = jnp.stack(packed, axis=2).reshape(
             group_count, len(arrays), slot_count, group_features
         )
-        return lax.all_to_all(stacked, axes, split_axis=0, concat_axis=0, tiled=True)
+        arrived = lax.all_to_all(stacked, axes, split_axis=0, concat_axis=0, tiled=True)
+        return arrived
+
+    def gather_block(arrived, gather):
+        rows = jnp.einsum("irk,rakf->aif", gather, arrived, preferred_element_type=jnp.bfloat16)
+        return rows.reshape(rows.shape[0], 1, block_rows, heads_dev, HEAD_DIM)
 
     def give_back(results, gather, send):
         placed = jnp.einsum("airk,aif->rakf", gather, results, preferred_element_type=jnp.bfloat16)
@@ -139,23 +146,21 @@
         rows = jnp.einsum("askt,smakf->atmf", send, arrived, preferred_element_type=jnp.bfloat16)
         return [row.reshape(1, tok_dev, features) for row in rows]
 
-    positions_f = own_f[2].reshape(-1, CLUSTER)
-    positions_b = own_b[2].reshape(-1, CLUSTER)
-    send_in = jnp.stack([own_b[0]] * 3 + [own_f[0]] * 2)
-    gather_in = jnp.stack([own_b[1]] * 3 + [own_f[1]] * 2)
-    arrived = exchange((shared_bwd, values_bwd, upstream_bwd, shared_fwd, values_fwd), send_in)
-    rows = jnp.einsum("airk,rakf->aif", gather_in, arrived, preferred_element_type=jnp.bfloat16)
-    rows = rows.reshape(5, 1, block_rows, heads_dev, HEAD_DIM)
-    shared_grad, value_grad = backward_block(rows[0], rows[1], rows[2], positions_b, score_scale)
-    moved_b = shifted(
-        jnp.stack([shared_grad, value_grad]).reshape(2, block_rows, group_features), "pipe", -1
+    arrived_f = exchange((shared_fwd, values_fwd), own_f[0])
+    rows_f = gather_block(arrived_f, own_f[1])
+    arrived_b = exchange((shared_bwd, values_bwd, upstream_bwd), next_b[0])
+    attended = forward_block(rows_f[0], rows_f[1], own_f[2].reshape(-1, CLUSTER), score_scale)
+    moved_f = shifted(attended.reshape(1, block_rows, group_features), "pipe", 1)
+    rows_b = gather_block(arrived_b, next_b[1])
+    shared_grad, value_grad = backward_block(
+        rows_b[0], rows_b[1], rows_b[2], next_b[2].reshape(-1, CLUSTER), score_scale
     )
-    attended = forward_block(rows[3], rows[4], positions_f, score_scale)
-    moved_f = shifted(attended.reshape(1, block_rows, group_features), "pipe", 1)
+    results_b = jnp.stack([shared_grad, value_grad]).reshape(2, block_rows, group_features)
+    results_b = jnp.where(last_plane, jnp.zeros_like(results_b), results_b)
     shared_grad_in, values_grad_in, forward_in = give_back(
-        jnp.concatenate([moved_b, moved_f]),
-        jnp.stack([back_b[1]] * 2 + [back_f[1]]),
-        jnp.stack([back_b[0]] * 2 + [back_f[0]]),
+        jnp.concatenate([results_b, moved_f]),
+        jnp.stack([next_b[1]] * 2 + [prev_f[1]]),
+        jnp.stack([next_b[0]] * 2 + [prev_f[0]]),
     )
     return (forward_in, shared_grad_in, values_grad_in)
 

time: 146 us -> 140 us (0.959)
  the two profiles are of different devices: /device:TPU:96 before, /device:TPU:232 now
where the time goes in v7:
time: 140 us; the launch traced here: 139 us
  waiting for transfers between devices  57.5 us (41%)
  starting transfers between devices  35.1 us (25%)
  matrix products  17 us (12%)
  other arithmetic  15.6 us (11%)
  local copies, waits for them, and re-layouts  12.5 us (9%)
    all_to_all x2, waiting for transfers between devices, exchange(): lax.all_to_all(stacked, axes, split_axis=0, concat_axis=0, tiled=True)  29 us
    all_to_all x1, waiting for transfers between devices, give_back(): lax.all_to_all(placed, axes, split_axis=0, concat_axis=0, tiled=True)  28.4 us
    ppermute x6, starting transfers between devices, shifted(): return lax.ppermute(block, axis, route)  17.3 us
    all_to_all x2, starting transfers between devices, exchange(): lax.all_to_all(stacked, axes, split_axis=0, concat_axis=0, tiled=True)  12.7 us
    all_to_all x1, starting transfers between devices, give_back(): lax.all_to_all(placed, axes, split_axis=0, concat_axis=0, tiled=True)  5.12 us
    sub x2, matrix products, softmax_weights(): exponent = jnp.exp(scores - largest)  4.33 us
    another operation x12, other arithmetic  3.74 us
    another operation x5, local copies, waits for them, and re-layouts, exchange(): array[0].reshape(tok_dev, mp_count, group_features)  3.41 us
  transfers between devices with their start and end apart: 9, of which 3 were waited for; matrix products, arithmetic and copies ran while one was open for 26% of the time, Pallas kernels for 0%

profile of v7, /device:TPU:232, one launch (start us, length us, event | category | flops | bytes accessed | tf_op | source)
XLA Modules:
  0.0 138.9 jit_solution(16826416933056055702)
XLA Ops:
  1.5 1.3 collective-permute-start.1
  2.8 4.5 %collective-permute-start = (s32[2048]{0:T(1024)S(1)}, s32[2048]{0:T(1024)S(1)}, u32[]{:S(2)}, u32[]{:S(2)}) collective-permute-start(s32[2048]{0:T(1024)S(1)} %bitcast.238), channel_id=1, source_target_pairs={{32,0},{64,32},{96,64},{128,96},{160,128},{192,160},{224,192},{33,... | collective-permute-start | bytes 24584 | tf_op jit(solution)/shard_map/ppermute | solution.py:18
  7.3 2.9 %collective-permute-start.2 = (bf16[1,64,3072]{2,1,0:T(8,128)(2,1)}, bf16[1,64,3072]{2,1,0:T(8,128)(2,1)S(1)}, u32[]{:S(2)}, u32[]{:S(2)}) collective-permute-start(bf16[1,64,3072]{2,1,0:T(8,128)(2,1)} %param.8), channel_id=1, source_target_pairs={{32,0},{64,32},{96,64},{128,96},{160,128},{192,160},{224,192},{33,... | collective-permute-start | bytes 1179656 | tf_op jit(solution)/shard_map/ppermute | solution.py:18
  10.3 2.9 %collective-permute-start.3 = (bf16[1,64,3072]{2,1,0:T(8,128)(2,1)}, bf16[1,64,3072]{2,1,0:T(8,128)(2,1)S(1)}, u32[]{:S(2)}, u32[]{:S(2)}) collective-permute-start(bf16[1,64,3072]{2,1,0:T(8,128)(2,1)} %param.9), channel_id=1, source_target_pairs={{32,0},{64,32},{96,64},{128,96},{160,128},{192,160},{224,192},{33,... | collective-permute-start | bytes 1179656 | tf_op jit(solution)/shard_map/ppermute | solution.py:18
  13.2 4.1 %collective-permute-start.4 = (bf16[1,64,3072]{2,1,0:T(8,128)(2,1)}, bf16[1,64,3072]{2,1,0:T(8,128)(2,1)S(1)}, u32[]{:S(2)}, u32[]{:S(2)}) collective-permute-start(bf16[1,64,3072]{2,1,0:T(8,128)(2,1)} %param.10), channel_id=1, source_target_pairs={{32,0},{64,32},{96,64},{128,96},{160,128},{192,160},{224,192},{33,... | collective-permute-start | bytes 1179656 | tf_op jit(solution)/shard_map/ppermute | solution.py:18
  18.8 1.3 reshape_squeeze.18
  20.1 1.3 reshape_squeeze.19
  22.2 1.3 pad_maximum_fusion.1
  23.5 7.5 %all-to-all-start.1 = ((bf16[32,2,16,768]{3,2,1,0:T(8,128)(2,1)}), bf16[32,2,16,768]{3,2,1,0:T(8,128)(2,1)S(1)}, u32[]{:S(2)}, u32[]{:S(2)}) async-start(bf16[32,2,16,768]{3,2,1,0:T(8,128)(2,1)} %pad_maximum_fusion.1), calls=%async_computation.1 | async-start | bytes 3145728 | tf_op jit(solution)/shard_map/all_to_all | solution.py:135
  43.3 1.7 %pad_maximum_fusion = bf16[32,3,16,768]{3,2,1,0:T(8,128)(2,1)} fusion(bf16[32,1,16,768]{3,2,1,0:T(8,128)(2,1)S(1)} %bitcast.213, bf16[32,1,16,768]{3,2,1,0:T(8,128)(2,1)S(1)} %bitcast.212, bf16[32,1,16,768]{3,2,1,0:T(8,128)(2,1)S(1)} %bitcast.211), kind=kLoop, calls=%fused_computation.2 | loop fusion | flops 2359296 | bytes 4718592 | tf_op jit(solution)/shard_map/stack | solution.py:132
  44.9 7.8 %all-to-all-done.1 = bf16[32,2,16,768]{3,2,1,0:T(8,128)(2,1)S(1)} async-done(((bf16[32,2,16,768]{3,2,1,0:T(8,128)(2,1)}), bf16[32,2,16,768]{3,2,1,0:T(8,128)(2,1)S(1)}, u32[]{:S(2)}, u32[]{:S(2)}) %all-to-all-start.1) | async-done | bytes 1572896 | tf_op jit(solution)/shard_map/all_to_all | solution.py:135
  52.8 1.2 copy-done
  53.9 5.1 %all-to-all-start = ((bf16[32,3,16,768]{3,2,1,0:T(8,128)(2,1)}), bf16[32,3,16,768]{3,2,1,0:T(8,128)(2,1)S(1)}, u32[]{:S(2)}, u32[]{:S(2)}) async-start(bf16[32,3,16,768]{3,2,1,0:T(8,128)(2,1)} %pad_maximum_fusion), calls=%async_computation | async-start | bytes 4718592 | tf_op jit(solution)/shard_map/all_to_all | solution.py:135
  60.0 2.0 %convolution_bitcast_fusion.2 = bf16[2,256,768]{1,2,0:T(8,128)(2,1)S(1)} fusion(bf16[32,2,16,768]{3,2,1,0:T(8,128)(2,1)} %copy-done, pred[256,16]{0,1:T(8,128)(4,1)S(1)} %copy-done.9, pred[256,32]{0,1:T(8,128)(4,1)S(1)} %copy-done.8), kind=kOutput, calls=%fused_computation.23 | convolution fusion | flops 402784256 | bytes 2371584 | tf_op jit(solution)/shard_map/irk,rakf->aif/dot_general | solution.py:139
  62.1 2.5 %fusion.126 = (f32[6,256]{1,0:T(8,128)}, f32[6,256,256]{1,2,0:T(8,128)}) fusion(bf16[256,6,128]{0,2,1:T(8,128)(2,1)S(1)} %bitcast.228, pred[256,256]{0,1:T(8,128)(4,1)S(1)} %fusion.48), kind=kOutput, calls=%fused_computation.217 | convolution fusion | flops 102236416 | bytes 2037760 | tf_op jit(solution)/shard_map/sub | solution.py:36
  64.6 1.7 %convolution_convert_fusion = bf16[6,128,256]{2,1,0:T(8,128)(2,1)S(1)} fusion(bf16[256,6,128]{0,2,1:T(8,128)(2,1)S(1)} %bitcast.227, f32[6,256,256]{1,2,0:T(8,128)} %get-tuple-element.23, f32[6,256]{1,0:T(8,128)} %get-tuple-element.22), kind=kOutput, calls=%fused_computation.28 | convolution fusion | flops 101646336 | bytes 2365440 | tf_op jit(solution)/shard_map/nhqk,nkhd->nqhd/dot_general | solution.py:42
  66.5 1.5 %collective-permute-start.5 = (bf16[1,256,768]{2,1,0:T(8,128)(2,1)S(1)}, bf16[1,256,768]{2,1,0:T(8,128)(2,1)S(1)}, u32[]{:S(2)}, u32[]{:S(2)}) collective-permute-start(bf16[1,256,768]{2,1,0:T(8,128)(2,1)S(1)} %copy.181), channel_id=1, source_target_pairs={{0,32},{32,64},{64,96},{96,128},{128,160},{160,192},{192,224},{1,3... | collective-permute-start | bytes 1179656 | tf_op jit(solution)/shard_map/ppermute | solution.py:18
  67.9 21.2 %all-to-all-done = bf16[32,3,16,768]{3,2,1,0:T(8,128)(2,1)S(1)} async-done(((bf16[32,3,16,768]{3,2,1,0:T(8,128)(2,1)}), bf16[32,3,16,768]{3,2,1,0:T(8,128)(2,1)S(1)}, u32[]{:S(2)}, u32[]{:S(2)}) %all-to-all-start) | async-done | bytes 2359328 | tf_op jit(solution)/shard_map/all_to_all | solution.py:135
  90.1 1.9 %fusion.127 = (f32[6,256]{1,0:T(8,128)S(1)}, f32[6,256,256]{1,2,0:T(8,128)}) fusion(pred[256,256]{0,1:T(8,128)(4,1)S(1)} %fusion.47, bf16[256,6,128]{0,2,1:T(8,128)(2,1)S(1)} %bitcast.208), kind=kOutput, calls=%fused_computation.218 | convolution fusion | flops 102236416 | bytes 2037760 | tf_op jit(solution)/shard_map/sub | solution.py:36
  91.9 1.8 %fusion.19 = f32[256,6]{0,1:T(8,128)S(1)} fusion(bf16[256,6,128]{0,2,1:T(8,128)(2,1)S(1)} %bitcast.220, bf16[1,256,6,128]{1,3,2,0:T(8,128)(2,1)S(1)} %bitcast.217, f32[6,256,256]{1,2,0:T(8,128)} %get-tuple-element.25, f32[6,256]{1,0:T(8,128)S(1)} %get-tuple-element.24), kind=kOutput, calls=%fused_computation.30 | convolution fusion | flops 102038016 | bytes 2371584 | tf_op jit(solution)/shard_map/nhqk,nkhd->nqhd/dot_general | solution.py:50
  95.1 1.8 %convolution_convert_fusion.1 = bf16[6,128,256]{2,1,0:T(8,128)(2,1)S(1)} fusion(bf16[256,6,128]{0,2,1:T(8,128)(2,1)S(1)} %bitcast.219, f32[6,256,256]{1,2,0:T(8,128)} %get-tuple-element.25, f32[6,256]{1,0:T(8,128)S(1)} %get-tuple-element.24), kind=kOutput, calls=%fused_computation.29 | convolution fusion | flops 101646336 | bytes 2365440 | tf_op jit(solution)/shard_map/nhqk,nqhd->nkhd/dot_general | solution.py:52
  98.0 2.7 %copy.183 = bf16[32,3,16,768]{3,2,1,0:T(8,128)(2,1)} copy(bf16[32,3,16,768]{3,0,2,1:T(8,128)(2,1)S(1)} %convolution_bitcast_fusion) | data formatting | bytes 4718592 | tf_op jit(solution)/shard_map/airk,aif->rakf/transpose | solution.py:143
  100.7 5.1 %all-to-all-start.2 = ((bf16[32,3,16,768]{3,2,1,0:T(8,128)(2,1)}), bf16[32,3,16,768]{3,2,1,0:T(8,128)(2,1)S(1)}, u32[]{:S(2)}, u32[]{:S(2)}) async-start(bf16[32,3,16,768]{3,2,1,0:T(8,128)(2,1)} %copy.183), calls=%async_computation.2 | async-start | bytes 4718592 | tf_op jit(solution)/shard_map/all_to_all | solution.py:144
  107.5 28.4 %all-to-all-done.2 = bf16[32,3,16,768]{3,2,1,0:T(8,128)(2,1)S(1)} async-done(((bf16[32,3,16,768]{3,2,1,0:T(8,128)(2,1)}), bf16[32,3,16,768]{3,2,1,0:T(8,128)(2,1)S(1)}, u32[]{:S(2)}, u32[]{:S(2)}) %all-to-all-start.2) | async-done | bytes 2359328 | tf_op jit(solution)/shard_map/all_to_all | solution.py:144
  (126 shorter events, 24.0 us)
Async XLA Ops:
  1.5 33.2 %collective-permute-start.1 = (s32[2048]{0:T(1024)S(1)}, s32[2048]{0:T(1024)S(1)}, u32[]{:S(2)}, u32[]{:S(2)}) collective-permute-start(s32[2048]{0:T(1024)S(1)} %bitcast.229), channel_id=1, source_target_pairs={{0,32},{32,64},{64,96},{96,128},{128,160},{160,192},{192,224},{1,3... | collective-permute-start | bytes 24584 | tf_op jit(solution)/shard_map/ppermute | solution.py:18
  2.8 31.9 %collective-permute-start = (s32[2048]{0:T(1024)S(1)}, s32[2048]{0:T(1024)S(1)}, u32[]{:S(2)}, u32[]{:S(2)}) collective-permute-start(s32[2048]{0:T(1024)S(1)} %bitcast.238), channel_id=1, source_target_pairs={{32,0},{64,32},{96,64},{128,96},{160,128},{192,160},{224,192},{33,... | collective-permute-start | bytes 24584 | tf_op jit(solution)/shard_map/ppermute | solution.py:18
  7.3 33.8 %collective-permute-start.2 = (bf16[1,64,3072]{2,1,0:T(8,128)(2,1)}, bf16[1,64,3072]{2,1,0:T(8,128)(2,1)S(1)}, u32[]{:S(2)}, u32[]{:S(2)}) collective-permute-start(bf16[1,64,3072]{2,1,0:T(8,128)(2,1)} %param.8), channel_id=1, source_target_pairs={{32,0},{64,32},{96,64},{128,96},{160,128},{192,160},{224,192},{33,... | collective-permute-start | bytes 1179656 | tf_op jit(solution)/shard_map/ppermute | solution.py:18
  10.3 31.2 %collective-permute-start.3 = (bf16[1,64,3072]{2,1,0:T(8,128)(2,1)}, bf16[1,64,3072]{2,1,0:T(8,128)(2,1)S(1)}, u32[]{:S(2)}, u32[]{:S(2)}) collective-permute-start(bf16[1,64,3072]{2,1,0:T(8,128)(2,1)} %param.9), channel_id=1, source_target_pairs={{32,0},{64,32},{96,64},{128,96},{160,128},{192,160},{224,192},{33,... | collective-permute-start | bytes 1179656 | tf_op jit(solution)/shard_map/ppermute | solution.py:18
  13.2 28.5 %collective-permute-start.4 = (bf16[1,64,3072]{2,1,0:T(8,128)(2,1)}, bf16[1,64,3072]{2,1,0:T(8,128)(2,1)S(1)}, u32[]{:S(2)}, u32[]{:S(2)}) collective-permute-start(bf16[1,64,3072]{2,1,0:T(8,128)(2,1)} %param.10), channel_id=1, source_target_pairs={{32,0},{64,32},{96,64},{128,96},{160,128},{192,160},{224,192},{33,... | collective-permute-start | bytes 1179656 | tf_op jit(solution)/shard_map/ppermute | solution.py:18
  23.5 29.2 %all-to-all-start.1 = ((bf16[32,2,16,768]{3,2,1,0:T(8,128)(2,1)}), bf16[32,2,16,768]{3,2,1,0:T(8,128)(2,1)S(1)}, u32[]{:S(2)}, u32[]{:S(2)}) async-start(bf16[32,2,16,768]{3,2,1,0:T(8,128)(2,1)} %pad_maximum_fusion.1), calls=%async_computation.1 | async-start | bytes 3145728 | tf_op jit(solution)/shard_map/all_to_all | solution.py:135
  37.9 21.9 %copy-start.4 = (pred[256,16]{0,1:T(8,128)(4,1)}, pred[256,16]{0,1:T(8,128)(4,1)S(1)}, u32[]{:S(2)}) copy-start(pred[256,16]{0,1:T(8,128)(4,1)S(1)} %iota_compare_fusion.16) | copy-start | bytes 12292
  44.9 15.0 %copy-start.1 = (pred[256,32]{0,1:T(8,128)(4,1)S(1)}, pred[256,32]{0,1:T(8,128)(4,1)}, u32[]{:S(2)}) copy-start(pred[256,32]{0,1:T(8,128)(4,1)} %iota_compare_fusion.9) | copy-start | bytes 24580
  44.9 15.0 %copy-start.6 = (pred[256,16]{0,1:T(8,128)(4,1)S(1)}, pred[256,16]{0,1:T(8,128)(4,1)}, u32[]{:S(2)}) copy-start(pred[256,16]{0,1:T(8,128)(4,1)} %iota_compare_fusion.14) | copy-start | bytes 12292
  44.9 15.1 %copy-start.8 = (pred[256,32]{0,1:T(8,128)(4,1)S(1)}, pred[256,32]{0,1:T(8,128)(4,1)}, u32[]{:S(2)}) copy-start(pred[256,32]{0,1:T(8,128)(4,1)} %iota_compare_fusion.11) | copy-start | bytes 24580
  44.9 15.1 %copy-start.9 = (pred[256,16]{0,1:T(8,128)(4,1)S(1)}, pred[256,16]{0,1:T(8,128)(4,1)}, u32[]{:S(2)}) copy-start(pred[256,16]{0,1:T(8,128)(4,1)} %iota_compare_fusion.15) | copy-start | bytes 12292
  52.8 1.2 copy-start
  53.9 35.2 %all-to-all-start = ((bf16[32,3,16,768]{3,2,1,0:T(8,128)(2,1)}), bf16[32,3,16,768]{3,2,1,0:T(8,128)(2,1)S(1)}, u32[]{:S(2)}, u32[]{:S(2)}) async-start(bf16[32,3,16,768]{3,2,1,0:T(8,128)(2,1)} %pad_maximum_fusion), calls=%async_computation | async-start | bytes 4718592 | tf_op jit(solution)/shard_map/all_to_all | solution.py:135
  64.6 24.5 %copy-start.5 = (pred[256,16]{0,1:T(8,128)(4,1)S(1)}, pred[256,16]{0,1:T(8,128)(4,1)}, u32[]{:S(2)}) copy-start(pred[256,16]{0,1:T(8,128)(4,1)} %copy-done.4) | copy-start | bytes 12292
  66.5 30.8 %collective-permute-start.5 = (bf16[1,256,768]{2,1,0:T(8,128)(2,1)S(1)}, bf16[1,256,768]{2,1,0:T(8,128)(2,1)S(1)}, u32[]{:S(2)}, u32[]{:S(2)}) collective-permute-start(bf16[1,256,768]{2,1,0:T(8,128)(2,1)S(1)} %copy.181), channel_id=1, source_target_pairs={{0,32},{32,64},{64,96},{96,128},{128,160},{160,192},{192,224},{1,3... | collective-permute-start | bytes 1179656 | tf_op jit(solution)/shard_map/ppermute | solution.py:18
  91.9 1.9 %copy-start.10 = (f32[6,256,256]{1,2,0:T(8,128)S(1)}, f32[6,256,256]{1,2,0:T(8,128)}, u32[]{:S(2)}) copy-start(f32[6,256,256]{1,2,0:T(8,128)} %get-tuple-element.25) | copy-start | bytes 4718596
  100.7 5.1 %copy-start.2 = (s32[2048]{0:T(1024)S(1)}, s32[2048]{0:T(1024)}, u32[]{:S(2)}) copy-start(s32[2048]{0:T(1024)} %get-tuple-element.3) | copy-start | bytes 24580
  100.7 6.0 %copy-start.7 = (pred[2048]{0:T(1024)(128)(4,1)S(1)}, pred[2048]{0:T(1024)(128)(4,1)}, u32[]{:S(2)}) copy-start(pred[2048]{0:T(1024)(128)(4,1)} %get-tuple-element.4) | copy-start | bytes 6148
  100.7 6.0 %copy-start.3 = (s32[2048]{0:T(1024)S(1)}, s32[2048]{0:T(1024)}, u32[]{:S(2)}) copy-start(s32[2048]{0:T(1024)} %get-tuple-element.29) | copy-start | bytes 24580
  100.7 35.2 %all-to-all-start.2 = ((bf16[32,3,16,768]{3,2,1,0:T(8,128)(2,1)}), bf16[32,3,16,768]{3,2,1,0:T(8,128)(2,1)S(1)}, u32[]{:S(2)}, u32[]{:S(2)}) async-start(bf16[32,3,16,768]{3,2,1,0:T(8,128)(2,1)} %copy.183), calls=%async_computation.2 | async-start | bytes 4718592 | tf_op jit(solution)/shard_map/all_to_all | solution.py:144

commit v8 on v7

--- a/solution.py
+++ b/solution.py
@@ -109,9 +109,7 @@
     pipe_index = lax.axis_index("pipe")
     last_plane = pipe_index == lax.axis_size("pipe") - 1
     order_fwd = cluster_order[0, 0]
-    order_next_bwd, shared_bwd, values_bwd, upstream_bwd = shifted(
-        (cluster_order[0, 1], shared_bwd, values_bwd, upstream_bwd), "pipe", -1
-    )
+    order_next_bwd = shifted(cluster_order[0, 1], "pipe", -1)
     order_prev_fwd = shifted(order_fwd, "pipe", 1)
 
     def plan(order):
@@ -119,7 +117,7 @@
 
     own_f, next_b, prev_f = plan(order_fwd), plan(order_next_bwd), plan(order_prev_fwd)
 
-    def exchange(arrays, send):
+    def pack(arrays, send):
         packed = [
             jnp.einsum(
                 "skt,tmf->smkf",
@@ -129,11 +127,12 @@
             )
             for array in arrays
         ]
-        stacked = jnp.stack(packed, axis=2).reshape(
+        return jnp.stack(packed, axis=2).reshape(
             group_count, len(arrays), slot_count, group_features
         )
-        arrived = lax.all_to_all(stacked, axes, split_axis=0, concat_axis=0, tiled=True)
-        return arrived
+
+    def exchange(packed):
+        return lax.all_to_all(packed, axes, split_axis=0, concat_axis=0, tiled=True)
 
     def gather_block(arrived, gather):
         rows = jnp.einsum("irk,rakf->aif", gather, arrived, preferred_element_type=jnp.bfloat16)
@@ -143,12 +142,23 @@
         placed = jnp.einsum("airk,aif->rakf", gather, results, preferred_element_type=jnp.bfloat16)
         arrived = lax.all_to_all(placed, axes, split_axis=0, concat_axis=0, tiled=True)
         arrived = arrived.reshape(seq_count, mp_count, results.shape[0], slot_count, group_features)
-        rows = jnp.einsum("askt,smakf->atmf", send, arrived, preferred_element_type=jnp.bfloat16)
-        return [row.reshape(1, tok_dev, features) for row in rows]
+        return [
+            jnp.einsum(
+                "skt,smkf->tmf", send[index], arrived[:, :, index],
+                preferred_element_type=jnp.bfloat16,
+            ).reshape(1, tok_dev, features)
+            for index in range(results.shape[0])
+        ]
 
-    arrived_f = exchange((shared_fwd, values_fwd), own_f[0])
+    packed_f = pack((shared_fwd, values_fwd), own_f[0])
+    packed_f, inputs_b = lax.optimization_barrier(
+        (packed_f, jnp.concatenate([shared_bwd, values_bwd, upstream_bwd]))
+    )
+    arrived_f = exchange(packed_f)
+    inputs_b = shifted(inputs_b, "pipe", -1)
+    shared_bwd, values_bwd, upstream_bwd = inputs_b[0:1], inputs_b[1:2], inputs_b[2:3]
     rows_f = gather_block(arrived_f, own_f[1])
-    arrived_b = exchange((shared_bwd, values_bwd, upstream_bwd), next_b[0])
+    arrived_b = exchange(pack((shared_bwd, values_bwd, upstream_bwd), next_b[0]))
     attended = forward_block(rows_f[0], rows_f[1], own_f[2].reshape(-1, CLUSTER), score_scale)
     moved_f = shifted(attended.reshape(1, block_rows, group_features), "pipe", 1)
     rows_b = gather_block(arrived_b, next_b[1])

time: 140 us -> 152 us (1.086)
  the two profiles are of different devices: /device:TPU:232 before, /device:TPU:96 now
where the time goes in v8:
time: 152 us; the launch traced here: 151 us
  waiting for transfers between devices  68.6 us (45%)
  starting transfers between devices  31.4 us (21%)
  matrix products  19.9 us (13%)
  local copies, waits for them, and re-layouts  16.3 us (11%)
  other arithmetic  13.6 us (9%)
    all_to_all x1, waiting for transfers between devices, give_back(): lax.all_to_all(placed, axes, split_axis=0, concat_axis=0, tiled=True)  28.8 us
    all_to_all x2, waiting for transfers between devices, exchange(): return lax.all_to_all(packed, axes, split_axis=0, concat_axis=0, tiled=True)  20.1 us
    ppermute x4, waiting for transfers between devices, shifted(): return lax.ppermute(block, axis, route)  19.8 us
    all_to_all x2, starting transfers between devices, exchange(): return lax.all_to_all(packed, axes, split_axis=0, concat_axis=0, tiled=True)  14.7 us
    ppermute x4, starting transfers between devices, shifted(): return lax.ppermute(block, axis, route)  11.8 us
    all_to_all x1, starting transfers between devices, give_back(): lax.all_to_all(placed, axes, split_axis=0, concat_axis=0, tiled=True)  4.96 us
    sub x2, matrix products, softmax_weights(): exponent = jnp.exp(scores - largest)  4.33 us
    another operation x12, other arithmetic  3.74 us
  transfers between devices with their start and end apart: 7, of which 3 were waited for; matrix products, arithmetic and copies ran while one was open for 24% of the time, Pallas kernels for 0%

profile of v8, /device:TPU:96, one launch (start us, length us, event | category | flops | bytes accessed | tf_op | source)
XLA Modules:
  0.0 151.0 jit_solution(17406283278663347764)
XLA Ops:
  1.5 2.0 %collective-permute-start.2 = (s32[2048]{0:T(1024)S(1)}, s32[2048]{0:T(1024)S(1)}, u32[]{:S(2)}, u32[]{:S(2)}) collective-permute-start(s32[2048]{0:T(1024)S(1)} %bitcast.252), channel_id=1, source_target_pairs={{32,0},{64,32},{96,64},{128,96},{160,128},{192,160},{224,192},{33,... | collective-permute-start | bytes 24584 | tf_op jit(solution)/shard_map/ppermute | solution.py:18
  3.5 5.0 %collective-permute-start = (s32[2048]{0:T(1024)S(1)}, s32[2048]{0:T(1024)S(1)}, u32[]{:S(2)}, u32[]{:S(2)}) collective-permute-start(s32[2048]{0:T(1024)S(1)} %bitcast.240), channel_id=1, source_target_pairs={{0,32},{32,64},{64,96},{96,128},{128,160},{160,192},{192,224},{1,3... | collective-permute-start | bytes 24584 | tf_op jit(solution)/shard_map/ppermute | solution.py:18
  8.5 1.3 reshape_squeeze.16
  11.3 1.3 reshape_squeeze.15
  13.4 1.3 pad_maximum_fusion.1
  15.2 7.4 %all-to-all-start.1 = ((bf16[32,2,16,768]{3,2,1,0:T(8,128)(2,1)}), bf16[32,2,16,768]{3,2,1,0:T(8,128)(2,1)}, u32[]{:S(2)}, u32[]{:S(2)}) async-start(bf16[32,2,16,768]{3,2,1,0:T(8,128)(2,1)} %pad_maximum_fusion.1), calls=%async_computation.1 | async-start | bytes 3145728 | tf_op jit(solution)/shard_map/all_to_all | solution.py:135
  22.6 1.9 %collective-permute-start.1 = (bf16[3,64,3072]{2,1,0:T(8,128)(2,1)S(1)}, bf16[3,64,3072]{2,1,0:T(8,128)(2,1)S(1)}, u32[]{:S(2)}, u32[]{:S(2)}) collective-permute-start(bf16[3,64,3072]{2,1,0:T(8,128)(2,1)S(1)} %pad_maximum_fusion.2), channel_id=1, source_target_pairs={{32,0},{64,32},{96,64},{128,96},{160,128},{192,160},{224,192},{33,... | collective-permute-start | bytes 3538952 | tf_op jit(solution)/shard_map/ppermute | solution.py:18
  34.0 19.8 %collective-permute-done.1 = bf16[3,64,3072]{2,1,0:T(8,128)(2,1)S(1)} collective-permute-done((bf16[3,64,3072]{2,1,0:T(8,128)(2,1)S(1)}, bf16[3,64,3072]{2,1,0:T(8,128)(2,1)S(1)}, u32[]{:S(2)}, u32[]{:S(2)}) %collective-permute-start.1) | collective-permute-done | bytes 1179680 | tf_op jit(solution)/shard_map/ppermute | solution.py:18
  56.5 1.6 %copy.128 = bf16[32,3,16,768]{3,2,1,0:T(8,128)(2,1)} copy(bf16[32,3,16,768]{3,2,0,1:T(8,128)(2,1)S(1)} %pad_maximum_fusion) | data formatting | bytes 4718592 | tf_op jit(solution)/shard_map/stack | solution.py:130
  58.1 7.2 %all-to-all-start = ((bf16[32,3,16,768]{3,2,1,0:T(8,128)(2,1)}), bf16[32,3,16,768]{3,2,1,0:T(8,128)(2,1)S(1)}, u32[]{:S(2)}, u32[]{:S(2)}) async-start(bf16[32,3,16,768]{3,2,1,0:T(8,128)(2,1)} %copy.128), calls=%async_computation | async-start | bytes 4718592 | tf_op jit(solution)/shard_map/all_to_all | solution.py:135
  66.2 2.0 %convolution_bitcast_fusion.5 = bf16[2,256,768]{1,2,0:T(8,128)(2,1)S(1)} fusion(bf16[32,2,16,768]{3,2,1,0:T(8,128)(2,1)} %all-to-all-done.1, pred[256,16]{0,1:T(8,128)(4,1)S(1)} %copy-done.11, pred[256,32]{0,1:T(8,128)(4,1)S(1)} %copy-done.10), kind=kOutput, calls=%fused_computation.23 | convolution fusion | flops 402784256 | bytes 2371584 | tf_op jit(solution)/shard_map/irk,rakf->aif/dot_general | solution.py:138
  68.4 2.5 %fusion.121 = (f32[6,256]{1,0:T(8,128)}, f32[6,256,256]{1,2,0:T(8,128)}) fusion(bf16[256,6,128]{0,2,1:T(8,128)(2,1)S(1)} %bitcast.237, pred[256,256]{0,1:T(8,128)(4,1)S(1)} %fusion.37), kind=kOutput, calls=%fused_computation.217 | convolution fusion | flops 102236416 | bytes 2037760 | tf_op jit(solution)/shard_map/sub | solution.py:36
  70.8 1.7 %convolution_convert_fusion = bf16[6,128,256]{2,1,0:T(8,128)(2,1)S(1)} fusion(bf16[256,6,128]{0,2,1:T(8,128)(2,1)S(1)} %bitcast.236, f32[6,256,256]{1,2,0:T(8,128)} %get-tuple-element.30, f32[6,256]{1,0:T(8,128)} %get-tuple-element.29), kind=kOutput, calls=%fused_computation.31 | convolution fusion | flops 101646336 | bytes 2365440 | tf_op jit(solution)/shard_map/nhqk,nkhd->nqhd/dot_general | solution.py:42
  72.7 2.8 %collective-permute-start.3 = (bf16[1,256,768]{2,1,0:T(8,128)(2,1)S(1)}, bf16[1,256,768]{2,1,0:T(8,128)(2,1)S(1)}, u32[]{:S(2)}, u32[]{:S(2)}) collective-permute-start(bf16[1,256,768]{2,1,0:T(8,128)(2,1)S(1)} %copy.145), channel_id=1, source_target_pairs={{0,32},{32,64},{64,96},{96,128},{128,160},{160,192},{192,224},{1,3... | collective-permute-start | bytes 1179656 | tf_op jit(solution)/shard_map/ppermute | solution.py:18
  75.5 20.1 %all-to-all-done = bf16[32,3,16,768]{3,2,1,0:T(8,128)(2,1)S(1)} async-done(((bf16[32,3,16,768]{3,2,1,0:T(8,128)(2,1)}), bf16[32,3,16,768]{3,2,1,0:T(8,128)(2,1)S(1)}, u32[]{:S(2)}, u32[]{:S(2)}) %all-to-all-start) | async-done | bytes 2359328 | tf_op jit(solution)/shard_map/all_to_all | solution.py:135
  96.5 1.9 %fusion.122 = (f32[6,256]{1,0:T(8,128)S(1)}, f32[6,256,256]{1,2,0:T(8,128)}) fusion(pred[256,256]{0,1:T(8,128)(4,1)S(1)} %fusion.36, bf16[256,6,128]{0,2,1:T(8,128)(2,1)S(1)} %bitcast.214), kind=kOutput, calls=%fused_computation.218 | convolution fusion | flops 102236416 | bytes 2037760 | tf_op jit(solution)/shard_map/sub | solution.py:36
  98.4 1.8 %convolution_convert_fusion.1 = bf16[6,128,256]{2,1,0:T(8,128)(2,1)S(1)} fusion(bf16[256,6,128]{0,2,1:T(8,128)(2,1)S(1)} %bitcast.231, f32[6,256,256]{1,2,0:T(8,128)} %get-tuple-element.32, f32[6,256]{1,0:T(8,128)S(1)} %get-tuple-element.31), kind=kOutput, calls=%fused_computation.32 | convolution fusion | flops 101646336 | bytes 2365440 | tf_op jit(solution)/shard_map/nhqk,nqhd->nkhd/dot_general | solution.py:52
  100.4 1.8 %fusion.14 = f32[256,6]{0,1:T(8,128)S(1)} fusion(bf16[256,6,128]{0,2,1:T(8,128)(2,1)S(1)} %bitcast.229, bf16[1,256,6,128]{1,3,2,0:T(8,128)(2,1)S(1)} %bitcast.232, f32[6,256,256]{1,2,0:T(8,128)} %get-tuple-element.32, f32[6,256]{1,0:T(8,128)S(1)} %get-tuple-element.31), kind=kOutput, calls=%fused_computation.33 | convolution fusion | flops 102038016 | bytes 2371584 | tf_op jit(solution)/shard_map/nhqk,nkhd->nqhd/dot_general | solution.py:50
  104.4 2.7 %copy.147 = bf16[32,3,16,768]{3,2,1,0:T(8,128)(2,1)} copy(bf16[32,3,16,768]{3,0,2,1:T(8,128)(2,1)S(1)} %convolution_bitcast_fusion.3) | data formatting | bytes 4718592 | tf_op jit(solution)/shard_map/airk,aif->rakf/transpose | solution.py:142
  107.2 5.0 %all-to-all-start.2 = ((bf16[32,3,16,768]{3,2,1,0:T(8,128)(2,1)}), bf16[32,3,16,768]{3,2,1,0:T(8,128)(2,1)S(1)}, u32[]{:S(2)}, u32[]{:S(2)}) async-start(bf16[32,3,16,768]{3,2,1,0:T(8,128)(2,1)} %copy.147), calls=%async_computation.2 | async-start | bytes 4718592 | tf_op jit(solution)/shard_map/all_to_all | solution.py:143
  113.6 28.8 %all-to-all-done.2 = bf16[32,3,16,768]{3,2,1,0:T(8,128)(2,1)S(1)} async-done(((bf16[32,3,16,768]{3,2,1,0:T(8,128)(2,1)}), bf16[32,3,16,768]{3,2,1,0:T(8,128)(2,1)S(1)}, u32[]{:S(2)}, u32[]{:S(2)}) %all-to-all-start.2) | async-done | bytes 2359328 | tf_op jit(solution)/shard_map/all_to_all | solution.py:143
  145.0 1.4 dot_general.99
  147.6 1.1 convolution_bitcast_fusion.1
  148.7 1.1 convolution_bitcast_fusion
  (135 shorter events, 26.2 us)
Async XLA Ops:
  1.5 26.7 %collective-permute-start.2 = (s32[2048]{0:T(1024)S(1)}, s32[2048]{0:T(1024)S(1)}, u32[]{:S(2)}, u32[]{:S(2)}) collective-permute-start(s32[2048]{0:T(1024)S(1)} %bitcast.252), channel_id=1, source_target_pairs={{32,0},{64,32},{96,64},{128,96},{160,128},{192,160},{224,192},{33,... | collective-permute-start | bytes 24584 | tf_op jit(solution)/shard_map/ppermute | solution.py:18
  3.5 24.6 %collective-permute-start = (s32[2048]{0:T(1024)S(1)}, s32[2048]{0:T(1024)S(1)}, u32[]{:S(2)}, u32[]{:S(2)}) collective-permute-start(s32[2048]{0:T(1024)S(1)} %bitcast.240), channel_id=1, source_target_pairs={{0,32},{32,64},{64,96},{96,128},{128,160},{160,192},{192,224},{1,3... | collective-permute-start | bytes 24584 | tf_op jit(solution)/shard_map/ppermute | solution.py:18
  13.4 1.4 copy-start.2
  13.4 1.3 copy-start.3
  13.4 1.6 %copy-start.4 = (bf16[1,64,3072]{2,1,0:T(8,128)(2,1)S(1)}, bf16[1,64,3072]{2,1,0:T(8,128)(2,1)}, u32[]{:S(2)}) copy-start(bf16[1,64,3072]{2,1,0:T(8,128)(2,1)} %param.8) | copy-start | bytes 1179652
  15.2 42.9 %all-to-all-start.1 = ((bf16[32,2,16,768]{3,2,1,0:T(8,128)(2,1)}), bf16[32,2,16,768]{3,2,1,0:T(8,128)(2,1)}, u32[]{:S(2)}, u32[]{:S(2)}) async-start(bf16[32,2,16,768]{3,2,1,0:T(8,128)(2,1)} %pad_maximum_fusion.1), calls=%async_computation.1 | async-start | bytes 3145728 | tf_op jit(solution)/shard_map/all_to_all | solution.py:135
  22.6 31.2 %collective-permute-start.1 = (bf16[3,64,3072]{2,1,0:T(8,128)(2,1)S(1)}, bf16[3,64,3072]{2,1,0:T(8,128)(2,1)S(1)}, u32[]{:S(2)}, u32[]{:S(2)}) collective-permute-start(bf16[3,64,3072]{2,1,0:T(8,128)(2,1)S(1)} %pad_maximum_fusion.2), channel_id=1, source_target_pairs={{32,0},{64,32},{96,64},{128,96},{160,128},{192,160},{224,192},{33,... | collective-permute-start | bytes 3538952 | tf_op jit(solution)/shard_map/ppermute | solution.py:18
  58.0 8.1 %copy-start.7 = (pred[256,16]{0,1:T(8,128)(4,1)S(1)}, pred[256,16]{0,1:T(8,128)(4,1)}, u32[]{:S(2)}) copy-start(pred[256,16]{0,1:T(8,128)(4,1)} %iota_compare_fusion.16) | copy-start | bytes 12292
  58.1 8.2 %copy-start.10 = (pred[256,32]{0,1:T(8,128)(4,1)S(1)}, pred[256,32]{0,1:T(8,128)(4,1)}, u32[]{:S(2)}) copy-start(pred[256,32]{0,1:T(8,128)(4,1)} %iota_compare_fusion.11) | copy-start | bytes 24580
  58.1 8.2 %copy-start.11 = (pred[256,16]{0,1:T(8,128)(4,1)S(1)}, pred[256,16]{0,1:T(8,128)(4,1)}, u32[]{:S(2)}) copy-start(pred[256,16]{0,1:T(8,128)(4,1)} %iota_compare_fusion.15) | copy-start | bytes 12292
  58.1 37.5 %all-to-all-start = ((bf16[32,3,16,768]{3,2,1,0:T(8,128)(2,1)}), bf16[32,3,16,768]{3,2,1,0:T(8,128)(2,1)S(1)}, u32[]{:S(2)}, u32[]{:S(2)}) async-start(bf16[32,3,16,768]{3,2,1,0:T(8,128)(2,1)} %copy.128), calls=%async_computation | async-start | bytes 4718592 | tf_op jit(solution)/shard_map/all_to_all | solution.py:135
  70.8 24.7 %copy-start.8 = (pred[256,16]{0,1:T(8,128)(4,1)S(1)}, pred[256,16]{0,1:T(8,128)(4,1)}, u32[]{:S(2)}) copy-start(pred[256,16]{0,1:T(8,128)(4,1)} %iota_compare_fusion.16) | copy-start | bytes 12292
  72.7 30.9 %collective-permute-start.3 = (bf16[1,256,768]{2,1,0:T(8,128)(2,1)S(1)}, bf16[1,256,768]{2,1,0:T(8,128)(2,1)S(1)}, u32[]{:S(2)}, u32[]{:S(2)}) collective-permute-start(bf16[1,256,768]{2,1,0:T(8,128)(2,1)S(1)} %copy.145), channel_id=1, source_target_pairs={{0,32},{32,64},{64,96},{96,128},{128,160},{160,192},{192,224},{1,3... | collective-permute-start | bytes 1179656 | tf_op jit(solution)/shard_map/ppermute | solution.py:18
  100.3 1.9 %copy-start.12 = (f32[6,256,256]{1,2,0:T(8,128)S(1)}, f32[6,256,256]{1,2,0:T(8,128)}, u32[]{:S(2)}) copy-start(f32[6,256,256]{1,2,0:T(8,128)} %get-tuple-element.32) | copy-start | bytes 4718596
  107.2 5.0 %copy-start.5 = (s32[2048]{0:T(1024)S(1)}, s32[2048]{0:T(1024)}, u32[]{:S(2)}) copy-start(s32[2048]{0:T(1024)} %get-tuple-element.37) | copy-start | bytes 24580
  107.2 5.0 %copy-start.6 = (s32[2048]{0:T(1024)S(1)}, s32[2048]{0:T(1024)}, u32[]{:S(2)}) copy-start(s32[2048]{0:T(1024)} %get-tuple-element.7) | copy-start | bytes 24580
  107.2 5.9 %copy-start.9 = (pred[2048]{0:T(1024)(128)(4,1)S(1)}, pred[2048]{0:T(1024)(128)(4,1)}, u32[]{:S(2)}) copy-start(pred[2048]{0:T(1024)(128)(4,1)} %get-tuple-element.8) | copy-start | bytes 6148
  107.2 35.2 %all-to-all-start.2 = ((bf16[32,3,16,768]{3,2,1,0:T(8,128)(2,1)}), bf16[32,3,16,768]{3,2,1,0:T(8,128)(2,1)S(1)}, u32[]{:S(2)}, u32[]{:S(2)}) async-start(bf16[32,3,16,768]{3,2,1,0:T(8,128)(2,1)} %copy.147), calls=%async_computation.2 | async-start | bytes 4718592 | tf_op jit(solution)/shard_map/all_to_all | solution.py:143
  143.5 1.1 copy-start
  146.5 1.1 copy-start.1

commit v9 on v7

--- a/solution.py
+++ b/solution.py
@@ -109,9 +109,9 @@
     pipe_index = lax.axis_index("pipe")
     last_plane = pipe_index == lax.axis_size("pipe") - 1
     order_fwd = cluster_order[0, 0]
-    order_next_bwd, shared_bwd, values_bwd, upstream_bwd = shifted(
-        (cluster_order[0, 1], shared_bwd, values_bwd, upstream_bwd), "pipe", -1
-    )
+    order_next_bwd = shifted(cluster_order[0, 1], "pipe", -1)
+    inputs_b = shifted(jnp.concatenate([shared_bwd, values_bwd, upstream_bwd]), "pipe", -1)
+    shared_bwd, values_bwd, upstream_bwd = inputs_b[0:1], inputs_b[1:2], inputs_b[2:3]
     order_prev_fwd = shifted(order_fwd, "pipe", 1)
 
     def plan(order):
@@ -121,15 +121,13 @@
 
     def exchange(arrays, send):
         packed = [
-            jnp.einsum(
-                "skt,tmf->smkf",
-                send,
-                array[0].reshape(tok_dev, mp_count, group_features),
-                preferred_element_type=jnp.bfloat16,
-            )
+            jnp.einsum("skt,tf->skf", send, array[0], preferred_element_type=jnp.bfloat16)
             for array in arrays
         ]
-        stacked = jnp.stack(packed, axis=2).reshape(
+        stacked = jnp.stack(packed, axis=1).reshape(
+            seq_count, len(arrays), slot_count, mp_count, group_features
+        )
+        stacked = jnp.transpose(stacked, (0, 3, 1, 2, 4)).reshape(
             group_count, len(arrays), slot_count, group_features
         )
         arrived = lax.all_to_all(stacked, axes, split_axis=0, concat_axis=0, tiled=True)

time: 140 us -> 140 us (level)
  the two profiles are of different devices: /device:TPU:232 before, /device:TPU:96 now
where the time goes in v9:
time: 140 us; the launch traced here: 139 us
  waiting for transfers between devices  54.1 us (39%)
  starting transfers between devices  32.4 us (23%)
  matrix products  22.5 us (16%)
  other arithmetic  15 us (11%)
  local copies, waits for them, and re-layouts  13.7 us (10%)
    all_to_all x1, waiting for transfers between devices, give_back(): lax.all_to_all(placed, axes, split_axis=0, concat_axis=0, tiled=True)  28.6 us
    all_to_all x2, waiting for transfers between devices, exchange(): lax.all_to_all(stacked, axes, split_axis=0, concat_axis=0, tiled=True)  16.3 us
    all_to_all x2, starting transfers between devices, exchange(): lax.all_to_all(stacked, axes, split_axis=0, concat_axis=0, tiled=True)  14.6 us
    ppermute x4, starting transfers between devices, shifted(): return lax.ppermute(block, axis, route)  12.8 us
    ppermute x4, waiting for transfers between devices, shifted(): return lax.ppermute(block, axis, route)  9.18 us
    sub x2, matrix products, softmax_weights(): exponent = jnp.exp(scores - largest)  5.17 us
    dot_general x5, matrix products, exchange(): jnp.einsum('skt,tf->skf', send, array[0], preferred_element_type=jnp.bflo...  5.06 us
    all_to_all x1, starting transfers between devices, give_back(): lax.all_to_all(placed, axes, split_axis=0, concat_axis=0, tiled=True)  4.96 us
  transfers between devices with their start and end apart: 7, of which 3 were waited for; matrix products, arithmetic and copies ran while one was open for 29% of the time, Pallas kernels for 0%

profile of v9, /device:TPU:96, one launch (start us, length us, event | category | flops | bytes accessed | tf_op | source)
XLA Modules:
  0.0 138.9 jit_solution(2654973469657116715)
XLA Ops:
  1.5 5.0 %collective-permute-start.1 = (s32[2048]{0:T(1024)S(1)}, s32[2048]{0:T(1024)S(1)}, u32[]{:S(2)}, u32[]{:S(2)}) collective-permute-start(s32[2048]{0:T(1024)S(1)} %bitcast.203), channel_id=1, source_target_pairs={{0,32},{32,64},{64,96},{96,128},{128,160},{160,192},{192,224},{1,3... | collective-permute-start | bytes 24584 | tf_op jit(solution)/shard_map/ppermute | solution.py:18
  6.5 2.1 %collective-permute-start = (s32[2048]{0:T(1024)S(1)}, s32[2048]{0:T(1024)S(1)}, u32[]{:S(2)}, u32[]{:S(2)}) collective-permute-start(s32[2048]{0:T(1024)S(1)} %bitcast.212), channel_id=1, source_target_pairs={{32,0},{64,32},{96,64},{128,96},{160,128},{192,160},{224,192},{33,... | collective-permute-start | bytes 24584 | tf_op jit(solution)/shard_map/ppermute | solution.py:18
  8.6 1.4 pad_maximum_fusion.3
  10.0 1.9 %collective-permute-start.2 = (bf16[3,64,3072]{2,1,0:T(8,128)(2,1)S(1)}, bf16[3,64,3072]{2,1,0:T(8,128)(2,1)}, u32[]{:S(2)}, u32[]{:S(2)}) collective-permute-start(bf16[3,64,3072]{2,1,0:T(8,128)(2,1)S(1)} %pad_maximum_fusion.3), channel_id=1, source_target_pairs={{32,0},{64,32},{96,64},{128,96},{160,128},{192,160},{224,192},{33,... | collective-permute-start | bytes 3538952 | tf_op jit(solution)/shard_map/ppermute | solution.py:18
  15.8 7.3 %all-to-all-start.1 = ((bf16[32,2,16,768]{3,2,1,0:T(8,128)(2,1)}), bf16[32,2,16,768]{3,2,1,0:T(8,128)(2,1)S(1)}, u32[]{:S(2)}, u32[]{:S(2)}) async-start(bf16[32,2,16,768]{3,2,1,0:T(8,128)(2,1)} %bitcast.48), calls=%async_computation.1 | async-start | bytes 3145728 | tf_op jit(solution)/shard_map/all_to_all | solution.py:133
  31.4 9.2 %collective-permute-done.2 = bf16[3,64,3072]{2,1,0:T(8,128)(2,1)} collective-permute-done((bf16[3,64,3072]{2,1,0:T(8,128)(2,1)S(1)}, bf16[3,64,3072]{2,1,0:T(8,128)(2,1)}, u32[]{:S(2)}, u32[]{:S(2)}) %collective-permute-start.2) | collective-permute-done | bytes 1179680 | tf_op jit(solution)/shard_map/ppermute | solution.py:18
  40.6 1.4 %convolution_bitcast_fusion.2 = bf16[8,1,16,3072]{3,2,0,1:T(8,128)(2,1)S(1)} fusion(bf16[3,64,3072]{2,1,0:T(8,128)(2,1)} %collective-permute-done.2, s32[8,16]{1,0:T(8,128)S(1)} %select_reduce_fusion.2, pred[8,16]{1,0:T(8,128)(4,1)S(1)} %fusion.49), kind=kOutput, calls=%fused_computation.4 | convolution fusion | flops 50348032 | bytes 1180288 | tf_op jit(solution)/shard_map/skt,tf->skf/dot_general | solution.py:124
  42.0 1.4 %convolution_bitcast_fusion.3 = bf16[8,1,16,3072]{3,2,0,1:T(8,128)(2,1)S(1)} fusion(bf16[3,64,3072]{2,1,0:T(8,128)(2,1)} %collective-permute-done.2, s32[8,16]{1,0:T(8,128)S(1)} %select_reduce_fusion.2, pred[8,16]{1,0:T(8,128)(4,1)S(1)} %fusion.49), kind=kOutput, calls=%fused_computation.5 | convolution fusion | flops 50348032 | bytes 1180288 | tf_op jit(solution)/shard_map/skt,tf->skf/dot_general | solution.py:124
  43.4 1.4 %convolution_bitcast_fusion.4 = bf16[8,1,16,3072]{3,2,0,1:T(8,128)(2,1)S(1)} fusion(bf16[3,64,3072]{2,1,0:T(8,128)(2,1)} %collective-permute-done.2, s32[8,16]{1,0:T(8,128)S(1)} %select_reduce_fusion.2, pred[8,16]{1,0:T(8,128)(4,1)S(1)} %fusion.49), kind=kOutput, calls=%fused_computation.6 | convolution fusion | flops 50348032 | bytes 1180288 | tf_op jit(solution)/shard_map/skt,tf->skf/dot_general | solution.py:124
  45.7 1.6 %copy.122 = bf16[8,12,16,768]{3,2,1,0:T(8,128)(2,1)} copy(bf16[8,12,16,768]{3,2,0,1:T(8,128)(2,1)S(1)} %pad_maximum_fusion.1) | data formatting | bytes 4718592 | tf_op jit(solution)/shard_map/concatenate
  48.4 7.3 %all-to-all-start = ((bf16[32,3,16,768]{3,2,1,0:T(8,128)(2,1)}), bf16[32,3,16,768]{3,2,1,0:T(8,128)(2,1)S(1)}, u32[]{:S(2)}, u32[]{:S(2)}) async-start(bf16[32,3,16,768]{3,2,1,0:T(8,128)(2,1)} %bitcast.17), calls=%async_computation | async-start | bytes 4718592 | tf_op jit(solution)/shard_map/all_to_all | solution.py:133
  58.6 2.0 %convolution_bitcast_fusion.7 = bf16[2,256,768]{1,2,0:T(8,128)(2,1)S(1)} fusion(bf16[32,2,16,768]{3,2,1,0:T(8,128)(2,1)} %copy-done.1, pred[256,16]{0,1:T(8,128)(4,1)S(1)} %iota_compare_fusion.15, pred[256,32]{0,1:T(8,128)(4,1)S(1)} %iota_compare_fusion.11), kind=kOutput, calls=%fused_computation.36 | convolution fusion | flops 402784256 | bytes 2371584 | tf_op jit(solution)/shard_map/irk,rakf->aif/dot_general | solution.py:137
  60.7 3.3 %fusion.116 = (f32[6,256]{1,0:T(8,128)}, f32[6,256,256]{1,2,0:T(8,128)}) fusion(bf16[256,6,128]{0,2,1:T(8,128)(2,1)S(1)} %bitcast.202, pred[256,256]{0,1:T(8,128)(4,1)} %fusion.39), kind=kOutput, calls=%fused_computation.223 | convolution fusion | flops 102236416 | bytes 2037760 | tf_op jit(solution)/shard_map/sub | solution.py:36
  64.0 1.7 %convolution_convert_fusion = bf16[6,128,256]{2,1,0:T(8,128)(2,1)S(1)} fusion(bf16[256,6,128]{0,2,1:T(8,128)(2,1)S(1)} %bitcast.201, f32[6,256,256]{1,2,0:T(8,128)} %get-tuple-element.30, f32[6,256]{1,0:T(8,128)} %get-tuple-element.29), kind=kOutput, calls=%fused_computation.41 | convolution fusion | flops 101646336 | bytes 2365440 | tf_op jit(solution)/shard_map/nhqk,nkhd->nqhd/dot_general | solution.py:42
  65.9 3.8 %collective-permute-start.3 = (bf16[1,256,768]{2,1,0:T(8,128)(2,1)S(1)}, bf16[1,256,768]{2,1,0:T(8,128)(2,1)}, u32[]{:S(2)}, u32[]{:S(2)}) collective-permute-start(bf16[1,256,768]{2,1,0:T(8,128)(2,1)S(1)} %copy.144), channel_id=1, source_target_pairs={{0,32},{32,64},{64,96},{96,128},{128,160},{160,192},{192,224},{1,3... | collective-permute-start | bytes 1179656 | tf_op jit(solution)/shard_map/ppermute | solution.py:18
  69.7 16.3 %all-to-all-done = bf16[32,3,16,768]{3,2,1,0:T(8,128)(2,1)S(1)} async-done(((bf16[32,3,16,768]{3,2,1,0:T(8,128)(2,1)}), bf16[32,3,16,768]{3,2,1,0:T(8,128)(2,1)S(1)}, u32[]{:S(2)}, u32[]{:S(2)}) %all-to-all-start) | async-done | bytes 2359328 | tf_op jit(solution)/shard_map/all_to_all | solution.py:133
  86.0 1.5 %convolution_bitcast_fusion.6 = bf16[3,256,768]{1,2,0:T(8,128)(2,1)S(1)} fusion(bf16[32,3,16,768]{3,2,1,0:T(8,128)(2,1)S(1)} %all-to-all-done, pred[256,16]{0,1:T(8,128)(4,1)} %copy-done.8, pred[256,32]{0,1:T(8,128)(4,1)S(1)} %iota_compare_fusion.13), kind=kOutput, calls=%fused_computation.34 | convolution fusion | flops 604110848 | bytes 3551232 | tf_op jit(solution)/shard_map/irk,rakf->aif/dot_general | solution.py:137
  88.4 1.9 %fusion.117 = (f32[6,256]{1,0:T(8,128)S(1)}, f32[6,256,256]{1,2,0:T(8,128)}) fusion(pred[256,256]{0,1:T(8,128)(4,1)S(1)} %copy-done.5, bf16[256,6,128]{0,2,1:T(8,128)(2,1)S(1)} %bitcast.187), kind=kOutput, calls=%fused_computation.224 | convolution fusion | flops 102236416 | bytes 2037760 | tf_op jit(solution)/shard_map/sub | solution.py:36
  90.2 1.8 %fusion.20 = f32[256,6]{0,1:T(8,128)S(1)} fusion(bf16[256,6,128]{0,2,1:T(8,128)(2,1)S(1)} %bitcast.194, bf16[1,256,6,128]{1,3,2,0:T(8,128)(2,1)S(1)} %bitcast.191, f32[6,256,256]{1,2,0:T(8,128)} %get-tuple-element.32, f32[6,256]{1,0:T(8,128)S(1)} %get-tuple-element.31), kind=kOutput, calls=%fused_computation.43 | convolution fusion | flops 102038016 | bytes 2371584 | tf_op jit(solution)/shard_map/nhqk,nkhd->nqhd/dot_general | solution.py:50
  93.4 1.8 %convolution_convert_fusion.1 = bf16[6,128,256]{2,1,0:T(8,128)(2,1)S(1)} fusion(bf16[256,6,128]{0,2,1:T(8,128)(2,1)S(1)} %bitcast.193, f32[6,256,256]{1,2,0:T(8,128)} %get-tuple-element.32, f32[6,256]{1,0:T(8,128)S(1)} %get-tuple-element.31), kind=kOutput, calls=%fused_computation.42 | convolution fusion | flops 101646336 | bytes 2365440 | tf_op jit(solution)/shard_map/nhqk,nqhd->nkhd/dot_general | solution.py:52
  96.2 1.8 %convolution_bitcast_fusion.5 = bf16[32,3,16,768]{3,0,2,1:T(8,128)(2,1)S(1)} fusion(pred[1,256,32,16]{1,2,3,0:T(32,128)(4,1)S(1)} %copy-done.4, pred[1,256,32,16]{1,2,3,0:T(32,128)(4,1)S(1)} %copy-done.3, bf16[1,256,768]{2,1,0:T(8,128)(2,1)} %collective-permute-done.3, bf16[2,256,768]{2,1,0:T(8,128)(2,1)S(1)} %maximum_select_fusion), kind=kOutput, calls=%fused_computation.19 | convolution fusion | flops 607125504 | bytes 3801088 | tf_op jit(solution)/shard_map/airk,aif->rakf/dot_general | solution.py:141
  98.0 2.7 %copy.146 = bf16[32,3,16,768]{3,2,1,0:T(8,128)(2,1)} copy(bf16[32,3,16,768]{3,0,2,1:T(8,128)(2,1)S(1)} %convolution_bitcast_fusion.5) | data formatting | bytes 4718592 | tf_op jit(solution)/shard_map/airk,aif->rakf/transpose | solution.py:141
  100.7 5.0 %all-to-all-start.2 = ((bf16[32,3,16,768]{3,2,1,0:T(8,128)(2,1)}), bf16[32,3,16,768]{3,2,1,0:T(8,128)(2,1)S(1)}, u32[]{:S(2)}, u32[]{:S(2)}) async-start(bf16[32,3,16,768]{3,2,1,0:T(8,128)(2,1)} %copy.146), calls=%async_computation.2 | async-start | bytes 4718592 | tf_op jit(solution)/shard_map/all_to_all | solution.py:142
  107.3 28.6 %all-to-all-done.2 = bf16[32,3,16,768]{3,2,1,0:T(8,128)(2,1)S(1)} async-done(((bf16[32,3,16,768]{3,2,1,0:T(8,128)(2,1)}), bf16[32,3,16,768]{3,2,1,0:T(8,128)(2,1)S(1)}, u32[]{:S(2)}, u32[]{:S(2)}) %all-to-all-start.2) | async-done | bytes 2359328 | tf_op jit(solution)/shard_map/all_to_all | solution.py:142
  (123 shorter events, 25.4 us)
Async XLA Ops:
  0.6 12.7 %copy-start = (bf16[1,64,3072]{2,1,0:T(8,128)(2,1)S(1)}, bf16[1,64,3072]{2,1,0:T(8,128)(2,1)}, u32[]{:S(2)}) copy-start(bf16[1,64,3072]{2,1,0:T(8,128)(2,1)} %param.7) | copy-start | bytes 1179652
  1.5 24.6 %collective-permute-start.1 = (s32[2048]{0:T(1024)S(1)}, s32[2048]{0:T(1024)S(1)}, u32[]{:S(2)}, u32[]{:S(2)}) collective-permute-start(s32[2048]{0:T(1024)S(1)} %bitcast.203), channel_id=1, source_target_pairs={{0,32},{32,64},{64,96},{96,128},{128,160},{160,192},{192,224},{1,3... | collective-permute-start | bytes 24584 | tf_op jit(solution)/shard_map/ppermute | solution.py:18
  6.5 7.2 %copy-start.2 = (bf16[1,64,3072]{2,1,0:T(8,128)(2,1)S(1)}, bf16[1,64,3072]{2,1,0:T(8,128)(2,1)}, u32[]{:S(2)}) copy-start(bf16[1,64,3072]{2,1,0:T(8,128)(2,1)} %param.6) | copy-start | bytes 1179652
  6.5 19.6 %collective-permute-start = (s32[2048]{0:T(1024)S(1)}, s32[2048]{0:T(1024)S(1)}, u32[]{:S(2)}, u32[]{:S(2)}) collective-permute-start(s32[2048]{0:T(1024)S(1)} %bitcast.212), channel_id=1, source_target_pairs={{32,0},{64,32},{96,64},{128,96},{160,128},{192,160},{224,192},{33,... | collective-permute-start | bytes 24584 | tf_op jit(solution)/shard_map/ppermute | solution.py:18
  10.0 30.6 %collective-permute-start.2 = (bf16[3,64,3072]{2,1,0:T(8,128)(2,1)S(1)}, bf16[3,64,3072]{2,1,0:T(8,128)(2,1)}, u32[]{:S(2)}, u32[]{:S(2)}) collective-permute-start(bf16[3,64,3072]{2,1,0:T(8,128)(2,1)S(1)} %pad_maximum_fusion.3), channel_id=1, source_target_pairs={{32,0},{64,32},{96,64},{128,96},{160,128},{192,160},{224,192},{33,... | collective-permute-start | bytes 3538952 | tf_op jit(solution)/shard_map/ppermute | solution.py:18
  15.8 31.5 %all-to-all-start.1 = ((bf16[32,2,16,768]{3,2,1,0:T(8,128)(2,1)}), bf16[32,2,16,768]{3,2,1,0:T(8,128)(2,1)S(1)}, u32[]{:S(2)}, u32[]{:S(2)}) async-start(bf16[32,2,16,768]{3,2,1,0:T(8,128)(2,1)} %bitcast.48), calls=%async_computation.1 | async-start | bytes 3145728 | tf_op jit(solution)/shard_map/all_to_all | solution.py:133
  31.4 25.8 %copy-start.8 = (pred[256,16]{0,1:T(8,128)(4,1)}, pred[256,16]{0,1:T(8,128)(4,1)S(1)}, u32[]{:S(2)}) copy-start(pred[256,16]{0,1:T(8,128)(4,1)S(1)} %iota_compare_fusion.16) | copy-start | bytes 12292
  47.3 1.2 copy-start.1
  48.4 37.6 %all-to-all-start = ((bf16[32,3,16,768]{3,2,1,0:T(8,128)(2,1)}), bf16[32,3,16,768]{3,2,1,0:T(8,128)(2,1)S(1)}, u32[]{:S(2)}, u32[]{:S(2)}) async-start(bf16[32,3,16,768]{3,2,1,0:T(8,128)(2,1)} %bitcast.17), calls=%async_computation | async-start | bytes 4718592 | tf_op jit(solution)/shard_map/all_to_all | solution.py:133
  65.9 29.7 %collective-permute-start.3 = (bf16[1,256,768]{2,1,0:T(8,128)(2,1)S(1)}, bf16[1,256,768]{2,1,0:T(8,128)(2,1)}, u32[]{:S(2)}, u32[]{:S(2)}) collective-permute-start(bf16[1,256,768]{2,1,0:T(8,128)(2,1)S(1)} %copy.144), channel_id=1, source_target_pairs={{0,32},{32,64},{64,96},{96,128},{128,160},{160,192},{192,224},{1,3... | collective-permute-start | bytes 1179656 | tf_op jit(solution)/shard_map/ppermute | solution.py:18
  87.5 0.8 copy-start.5
  90.2 1.9 %copy-start.10 = (f32[6,256,256]{1,2,0:T(8,128)S(1)}, f32[6,256,256]{1,2,0:T(8,128)}, u32[]{:S(2)}) copy-start(f32[6,256,256]{1,2,0:T(8,128)} %get-tuple-element.32) | copy-start | bytes 4718596
  95.2 0.9 copy-start.3
  95.3 1.0 copy-start.4
  100.7 5.0 %copy-start.6 = (s32[2048]{0:T(1024)S(1)}, s32[2048]{0:T(1024)}, u32[]{:S(2)}) copy-start(s32[2048]{0:T(1024)} %get-tuple-element.3) | copy-start | bytes 24580
  100.7 5.8 %copy-start.9 = (pred[2048]{0:T(1024)(128)(4,1)S(1)}, pred[2048]{0:T(1024)(128)(4,1)}, u32[]{:S(2)}) copy-start(pred[2048]{0:T(1024)(128)(4,1)} %get-tuple-element.4) | copy-start | bytes 6148
  100.7 5.9 %copy-start.7 = (s32[2048]{0:T(1024)S(1)}, s32[2048]{0:T(1024)}, u32[]{:S(2)}) copy-start(s32[2048]{0:T(1024)} %get-tuple-element.36) | copy-start | bytes 24580
  100.7 35.2 %all-to-all-start.2 = ((bf16[32,3,16,768]{3,2,1,0:T(8,128)(2,1)}), bf16[32,3,16,768]{3,2,1,0:T(8,128)(2,1)S(1)}, u32[]{:S(2)}, u32[]{:S(2)}) async-start(bf16[32,3,16,768]{3,2,1,0:T(8,128)(2,1)} %copy.146), calls=%async_computation.2 | async-start | bytes 4718592 | tf_op jit(solution)/shard_map/all_to_all | solution.py:142

commit v10 on v9

--- a/solution.py
+++ b/solution.py
@@ -149,16 +149,15 @@
     arrived_b = exchange((shared_bwd, values_bwd, upstream_bwd), next_b[0])
     attended = forward_block(rows_f[0], rows_f[1], own_f[2].reshape(-1, CLUSTER), score_scale)
     moved_f = shifted(attended.reshape(1, block_rows, group_features), "pipe", 1)
+    (forward_in,) = give_back(moved_f, prev_f[1][None], prev_f[0][None])
     rows_b = gather_block(arrived_b, next_b[1])
     shared_grad, value_grad = backward_block(
         rows_b[0], rows_b[1], rows_b[2], next_b[2].reshape(-1, CLUSTER), score_scale
     )
     results_b = jnp.stack([shared_grad, value_grad]).reshape(2, block_rows, group_features)
     results_b = jnp.where(last_plane, jnp.zeros_like(results_b), results_b)
-    shared_grad_in, values_grad_in, forward_in = give_back(
-        jnp.concatenate([results_b, moved_f]),
-        jnp.stack([next_b[1]] * 2 + [prev_f[1]]),
-        jnp.stack([next_b[0]] * 2 + [prev_f[0]]),
+    shared_grad_in, values_grad_in = give_back(
+        results_b, jnp.stack([next_b[1]] * 2), jnp.stack([next_b[0]] * 2)
     )
     return (forward_in, shared_grad_in, values_grad_in)
 

time: 140 us -> 136 us (0.971)
  waiting for transfers between devices: 54.1 us -> 36.9 us
  other arithmetic: 15 us -> 21.5 us
  starting transfers between devices: 32.4 us -> 37.5 us
  matrix products: 22.5 us -> 24.1 us
    all_to_all x2, waiting for transfers between devices: 16.3 us -> 6.11 us  [exchange(): lax.all_to_all(stacked, axes, split_axis=0, concat_axis=0, tiled=True)]
    all_to_all x1 -> x2, waiting for transfers between devices: 28.6 us -> 18.5 us  [give_back(): lax.all_to_all(placed, axes, split_axis=0, concat_axis=0, tiled=True)]
    all_to_all x1 -> x2, starting transfers between devices: 4.96 us -> 10.2 us  [give_back(): lax.all_to_all(placed, axes, split_axis=0, concat_axis=0, tiled=True)]
    ppermute x4, waiting for transfers between devices: 9.18 us -> 12.2 us  [shifted(): return lax.ppermute(block, axis, route)]
    eq x3, other arithmetic: 0.02 us -> 1.85 us  [route_plan(): block_rank[:, None, None] == jnp.arange(slot_count)[None, None, :]]
    dot_general x1 -> x2, matrix products: 0.52 us -> 2.24 us  [give_back(): jnp.einsum('askt,smakf->atmf', send, arrived, preferred_element_type=jnp....]
    another operation x13 -> x14, local copies, waits for them, and re-layouts: 2.55 us -> 3.26 us
    transpose x1 -> x2, local copies, waits for them, and re-layouts: 2.71 us -> 3.35 us  [give_back(): jnp.einsum('airk,aif->rakf', gather, results, preferred_element_type=jnp....]
  transfers between devices with their start and end apart: 7 -> 8, of which waited for: 3 -> 5; matrix products, arithmetic and copies ran while one was open for 29% -> 40% of each run, Pallas kernels for 0% -> 0%
where the time goes in v10:
time: 136 us; the launch traced here: 135 us
  starting transfers between devices  37.5 us (28%)
  waiting for transfers between devices  36.9 us (27%)
  matrix products  24.1 us (18%)
  other arithmetic  21.5 us (16%)
  local copies, waits for them, and re-layouts  13.8 us (10%)
    all_to_all x2, waiting for transfers between devices, give_back(): lax.all_to_all(placed, axes, split_axis=0, concat_axis=0, tiled=True)  18.5 us
    all_to_all x2, starting transfers between devices, exchange(): lax.all_to_all(stacked, axes, split_axis=0, concat_axis=0, tiled=True)  14.6 us
    ppermute x4, starting transfers between devices, shifted(): return lax.ppermute(block, axis, route)  12.7 us
    ppermute x4, waiting for transfers between devices, shifted(): return lax.ppermute(block, axis, route)  12.2 us
    all_to_all x2, starting transfers between devices, give_back(): lax.all_to_all(placed, axes, split_axis=0, concat_axis=0, tiled=True)  10.2 us
    all_to_all x2, waiting for transfers between devices, exchange(): lax.all_to_all(stacked, axes, split_axis=0, concat_axis=0, tiled=True)  6.11 us
    sub x2, matrix products, softmax_weights(): exponent = jnp.exp(scores - largest)  5.17 us
    dot_general x5, matrix products, exchange(): jnp.einsum('skt,tf->skf', send, array[0], preferred_element_type=jnp.bflo...  5.06 us
  transfers between devices with their start and end apart: 8, of which 5 were waited for; matrix products, arithmetic and copies ran while one was open for 40% of the time, Pallas kernels for 0%

profile of v10, /device:TPU:96, one launch (start us, length us, event | category | flops | bytes accessed | tf_op | source)
XLA Modules:
  0.0 135.0 jit_solution(16334348345752592516)
XLA Ops:
  1.5 5.0 %collective-permute-start = (s32[2048]{0:T(1024)S(1)}, s32[2048]{0:T(1024)S(1)}, u32[]{:S(2)}, u32[]{:S(2)}) collective-permute-start(s32[2048]{0:T(1024)S(1)} %bitcast.222), channel_id=1, source_target_pairs={{0,32},{32,64},{64,96},{96,128},{128,160},{160,192},{192,224},{1,3... | collective-permute-start | bytes 24584 | tf_op jit(solution)/shard_map/ppermute | solution.py:18
  6.5 2.1 %collective-permute-start.2 = (s32[2048]{0:T(1024)S(1)}, s32[2048]{0:T(1024)S(1)}, u32[]{:S(2)}, u32[]{:S(2)}) collective-permute-start(s32[2048]{0:T(1024)S(1)} %bitcast.231), channel_id=1, source_target_pairs={{32,0},{64,32},{96,64},{128,96},{160,128},{192,160},{224,192},{33,... | collective-permute-start | bytes 24584 | tf_op jit(solution)/shard_map/ppermute | solution.py:18
  10.0 1.9 %collective-permute-start.3 = (bf16[3,64,3072]{2,1,0:T(8,128)(2,1)S(1)}, bf16[3,64,3072]{2,1,0:T(8,128)(2,1)}, u32[]{:S(2)}, u32[]{:S(2)}) collective-permute-start(bf16[3,64,3072]{2,1,0:T(8,128)(2,1)S(1)} %pad_maximum_fusion.3), channel_id=1, source_target_pairs={{32,0},{64,32},{96,64},{128,96},{160,128},{192,160},{224,192},{33,... | collective-permute-start | bytes 3538952 | tf_op jit(solution)/shard_map/ppermute | solution.py:18
  15.8 7.3 %all-to-all-start = ((bf16[32,2,16,768]{3,2,1,0:T(8,128)(2,1)}), bf16[32,2,16,768]{3,2,1,0:T(8,128)(2,1)S(1)}, u32[]{:S(2)}, u32[]{:S(2)}) async-start(bf16[32,2,16,768]{3,2,1,0:T(8,128)(2,1)} %bitcast.13), calls=%async_computation | async-start | bytes 3145728 | tf_op jit(solution)/shard_map/all_to_all | solution.py:133
  35.9 4.7 %collective-permute-done.3 = bf16[3,64,3072]{2,1,0:T(8,128)(2,1)} collective-permute-done((bf16[3,64,3072]{2,1,0:T(8,128)(2,1)S(1)}, bf16[3,64,3072]{2,1,0:T(8,128)(2,1)}, u32[]{:S(2)}, u32[]{:S(2)}) %collective-permute-start.3) | collective-permute-done | bytes 1179680 | tf_op jit(solution)/shard_map/ppermute | solution.py:18
  42.0 1.4 %convolution_bitcast_fusion.1 = bf16[8,1,16,3072]{3,2,0,1:T(8,128)(2,1)S(1)} fusion(bf16[3,64,3072]{2,1,0:T(8,128)(2,1)} %collective-permute-done.3, s32[8,16]{1,0:T(8,128)S(1)} %select_reduce_fusion, pred[8,16]{1,0:T(8,128)(4,1)S(1)} %fusion.55), kind=kOutput, calls=%fused_computation.3 | convolution fusion | flops 50348032 | bytes 1180288 | tf_op jit(solution)/shard_map/skt,tf->skf/dot_general | solution.py:124
  45.7 1.6 %copy.138 = bf16[8,12,16,768]{3,2,1,0:T(8,128)(2,1)} copy(bf16[8,12,16,768]{3,2,0,1:T(8,128)(2,1)S(1)} %pad_maximum_fusion.1) | data formatting | bytes 4718592 | tf_op jit(solution)/shard_map/concatenate.2
  48.4 7.3 %all-to-all-start.2 = ((bf16[32,3,16,768]{3,2,1,0:T(8,128)(2,1)}), bf16[32,3,16,768]{3,2,1,0:T(8,128)(2,1)S(1)}, u32[]{:S(2)}, u32[]{:S(2)}) async-start(bf16[32,3,16,768]{3,2,1,0:T(8,128)(2,1)} %bitcast.51), calls=%async_computation.2 | async-start | bytes 4718592 | tf_op jit(solution)/shard_map/all_to_all | solution.py:133
  57.0 2.0 %convolution_bitcast_fusion.9 = bf16[2,256,768]{1,2,0:T(8,128)(2,1)S(1)} fusion(bf16[32,2,16,768]{3,2,1,0:T(8,128)(2,1)} %copy-done.1, pred[256,16]{0,1:T(8,128)(4,1)} %iota_compare_fusion.16, pred[256,32]{0,1:T(8,128)(4,1)} %iota_compare_fusion.13), kind=kOutput, calls=%fused_computation.33 | convolution fusion | flops 402784256 | bytes 2371584 | tf_op jit(solution)/shard_map/irk,rakf->aif/dot_general | solution.py:137
  59.1 3.3 %fusion.125 = (f32[6,256]{1,0:T(8,128)}, f32[6,256,256]{1,2,0:T(8,128)}) fusion(bf16[256,6,128]{0,2,1:T(8,128)(2,1)S(1)} %bitcast.221, pred[256,256]{0,1:T(8,128)(4,1)} %fusion.42), kind=kOutput, calls=%fused_computation.230 | convolution fusion | flops 102236416 | bytes 2037760 | tf_op jit(solution)/shard_map/sub | solution.py:36
  62.4 1.7 %convolution_convert_fusion.1 = bf16[6,128,256]{2,1,0:T(8,128)(2,1)S(1)} fusion(bf16[256,6,128]{0,2,1:T(8,128)(2,1)S(1)} %bitcast.220, f32[6,256,256]{1,2,0:T(8,128)} %get-tuple-element.29, f32[6,256]{1,0:T(8,128)} %get-tuple-element.28), kind=kOutput, calls=%fused_computation.39 | convolution fusion | flops 101646336 | bytes 2365440 | tf_op jit(solution)/shard_map/nhqk,nkhd->nqhd/dot_general | solution.py:42
  64.3 3.6 %collective-permute-start.1 = (bf16[1,256,768]{2,1,0:T(8,128)(2,1)S(1)}, bf16[1,256,768]{2,1,0:T(8,128)(2,1)S(1)}, u32[]{:S(2)}, u32[]{:S(2)}) collective-permute-start(bf16[1,256,768]{2,1,0:T(8,128)(2,1)S(1)} %copy.133), channel_id=1, source_target_pairs={{0,32},{32,64},{64,96},{96,128},{128,160},{160,192},{192,224},{1,3... | collective-permute-start | bytes 1179656 | tf_op jit(solution)/shard_map/ppermute | solution.py:18
  70.0 7.5 %collective-permute-done.1 = bf16[1,256,768]{2,1,0:T(8,128)(2,1)S(1)} collective-permute-done((bf16[1,256,768]{2,1,0:T(8,128)(2,1)S(1)}, bf16[1,256,768]{2,1,0:T(8,128)(2,1)S(1)}, u32[]{:S(2)}, u32[]{:S(2)}) %collective-permute-start.1) | collective-permute-done | bytes 393248 | tf_op jit(solution)/shard_map/ppermute | solution.py:18
  79.9 6.1 %all-to-all-done.2 = bf16[32,3,16,768]{3,2,1,0:T(8,128)(2,1)S(1)} async-done(((bf16[32,3,16,768]{3,2,1,0:T(8,128)(2,1)}), bf16[32,3,16,768]{3,2,1,0:T(8,128)(2,1)S(1)}, u32[]{:S(2)}, u32[]{:S(2)}) %all-to-all-start.2) | async-done | bytes 2359328 | tf_op jit(solution)/shard_map/all_to_all | solution.py:133
  86.0 5.0 %all-to-all-start.1 = ((bf16[32,1,16,768]{3,2,1,0:T(8,128)(2,1)}), bf16[32,1,16,768]{3,2,1,0:T(8,128)(2,1)S(1)}, u32[]{:S(2)}, u32[]{:S(2)}) async-start(bf16[32,1,16,768]{3,2,1,0:T(8,128)(2,1)} %copy.135), calls=%async_computation.1 | async-start | bytes 1572864 | tf_op jit(solution)/shard_map/all_to_all | solution.py:142
  91.0 1.5 %convolution_bitcast_fusion.7 = bf16[3,256,768]{1,2,0:T(8,128)(2,1)S(1)} fusion(bf16[32,3,16,768]{3,2,1,0:T(8,128)(2,1)S(1)} %all-to-all-done.2, pred[256,16]{0,1:T(8,128)(4,1)} %iota_compare_fusion.14, pred[256,32]{0,1:T(8,128)(4,1)S(1)} %iota_compare_fusion.9), kind=kOutput, calls=%fused_computation.29 | convolution fusion | flops 604110848 | bytes 3551232 | tf_op jit(solution)/shard_map/irk,rakf->aif/dot_general | solution.py:137
  93.4 1.9 %fusion.126 = (f32[6,256]{1,0:T(8,128)S(1)}, f32[6,256,256]{1,2,0:T(8,128)}) fusion(pred[256,256]{0,1:T(8,128)(4,1)S(1)} %copy-done.5, bf16[256,6,128]{0,2,1:T(8,128)(2,1)S(1)} %bitcast.205), kind=kOutput, calls=%fused_computation.231 | convolution fusion | flops 102236416 | bytes 2037760 | tf_op jit(solution)/shard_map/sub | solution.py:36
  95.2 1.8 %fusion.15 = f32[256,6]{0,1:T(8,128)S(1)} fusion(bf16[256,6,128]{0,2,1:T(8,128)(2,1)S(1)} %bitcast.214, bf16[1,256,6,128]{1,3,2,0:T(8,128)(2,1)S(1)} %bitcast.211, f32[6,256,256]{1,2,0:T(8,128)} %get-tuple-element.31, f32[6,256]{1,0:T(8,128)S(1)} %get-tuple-element.30), kind=kOutput, calls=%fused_computation.40 | convolution fusion | flops 102038016 | bytes 2371584 | tf_op jit(solution)/shard_map/nhqk,nkhd->nqhd/dot_general | solution.py:50
  98.4 1.8 %convolution_convert_fusion = bf16[6,128,256]{2,1,0:T(8,128)(2,1)S(1)} fusion(bf16[256,6,128]{0,2,1:T(8,128)(2,1)S(1)} %bitcast.213, f32[6,256,256]{1,2,0:T(8,128)} %get-tuple-element.31, f32[6,256]{1,0:T(8,128)S(1)} %get-tuple-element.30), kind=kOutput, calls=%fused_computation.38 | convolution fusion | flops 101646336 | bytes 2365440 | tf_op jit(solution)/shard_map/nhqk,nqhd->nkhd/dot_general | solution.py:52
  101.1 2.0 %copy.151 = bf16[32,2,16,768]{3,2,1,0:T(8,128)(2,1)} copy(bf16[32,2,16,768]{3,0,2,1:T(8,128)(2,1)S(1)} %convolution_bitcast_fusion.6) | data formatting | bytes 3145728 | tf_op jit(solution)/shard_map/airk,aif->rakf/transpose | solution.py:141
  103.1 2.2 %all-to-all-done.1 = bf16[32,1,16,768]{3,2,1,0:T(8,128)(2,1)S(1)} async-done(((bf16[32,1,16,768]{3,2,1,0:T(8,128)(2,1)}), bf16[32,1,16,768]{3,2,1,0:T(8,128)(2,1)S(1)}, u32[]{:S(2)}, u32[]{:S(2)}) %all-to-all-start.1) | async-done | bytes 786464 | tf_op jit(solution)/shard_map/all_to_all | solution.py:142
  105.2 5.2 %all-to-all-start.3 = ((bf16[32,2,16,768]{3,2,1,0:T(8,128)(2,1)}), bf16[32,2,16,768]{3,2,1,0:T(8,128)(2,1)S(1)}, u32[]{:S(2)}, u32[]{:S(2)}) async-start(bf16[32,2,16,768]{3,2,1,0:T(8,128)(2,1)} %copy.151), calls=%async_computation.3 | async-start | bytes 3145728 | tf_op jit(solution)/shard_map/all_to_all | solution.py:142
  114.7 1.8 %convolution_bitcast_fusion.5 = bf16[1,64,3072]{2,1,0:T(8,128)(2,1)} fusion(bf16[3072,16,8]{0,1,2:T(8,128)(2,1)S(1)} %dot_general.75, s32[16,8]{0,1:T(8,128)} %bitcast.230, pred[16,8]{0,1:T(8,128)(4,1)} %bitcast.232), kind=kOutput, calls=%fused_computation.7 | convolution fusion | flops 50348032 | bytes 1180288 | tf_op jit(solution)/shard_map/askt,smakf->atmf/dot_general | solution.py:144
  116.6 16.4 %all-to-all-done.3 = bf16[32,2,16,768]{3,2,1,0:T(8,128)(2,1)S(1)} async-done(((bf16[32,2,16,768]{3,2,1,0:T(8,128)(2,1)}), bf16[32,2,16,768]{3,2,1,0:T(8,128)(2,1)S(1)}, u32[]{:S(2)}, u32[]{:S(2)}) %all-to-all-start.3) | async-done | bytes 1572896 | tf_op jit(solution)/shard_map/all_to_all | solution.py:142
  (126 shorter events, 38.6 us)
Async XLA Ops:
  0.6 12.7 %copy-start = (bf16[1,64,3072]{2,1,0:T(8,128)(2,1)S(1)}, bf16[1,64,3072]{2,1,0:T(8,128)(2,1)}, u32[]{:S(2)}) copy-start(bf16[1,64,3072]{2,1,0:T(8,128)(2,1)} %param.6) | copy-start | bytes 1179652
  1.5 26.6 %collective-permute-start = (s32[2048]{0:T(1024)S(1)}, s32[2048]{0:T(1024)S(1)}, u32[]{:S(2)}, u32[]{:S(2)}) collective-permute-start(s32[2048]{0:T(1024)S(1)} %bitcast.222), channel_id=1, source_target_pairs={{0,32},{32,64},{64,96},{96,128},{128,160},{160,192},{192,224},{1,3... | collective-permute-start | bytes 24584 | tf_op jit(solution)/shard_map/ppermute | solution.py:18
  6.5 7.2 %copy-start.2 = (bf16[1,64,3072]{2,1,0:T(8,128)(2,1)S(1)}, bf16[1,64,3072]{2,1,0:T(8,128)(2,1)}, u32[]{:S(2)}) copy-start(bf16[1,64,3072]{2,1,0:T(8,128)(2,1)} %param.7) | copy-start | bytes 1179652
  6.5 20.8 %collective-permute-start.2 = (s32[2048]{0:T(1024)S(1)}, s32[2048]{0:T(1024)S(1)}, u32[]{:S(2)}, u32[]{:S(2)}) collective-permute-start(s32[2048]{0:T(1024)S(1)} %bitcast.231), channel_id=1, source_target_pairs={{32,0},{64,32},{96,64},{128,96},{160,128},{192,160},{224,192},{33,... | collective-permute-start | bytes 24584 | tf_op jit(solution)/shard_map/ppermute | solution.py:18
  10.0 30.6 %collective-permute-start.3 = (bf16[3,64,3072]{2,1,0:T(8,128)(2,1)S(1)}, bf16[3,64,3072]{2,1,0:T(8,128)(2,1)}, u32[]{:S(2)}, u32[]{:S(2)}) collective-permute-start(bf16[3,64,3072]{2,1,0:T(8,128)(2,1)S(1)} %pad_maximum_fusion.3), channel_id=1, source_target_pairs={{32,0},{64,32},{96,64},{128,96},{160,128},{192,160},{224,192},{33,... | collective-permute-start | bytes 3538952 | tf_op jit(solution)/shard_map/ppermute | solution.py:18
  15.8 31.5 %all-to-all-start = ((bf16[32,2,16,768]{3,2,1,0:T(8,128)(2,1)}), bf16[32,2,16,768]{3,2,1,0:T(8,128)(2,1)S(1)}, u32[]{:S(2)}, u32[]{:S(2)}) async-start(bf16[32,2,16,768]{3,2,1,0:T(8,128)(2,1)} %bitcast.13), calls=%async_computation | async-start | bytes 3145728 | tf_op jit(solution)/shard_map/all_to_all | solution.py:133
  47.3 1.2 copy-start.1
  48.4 37.6 %all-to-all-start.2 = ((bf16[32,3,16,768]{3,2,1,0:T(8,128)(2,1)}), bf16[32,3,16,768]{3,2,1,0:T(8,128)(2,1)S(1)}, u32[]{:S(2)}, u32[]{:S(2)}) async-start(bf16[32,3,16,768]{3,2,1,0:T(8,128)(2,1)} %bitcast.51), calls=%async_computation.2 | async-start | bytes 4718592 | tf_op jit(solution)/shard_map/all_to_all | solution.py:133
  64.3 13.2 %collective-permute-start.1 = (bf16[1,256,768]{2,1,0:T(8,128)(2,1)S(1)}, bf16[1,256,768]{2,1,0:T(8,128)(2,1)S(1)}, u32[]{:S(2)}, u32[]{:S(2)}) collective-permute-start(bf16[1,256,768]{2,1,0:T(8,128)(2,1)S(1)} %copy.133), channel_id=1, source_target_pairs={{0,32},{32,64},{64,96},{96,128},{128,160},{160,192},{192,224},{1,3... | collective-permute-start | bytes 1179656 | tf_op jit(solution)/shard_map/ppermute | solution.py:18
  86.0 19.2 %all-to-all-start.1 = ((bf16[32,1,16,768]{3,2,1,0:T(8,128)(2,1)}), bf16[32,1,16,768]{3,2,1,0:T(8,128)(2,1)S(1)}, u32[]{:S(2)}, u32[]{:S(2)}) async-start(bf16[32,1,16,768]{3,2,1,0:T(8,128)(2,1)} %copy.135), calls=%async_computation.1 | async-start | bytes 1572864 | tf_op jit(solution)/shard_map/all_to_all | solution.py:142
  92.5 0.8 copy-start.5
  95.2 1.9 %copy-start.9 = (f32[6,256,256]{1,2,0:T(8,128)S(1)}, f32[6,256,256]{1,2,0:T(8,128)}, u32[]{:S(2)}) copy-start(f32[6,256,256]{1,2,0:T(8,128)} %get-tuple-element.31) | copy-start | bytes 4718596
  98.4 2.0 %copy-start.3 = (pred[1,256,32,16]{1,2,3,0:T(32,128)(4,1)S(1)}, pred[1,256,32,16]{1,2,3,0:T(32,128)(4,1)}, u32[]{:S(2)}) copy-start(pred[1,256,32,16]{1,2,3,0:T(32,128)(4,1)} %broadcast_and_fusion) | copy-start | bytes 393220
  103.1 7.4 %copy-start.6 = (s32[2048]{0:T(1024)S(1)}, s32[2048]{0:T(1024)}, u32[]{:S(2)}) copy-start(s32[2048]{0:T(1024)} %get-tuple-element.32) | copy-start | bytes 24580
  103.1 8.2 %copy-start.8 = (pred[2048]{0:T(1024)(128)(4,1)S(1)}, pred[2048]{0:T(1024)(128)(4,1)}, u32[]{:S(2)}) copy-start(pred[2048]{0:T(1024)(128)(4,1)} %get-tuple-element.33) | copy-start | bytes 6148
  103.1 8.2 %copy-start.7 = (s32[2048]{0:T(1024)S(1)}, s32[2048]{0:T(1024)}, u32[]{:S(2)}) copy-start(s32[2048]{0:T(1024)} %get-tuple-element.35) | copy-start | bytes 24580
  105.2 27.7 %all-to-all-start.3 = ((bf16[32,2,16,768]{3,2,1,0:T(8,128)(2,1)}), bf16[32,2,16,768]{3,2,1,0:T(8,128)(2,1)S(1)}, u32[]{:S(2)}, u32[]{:S(2)}) async-start(bf16[32,2,16,768]{3,2,1,0:T(8,128)(2,1)} %copy.151), calls=%async_computation.3 | async-start | bytes 3145728 | tf_op jit(solution)/shard_map/all_to_all | solution.py:142
  114.2 18.8 %copy-start.4 = (pred[1,8,16,64]{3,2,1,0:T(8,128)(4,1)S(1)}, pred[1,8,16,64]{3,2,1,0:T(8,128)(4,1)}, u32[]{:S(2)}) copy-start(pred[1,8,16,64]{3,2,1,0:T(8,128)(4,1)} %fusion.65) | copy-start | bytes 24580

commit v11 on v10

--- a/solution.py
+++ b/solution.py
@@ -112,12 +112,11 @@
     order_next_bwd = shifted(cluster_order[0, 1], "pipe", -1)
     inputs_b = shifted(jnp.concatenate([shared_bwd, values_bwd, upstream_bwd]), "pipe", -1)
     shared_bwd, values_bwd, upstream_bwd = inputs_b[0:1], inputs_b[1:2], inputs_b[2:3]
-    order_prev_fwd = shifted(order_fwd, "pipe", 1)
 
     def plan(order):
         return route_plan(order, seq_index, range_here, seq_count, group_count, tok_dev, slot_count)
 
-    own_f, next_b, prev_f = plan(order_fwd), plan(order_next_bwd), plan(order_prev_fwd)
+    own_f, next_b = plan(order_fwd), plan(order_next_bwd)
 
     def exchange(arrays, send):
         packed = [
@@ -148,8 +147,27 @@
     rows_f = gather_block(arrived_f, own_f[1])
     arrived_b = exchange((shared_bwd, values_bwd, upstream_bwd), next_b[0])
     attended = forward_block(rows_f[0], rows_f[1], own_f[2].reshape(-1, CLUSTER), score_scale)
-    moved_f = shifted(attended.reshape(1, block_rows, group_features), "pipe", 1)
-    (forward_in,) = give_back(moved_f, prev_f[1][None], prev_f[0][None])
+    placed_f = jnp.einsum(
+        "irk,if->rkf", own_f[1], attended.reshape(block_rows, group_features),
+        preferred_element_type=jnp.bfloat16,
+    ).reshape(group_count * slot_count, group_features)
+    unpack = own_f[0].reshape(-1)
+    extra = -(-unpack.shape[0] // group_features)
+    unpack = jnp.pad(unpack, (0, extra * group_features - unpack.shape[0]))
+    moved_f = shifted(
+        jnp.concatenate([placed_f, unpack.reshape(extra, group_features)]), "pipe", 1
+    )
+    unpack_f = moved_f[group_count * slot_count :].reshape(-1)[: own_f[0].size].reshape(
+        own_f[0].shape
+    )
+    placed_f = moved_f[: group_count * slot_count].reshape(
+        group_count, 1, slot_count, group_features
+    )
+    arrived_f = lax.all_to_all(placed_f, axes, split_axis=0, concat_axis=0, tiled=True)
+    arrived_f = arrived_f.reshape(seq_count, mp_count, 1, slot_count, group_features)
+    forward_in = jnp.einsum(
+        "skt,smakf->atmf", unpack_f, arrived_f, preferred_element_type=jnp.bfloat16
+    ).reshape(1, tok_dev, features)
     rows_b = gather_block(arrived_b, next_b[1])
     shared_grad, value_grad = backward_block(
         rows_b[0], rows_b[1], rows_b[2], next_b[2].reshape(-1, CLUSTER), score_scale

time: 136 us -> 134 us (0.985)
  waiting for transfers between devices: 36.9 us -> 49.2 us
  other arithmetic: 21.5 us -> 13 us
  matrix products: 24.1 us -> 20.7 us
  starting transfers between devices: 37.5 us -> 34.4 us
    ppermute x4 -> x3, waiting for transfers between devices: 12.2 us -> 25.2 us  [shifted(): return lax.ppermute(block, axis, route)]
    all_to_all x0 -> x1, starting transfers between devices: none -> 7.42 us  [per_device(): lax.all_to_all(placed_f, axes, split_axis=0, concat_axis=0, tiled=True)]
    all_to_all x2, waiting for transfers between devices: 6.11 us -> 0.01 us  [exchange(): lax.all_to_all(stacked, axes, split_axis=0, concat_axis=0, tiled=True)]
    all_to_all x2 -> x1, starting transfers between devices: 10.2 us -> 4.52 us  [give_back(): lax.all_to_all(placed, axes, split_axis=0, concat_axis=0, tiled=True)]
    ppermute x4 -> x3, starting transfers between devices: 12.7 us -> 7.81 us  [shifted(): return lax.ppermute(block, axis, route)]
    all_to_all x0 -> x1, waiting for transfers between devices: none -> 2.81 us  [per_device(): lax.all_to_all(placed_f, axes, split_axis=0, concat_axis=0, tiled=True)]
    all_to_all x2 -> x1, waiting for transfers between devices: 18.5 us -> 21.1 us  [give_back(): lax.all_to_all(placed, axes, split_axis=0, concat_axis=0, tiled=True)]
    dot_general x2 -> x1, matrix products: 2.24 us -> 0.42 us  [give_back(): jnp.einsum('askt,smakf->atmf', send, arrived, preferred_element_type=jnp....]
  transfers between devices with their start and end apart: 8 -> 7, of which waited for: 5 -> 4; matrix products, arithmetic and copies ran while one was open for 40% -> 32% of each run, Pallas kernels for 0% -> 0%
where the time goes in v11:
time: 134 us; the launch traced here: 133 us
  waiting for transfers between devices  49.2 us (37%)
  starting transfers between devices  34.4 us (26%)
  matrix products  20.7 us (15%)
  local copies, waits for them, and re-layouts  14.4 us (11%)
  other arithmetic  13 us (10%)
    ppermute x3, waiting for transfers between devices, shifted(): return lax.ppermute(block, axis, route)  25.2 us
    all_to_all x1, waiting for transfers between devices, give_back(): lax.all_to_all(placed, axes, split_axis=0, concat_axis=0, tiled=True)  21.1 us
    all_to_all x2, starting transfers between devices, exchange(): lax.all_to_all(stacked, axes, split_axis=0, concat_axis=0, tiled=True)  14.6 us
    ppermute x3, starting transfers between devices, shifted(): return lax.ppermute(block, axis, route)  7.81 us
    all_to_all x1, starting transfers between devices, per_device(): lax.all_to_all(placed_f, axes, split_axis=0, concat_axis=0, tiled=True)  7.42 us
    dot_general x5, matrix products, exchange(): jnp.einsum('skt,tf->skf', send, array[0], preferred_element_type=jnp.bflo...  5.06 us
    sub x2, matrix products, softmax_weights(): exponent = jnp.exp(scores - largest)  4.57 us
    all_to_all x1, starting transfers between devices, give_back(): lax.all_to_all(placed, axes, split_axis=0, concat_axis=0, tiled=True)  4.52 us
  transfers between devices with their start and end apart: 7, of which 4 were waited for; matrix products, arithmetic and copies ran while one was open for 32% of the time, Pallas kernels for 0%

profile of v11, /device:TPU:96, one launch (start us, length us, event | category | flops | bytes accessed | tf_op | source)
XLA Modules:
  0.0 133.0 jit_solution(4092312822079736120)
XLA Ops:
  1.5 2.1 %collective-permute-start.1 = (s32[2048]{0:T(1024)S(1)}, s32[2048]{0:T(1024)S(1)}, u32[]{:S(2)}, u32[]{:S(2)}) collective-permute-start(s32[2048]{0:T(1024)S(1)} %bitcast.209), channel_id=1, source_target_pairs={{32,0},{64,32},{96,64},{128,96},{160,128},{192,160},{224,192},{33,... | collective-permute-start | bytes 24584 | tf_op jit(solution)/shard_map/ppermute | solution.py:18
  3.6 1.4 %pad_maximum_fusion.3 = bf16[3,64,3072]{2,1,0:T(8,128)(2,1)S(1)} fusion(bf16[1,64,3072]{2,1,0:T(8,128)(2,1)} %param.10, bf16[1,64,3072]{2,1,0:T(8,128)(2,1)} %param.9, bf16[1,64,3072]{2,1,0:T(8,128)(2,1)} %param.8), kind=kLoop, calls=%fused_computation.40 | loop fusion | flops 1179648 | bytes 2359296 | tf_op jit(solution)/shard_map/concatenate | solution.py:113
  5.0 2.0 %collective-permute-start.2 = (bf16[3,64,3072]{2,1,0:T(8,128)(2,1)S(1)}, bf16[3,64,3072]{2,1,0:T(8,128)(2,1)}, u32[]{:S(2)}, u32[]{:S(2)}) collective-permute-start(bf16[3,64,3072]{2,1,0:T(8,128)(2,1)S(1)} %pad_maximum_fusion.3), channel_id=1, source_target_pairs={{32,0},{64,32},{96,64},{128,96},{160,128},{192,160},{224,192},{33,... | collective-permute-start | bytes 3538952 | tf_op jit(solution)/shard_map/ppermute | solution.py:18
  9.6 1.3 copy.118
  10.9 7.3 %all-to-all-start = ((bf16[32,2,16,768]{3,2,1,0:T(8,128)(2,1)}), bf16[32,2,16,768]{3,2,1,0:T(8,128)(2,1)S(1)}, u32[]{:S(2)}, u32[]{:S(2)}) async-start(bf16[32,2,16,768]{3,2,1,0:T(8,128)(2,1)} %bitcast.12), calls=%async_computation | async-start | bytes 3145728 | tf_op jit(solution)/shard_map/all_to_all | solution.py:132
  27.2 8.8 %collective-permute-done.2 = bf16[3,64,3072]{2,1,0:T(8,128)(2,1)} collective-permute-done((bf16[3,64,3072]{2,1,0:T(8,128)(2,1)S(1)}, bf16[3,64,3072]{2,1,0:T(8,128)(2,1)}, u32[]{:S(2)}, u32[]{:S(2)}) %collective-permute-start.2) | collective-permute-done | bytes 1179680 | tf_op jit(solution)/shard_map/ppermute | solution.py:18
  36.0 1.4 %convolution_bitcast_fusion = bf16[8,1,16,3072]{3,2,0,1:T(8,128)(2,1)S(1)} fusion(bf16[3,64,3072]{2,1,0:T(8,128)(2,1)} %collective-permute-done.2, s32[8,16]{1,0:T(8,128)S(1)} %select_reduce_fusion, pred[8,16]{1,0:T(8,128)(4,1)S(1)} %fusion.50), kind=kOutput, calls=%fused_computation.2 | convolution fusion | flops 50348032 | bytes 1180288 | tf_op jit(solution)/shard_map/skt,tf->skf/dot_general | solution.py:123
  37.4 1.4 %convolution_bitcast_fusion.1 = bf16[8,1,16,3072]{3,2,0,1:T(8,128)(2,1)S(1)} fusion(bf16[3,64,3072]{2,1,0:T(8,128)(2,1)} %collective-permute-done.2, s32[8,16]{1,0:T(8,128)S(1)} %select_reduce_fusion, pred[8,16]{1,0:T(8,128)(4,1)S(1)} %fusion.50), kind=kOutput, calls=%fused_computation.3 | convolution fusion | flops 50348032 | bytes 1180288 | tf_op jit(solution)/shard_map/skt,tf->skf/dot_general | solution.py:123
  38.8 1.4 %convolution_bitcast_fusion.2 = bf16[8,1,16,3072]{3,2,0,1:T(8,128)(2,1)S(1)} fusion(bf16[3,64,3072]{2,1,0:T(8,128)(2,1)} %collective-permute-done.2, s32[8,16]{1,0:T(8,128)S(1)} %select_reduce_fusion, pred[8,16]{1,0:T(8,128)(4,1)S(1)} %fusion.50), kind=kOutput, calls=%fused_computation.4 | convolution fusion | flops 50348032 | bytes 1180288 | tf_op jit(solution)/shard_map/skt,tf->skf/dot_general | solution.py:123
  41.1 1.6 %copy.125 = bf16[8,12,16,768]{3,2,1,0:T(8,128)(2,1)} copy(bf16[8,12,16,768]{3,2,0,1:T(8,128)(2,1)S(1)} %pad_maximum_fusion.1) | data formatting | bytes 4718592 | tf_op jit(solution)/shard_map/concatenate.1
  43.9 7.3 %all-to-all-start.2 = ((bf16[32,3,16,768]{3,2,1,0:T(8,128)(2,1)}), bf16[32,3,16,768]{3,2,1,0:T(8,128)(2,1)S(1)}, u32[]{:S(2)}, u32[]{:S(2)}) async-start(bf16[32,3,16,768]{3,2,1,0:T(8,128)(2,1)} %bitcast.44), calls=%async_computation.2 | async-start | bytes 4718592 | tf_op jit(solution)/shard_map/all_to_all | solution.py:132
  51.2 2.0 %convolution_bitcast_fusion.8 = bf16[2,256,768]{1,2,0:T(8,128)(2,1)S(1)} fusion(bf16[32,2,16,768]{3,2,1,0:T(8,128)(2,1)} %copy-done.1, pred[256,16]{0,1:T(8,128)(4,1)S(1)} %copy-done.14, pred[256,32]{0,1:T(8,128)(4,1)S(1)} %iota_compare_fusion.9), kind=kOutput, calls=%fused_computation.32 | convolution fusion | flops 402784256 | bytes 2371584 | tf_op jit(solution)/shard_map/irk,rakf->aif/dot_general | solution.py:136
  53.3 2.7 %fusion.105 = (f32[6,256]{1,0:T(8,128)S(1)}, f32[6,256,256]{1,2,0:T(8,128)}) fusion(bf16[256,6,128]{0,2,1:T(8,128)(2,1)S(1)} %bitcast.201, pred[256,256]{0,1:T(8,128)(4,1)} %fusion.41), kind=kOutput, calls=%fused_computation.193 | convolution fusion | flops 102236416 | bytes 2037760 | tf_op jit(solution)/shard_map/sub | solution.py:36
  56.0 1.7 %convolution_convert_fusion.1 = bf16[6,128,256]{2,1,0:T(8,128)(2,1)S(1)} fusion(bf16[256,6,128]{0,2,1:T(8,128)(2,1)S(1)} %bitcast.200, f32[6,256,256]{1,2,0:T(8,128)} %get-tuple-element.27, f32[6,256]{1,0:T(8,128)S(1)} %get-tuple-element.26), kind=kOutput, calls=%fused_computation.37 | convolution fusion | flops 101646336 | bytes 2365440 | tf_op jit(solution)/shard_map/nhqk,nkhd->nqhd/dot_general | solution.py:42
  58.3 3.6 %collective-permute-start = (bf16[523,768]{1,0:T(8,128)(2,1)S(1)}, bf16[523,768]{1,0:T(8,128)(2,1)S(1)}, u32[]{:S(2)}, u32[]{:S(2)}) collective-permute-start(bf16[523,768]{1,0:T(8,128)(2,1)S(1)} %pad_maximum_fusion.4), channel_id=1, source_target_pairs={{0,32},{32,64},{64,96},{96,128},{128,160},{160,192},{192,224},{1,3... | collective-permute-start | bytes 2409992 | tf_op jit(solution)/shard_map/ppermute | solution.py:18
  64.0 16.4 %collective-permute-done = bf16[523,768]{1,0:T(8,128)(2,1)S(1)} collective-permute-done((bf16[523,768]{1,0:T(8,128)(2,1)S(1)}, bf16[523,768]{1,0:T(8,128)(2,1)S(1)}, u32[]{:S(2)}, u32[]{:S(2)}) %collective-permute-start) | collective-permute-done | bytes 803360 | tf_op jit(solution)/shard_map/ppermute | solution.py:18
  82.3 7.4 %all-to-all-start.1 = ((bf16[32,1,16,768]{3,2,1,0:T(8,128)(2,1)}), bf16[32,1,16,768]{3,2,1,0:T(8,128)(2,1)S(1)}, u32[]{:S(2)}, u32[]{:S(2)}) async-start(bf16[32,1,16,768]{3,2,1,0:T(8,128)(2,1)} %bitcast.24), calls=%async_computation.1 | async-start | bytes 1572864 | tf_op jit(solution)/shard_map/all_to_all | solution.py:166
  91.4 1.9 %fusion.106 = (f32[6,256]{1,0:T(8,128)S(1)}, f32[6,256,256]{1,2,0:T(8,128)}) fusion(pred[256,256]{0,1:T(8,128)(4,1)S(1)} %copy-done.7, bf16[256,6,128]{0,2,1:T(8,128)(2,1)S(1)} %bitcast.185), kind=kOutput, calls=%fused_computation.194 | convolution fusion | flops 102236416 | bytes 2037760 | tf_op jit(solution)/shard_map/sub | solution.py:36
  93.2 1.8 %fusion.15 = f32[256,6]{0,1:T(8,128)S(1)} fusion(bf16[256,6,128]{0,2,1:T(8,128)(2,1)S(1)} %bitcast.194, bf16[1,256,6,128]{1,3,2,0:T(8,128)(2,1)S(1)} %bitcast.191, f32[6,256,256]{1,2,0:T(8,128)} %get-tuple-element.29, f32[6,256]{1,0:T(8,128)S(1)} %get-tuple-element.28), kind=kOutput, calls=%fused_computation.38 | convolution fusion | flops 102038016 | bytes 2371584 | tf_op jit(solution)/shard_map/nhqk,nkhd->nqhd/dot_general | solution.py:50
  96.4 1.8 %convolution_convert_fusion = bf16[6,128,256]{2,1,0:T(8,128)(2,1)S(1)} fusion(bf16[256,6,128]{0,2,1:T(8,128)(2,1)S(1)} %bitcast.193, f32[6,256,256]{1,2,0:T(8,128)} %get-tuple-element.29, f32[6,256]{1,0:T(8,128)S(1)} %get-tuple-element.28), kind=kOutput, calls=%fused_computation.36 | convolution fusion | flops 101646336 | bytes 2365440 | tf_op jit(solution)/shard_map/nhqk,nqhd->nkhd/dot_general | solution.py:52
  99.1 2.0 %copy.138 = bf16[32,2,16,768]{3,2,1,0:T(8,128)(2,1)} copy(bf16[32,2,16,768]{3,0,2,1:T(8,128)(2,1)S(1)} %convolution_bitcast_fusion.5) | data formatting | bytes 3145728 | tf_op jit(solution)/shard_map/airk,aif->rakf/transpose | solution.py:140
  101.1 2.8 %all-to-all-done.1 = bf16[32,1,16,768]{3,2,1,0:T(8,128)(2,1)S(1)} async-done(((bf16[32,1,16,768]{3,2,1,0:T(8,128)(2,1)}), bf16[32,1,16,768]{3,2,1,0:T(8,128)(2,1)S(1)}, u32[]{:S(2)}, u32[]{:S(2)}) %all-to-all-start.1) | async-done | bytes 786464 | tf_op jit(solution)/shard_map/all_to_all | solution.py:166
  103.9 4.5 %all-to-all-start.3 = ((bf16[32,2,16,768]{3,2,1,0:T(8,128)(2,1)}), bf16[32,2,16,768]{3,2,1,0:T(8,128)(2,1)S(1)}, u32[]{:S(2)}, u32[]{:S(2)}) async-start(bf16[32,2,16,768]{3,2,1,0:T(8,128)(2,1)} %copy.138), calls=%async_computation.3 | async-start | bytes 3145728 | tf_op jit(solution)/shard_map/all_to_all | solution.py:141
  109.8 21.1 %all-to-all-done.3 = bf16[32,2,16,768]{3,2,1,0:T(8,128)(2,1)S(1)} async-done(((bf16[32,2,16,768]{3,2,1,0:T(8,128)(2,1)}), bf16[32,2,16,768]{3,2,1,0:T(8,128)(2,1)S(1)}, u32[]{:S(2)}, u32[]{:S(2)}) %all-to-all-start.3) | async-done | bytes 1572896 | tf_op jit(solution)/shard_map/all_to_all | solution.py:141
  (126 shorter events, 25.6 us)
Async XLA Ops:
  0.6 7.8 %copy-start = (bf16[1,64,3072]{2,1,0:T(8,128)(2,1)S(1)}, bf16[1,64,3072]{2,1,0:T(8,128)(2,1)}, u32[]{:S(2)}) copy-start(bf16[1,64,3072]{2,1,0:T(8,128)(2,1)} %param.7) | copy-start | bytes 1179652
  1.5 7.4 %copy-start.4 = (bf16[1,64,3072]{2,1,0:T(8,128)(2,1)S(1)}, bf16[1,64,3072]{2,1,0:T(8,128)(2,1)}, u32[]{:S(2)}) copy-start(bf16[1,64,3072]{2,1,0:T(8,128)(2,1)} %param.6) | copy-start | bytes 1179652
  1.5 22.0 %collective-permute-start.1 = (s32[2048]{0:T(1024)S(1)}, s32[2048]{0:T(1024)S(1)}, u32[]{:S(2)}, u32[]{:S(2)}) collective-permute-start(s32[2048]{0:T(1024)S(1)} %bitcast.209), channel_id=1, source_target_pairs={{32,0},{64,32},{96,64},{128,96},{160,128},{192,160},{224,192},{33,... | collective-permute-start | bytes 24584 | tf_op jit(solution)/shard_map/ppermute | solution.py:18
  5.0 31.0 %collective-permute-start.2 = (bf16[3,64,3072]{2,1,0:T(8,128)(2,1)S(1)}, bf16[3,64,3072]{2,1,0:T(8,128)(2,1)}, u32[]{:S(2)}, u32[]{:S(2)}) collective-permute-start(bf16[3,64,3072]{2,1,0:T(8,128)(2,1)S(1)} %pad_maximum_fusion.3), channel_id=1, source_target_pairs={{32,0},{64,32},{96,64},{128,96},{160,128},{192,160},{224,192},{33,... | collective-permute-start | bytes 3538952 | tf_op jit(solution)/shard_map/ppermute | solution.py:18
  10.9 31.8 %all-to-all-start = ((bf16[32,2,16,768]{3,2,1,0:T(8,128)(2,1)}), bf16[32,2,16,768]{3,2,1,0:T(8,128)(2,1)S(1)}, u32[]{:S(2)}, u32[]{:S(2)}) async-start(bf16[32,2,16,768]{3,2,1,0:T(8,128)(2,1)} %bitcast.12), calls=%async_computation | async-start | bytes 3145728 | tf_op jit(solution)/shard_map/all_to_all | solution.py:132
  26.0 14.3 %copy-start.12 = (s32[256]{0:T(256)}, s32[256]{0:T(256)S(1)}, u32[]{:S(2)}) copy-start(s32[256]{0:T(256)S(1)} %and_select_fusion) | copy-start | bytes 3076
  26.4 13.9 %copy-start.8 = (pred[8,16]{1,0:T(8,128)(4,1)}, pred[8,16]{1,0:T(8,128)(4,1)S(1)}, u32[]{:S(2)}) copy-start(pred[8,16]{1,0:T(8,128)(4,1)S(1)} %fusion.50) | copy-start | bytes 388
  42.7 1.2 copy-start.1
  42.7 8.5 %copy-start.14 = (pred[256,16]{0,1:T(8,128)(4,1)S(1)}, pred[256,16]{0,1:T(8,128)(4,1)}, u32[]{:S(2)}) copy-start(pred[256,16]{0,1:T(8,128)(4,1)} %iota_compare_fusion.12) | copy-start | bytes 12292
  43.9 38.4 %all-to-all-start.2 = ((bf16[32,3,16,768]{3,2,1,0:T(8,128)(2,1)}), bf16[32,3,16,768]{3,2,1,0:T(8,128)(2,1)S(1)}, u32[]{:S(2)}, u32[]{:S(2)}) async-start(bf16[32,3,16,768]{3,2,1,0:T(8,128)(2,1)} %bitcast.44), calls=%async_computation.2 | async-start | bytes 4718592 | tf_op jit(solution)/shard_map/all_to_all | solution.py:132
  56.0 1.8 %copy-start.3 = (pred[32,16,256]{2,1,0:T(8,128)(4,1)S(1)}, pred[32,16,256]{2,1,0:T(8,128)(4,1)}, u32[]{:S(2)}) copy-start(pred[32,16,256]{2,1,0:T(8,128)(4,1)} %broadcast_and_fusion.1) | copy-start | bytes 393220
  56.0 2.2 %copy-start.6 = (bf16[11,768]{1,0:T(8,128)(2,1)S(1)}, bf16[11,768]{1,0:T(8,128)(2,1)}, u32[]{:S(2)}) copy-start(bf16[11,768]{1,0:T(8,128)(2,1)} %reshape.690) | copy-start | bytes 50692
  57.8 4.7 %copy-start.13 = (s32[256]{0:T(256)S(1)}, s32[256]{0:T(256)}, u32[]{:S(2)}) copy-start(s32[256]{0:T(256)} %copy-done.12) | copy-start | bytes 3076
  57.8 5.5 %copy-start.10 = (pred[256,16]{0,1:T(8,128)(4,1)S(1)}, pred[256,16]{0,1:T(8,128)(4,1)}, u32[]{:S(2)}) copy-start(pred[256,16]{0,1:T(8,128)(4,1)} %iota_compare_fusion.11) | copy-start | bytes 12292
  58.3 22.1 %collective-permute-start = (bf16[523,768]{1,0:T(8,128)(2,1)S(1)}, bf16[523,768]{1,0:T(8,128)(2,1)S(1)}, u32[]{:S(2)}, u32[]{:S(2)}) collective-permute-start(bf16[523,768]{1,0:T(8,128)(2,1)S(1)} %pad_maximum_fusion.4), channel_id=1, source_target_pairs={{0,32},{32,64},{64,96},{96,128},{128,160},{160,192},{192,224},{1,3... | collective-permute-start | bytes 2409992 | tf_op jit(solution)/shard_map/ppermute | solution.py:18
  64.0 25.7 %copy-start.11 = (pred[256,16]{0,1:T(8,128)(4,1)S(1)}, pred[256,16]{0,1:T(8,128)(4,1)}, u32[]{:S(2)}) copy-start(pred[256,16]{0,1:T(8,128)(4,1)} %iota_compare_fusion.11) | copy-start | bytes 12292
  80.4 0.9 copy-start.2
  82.3 21.6 %all-to-all-start.1 = ((bf16[32,1,16,768]{3,2,1,0:T(8,128)(2,1)}), bf16[32,1,16,768]{3,2,1,0:T(8,128)(2,1)S(1)}, u32[]{:S(2)}, u32[]{:S(2)}) async-start(bf16[32,1,16,768]{3,2,1,0:T(8,128)(2,1)} %bitcast.24), calls=%async_computation.1 | async-start | bytes 1572864 | tf_op jit(solution)/shard_map/all_to_all | solution.py:166
  90.5 0.8 copy-start.7
  93.2 1.9 %copy-start.15 = (f32[6,256,256]{1,2,0:T(8,128)S(1)}, f32[6,256,256]{1,2,0:T(8,128)}, u32[]{:S(2)}) copy-start(f32[6,256,256]{1,2,0:T(8,128)} %get-tuple-element.29) | copy-start | bytes 4718596
  96.4 2.0 %copy-start.5 = (pred[1,256,32,16]{1,2,3,0:T(32,128)(4,1)S(1)}, pred[1,256,32,16]{1,2,3,0:T(32,128)(4,1)}, u32[]{:S(2)}) copy-start(pred[1,256,32,16]{1,2,3,0:T(32,128)(4,1)} %broadcast_and_fusion) | copy-start | bytes 393220
  101.1 7.4 %copy-start.9 = (pred[8,16]{1,0:T(8,128)(4,1)S(1)}, pred[8,16]{1,0:T(8,128)(4,1)}, u32[]{:S(2)}) copy-start(pred[8,16]{1,0:T(8,128)(4,1)} %copy-done.8) | copy-start | bytes 388
  101.1 7.5 %slice-start = ((bf16[523,768]{1,0:T(8,128)(2,1)}), bf16[11,768]{1,0:T(8,128)(2,1)S(1)}, s32[]{:S(2)}) async-start(bf16[523,768]{1,0:T(8,128)(2,1)} %copy-done.2), calls=%async_computation.4 | async-start | bytes 49152 | tf_op jit(solution)/shard_map/slice | solution.py:160
  103.9 27.0 %all-to-all-start.3 = ((bf16[32,2,16,768]{3,2,1,0:T(8,128)(2,1)}), bf16[32,2,16,768]{3,2,1,0:T(8,128)(2,1)S(1)}, u32[]{:S(2)}, u32[]{:S(2)}) async-start(bf16[32,2,16,768]{3,2,1,0:T(8,128)(2,1)} %copy.138), calls=%async_computation.3 | async-start | bytes 3145728 | tf_op jit(solution)/shard_map/all_to_all | solution.py:141

commit v12 on v11

--- a/solution.py
+++ b/solution.py
@@ -145,7 +145,13 @@
 
     arrived_f = exchange((shared_fwd, values_fwd), own_f[0])
     rows_f = gather_block(arrived_f, own_f[1])
-    arrived_b = exchange((shared_bwd, values_bwd, upstream_bwd), next_b[0])
+    packed_b = jnp.einsum(
+        "skt,atf->skaf", next_b[0], inputs_b, preferred_element_type=jnp.bfloat16
+    ).reshape(seq_count, slot_count, 3, mp_count, group_features)
+    packed_b = jnp.transpose(packed_b, (0, 3, 2, 1, 4)).reshape(
+        group_count, 3, slot_count, group_features
+    )
+    arrived_b = lax.all_to_all(packed_b, axes, split_axis=0, concat_axis=0, tiled=True)
     attended = forward_block(rows_f[0], rows_f[1], own_f[2].reshape(-1, CLUSTER), score_scale)
     placed_f = jnp.einsum(
         "irk,if->rkf", own_f[1], attended.reshape(block_rows, group_features),

time: 134 us -> 135 us (level)
  local copies, waits for them, and re-layouts: 14.4 us -> 20.2 us
  waiting for transfers between devices: 49.2 us -> 47 us
  matrix products: 20.7 us -> 18.6 us
    all_to_all x0 -> x1, starting transfers between devices: none -> 7.45 us  [per_device(): lax.all_to_all(packed_b, axes, split_axis=0, concat_axis=0, tiled=True)]
    all_to_all x2 -> x1, starting transfers between devices: 14.6 us -> 7.43 us  [exchange(): lax.all_to_all(stacked, axes, split_axis=0, concat_axis=0, tiled=True)]
    dot_general x5 -> x2, matrix products: 5.06 us -> 0.83 us  [exchange(): jnp.einsum('skt,tf->skf', send, array[0], preferred_element_type=jnp.bflo...]
    transpose x0 -> x1, local copies, waits for them, and re-layouts: none -> 3.46 us  [per_device(): jnp.transpose(packed_b, (0, 3, 2, 1, 4))]
    reshape x0 -> x1, local copies, waits for them, and re-layouts: none -> 3 us  [per_device(): packed_b = jnp.einsum('skt,atf->skaf', next_b[0], inputs_b, preferred_ele...]
    dot_general x0 -> x1, matrix products: none -> 2.09 us  [per_device(): jnp.einsum('skt,atf->skaf', next_b[0], inputs_b, preferred_element_type=j...]
    all_to_all x1, waiting for transfers between devices: 21.1 us -> 19.1 us  [give_back(): lax.all_to_all(placed, axes, split_axis=0, concat_axis=0, tiled=True)]
    unnamed x33 -> x29, local copies, waits for them, and re-layouts: 2.98 us -> 0.92 us
  transfers between devices with their start and end apart: 7 -> 7, of which waited for: 4 -> 4; matrix products, arithmetic and copies ran while one was open for 32% -> 36% of each run, Pallas kernels for 0% -> 0%
where the time goes in v12:
time: 135 us; the launch traced here: 134 us
  waiting for transfers between devices  47 us (35%)
  starting transfers between devices  34.5 us (26%)
  local copies, waits for them, and re-layouts  20.2 us (15%)
  matrix products  18.6 us (14%)
  other arithmetic  12.6 us (9%)
    ppermute x3, waiting for transfers between devices, shifted(): return lax.ppermute(block, axis, route)  25.1 us
    all_to_all x1, waiting for transfers between devices, give_back(): lax.all_to_all(placed, axes, split_axis=0, concat_axis=0, tiled=True)  19.1 us
    ppermute x3, starting transfers between devices, shifted(): return lax.ppermute(block, axis, route)  7.81 us
    all_to_all x1, starting transfers between devices, per_device(): lax.all_to_all(packed_b, axes, split_axis=0, concat_axis=0, tiled=True)  7.45 us
    all_to_all x1, starting transfers between devices, exchange(): lax.all_to_all(stacked, axes, split_axis=0, concat_axis=0, tiled=True)  7.43 us
    all_to_all x1, starting transfers between devices, per_device(): lax.all_to_all(placed_f, axes, split_axis=0, concat_axis=0, tiled=True)  7.41 us
    sub x2, matrix products, softmax_weights(): exponent = jnp.exp(scores - largest)  4.57 us
    all_to_all x1, starting transfers between devices, give_back(): lax.all_to_all(placed, axes, split_axis=0, concat_axis=0, tiled=True)  4.39 us
  transfers between devices with their start and end apart: 7, of which 4 were waited for; matrix products, arithmetic and copies ran while one was open for 36% of the time, Pallas kernels for 0%

profile of v12, /device:TPU:96, one launch (start us, length us, event | category | flops | bytes accessed | tf_op | source)
XLA Modules:
  0.0 134.0 jit_solution(8950013259229386310)
XLA Ops:
  1.5 2.1 %collective-permute-start.1 = (s32[2048]{0:T(1024)S(1)}, s32[2048]{0:T(1024)S(1)}, u32[]{:S(2)}, u32[]{:S(2)}) collective-permute-start(s32[2048]{0:T(1024)S(1)} %bitcast.205), channel_id=1, source_target_pairs={{32,0},{64,32},{96,64},{128,96},{160,128},{192,160},{224,192},{33,... | collective-permute-start | bytes 24584 | tf_op jit(solution)/shard_map/ppermute | solution.py:18
  3.6 1.4 %pad_maximum_fusion.1 = bf16[3,64,3072]{2,1,0:T(8,128)(2,1)S(1)} fusion(bf16[1,64,3072]{2,1,0:T(8,128)(2,1)} %param.10, bf16[1,64,3072]{2,1,0:T(8,128)(2,1)} %param.9, bf16[1,64,3072]{2,1,0:T(8,128)(2,1)} %param.8), kind=kLoop, calls=%fused_computation.35 | loop fusion | flops 1179648 | bytes 2359296 | tf_op jit(solution)/shard_map/concatenate | solution.py:113
  5.0 2.0 %collective-permute-start.2 = (bf16[3,64,3072]{2,1,0:T(8,128)(2,1)S(1)}, bf16[3,64,3072]{2,1,0:T(8,128)(2,1)}, u32[]{:S(2)}, u32[]{:S(2)}) collective-permute-start(bf16[3,64,3072]{2,1,0:T(8,128)(2,1)S(1)} %pad_maximum_fusion.1), channel_id=1, source_target_pairs={{32,0},{64,32},{96,64},{128,96},{160,128},{192,160},{224,192},{33,... | collective-permute-start | bytes 3538952 | tf_op jit(solution)/shard_map/ppermute | solution.py:18
  10.9 7.4 %all-to-all-start = ((bf16[32,2,16,768]{3,2,1,0:T(8,128)(2,1)}), bf16[32,2,16,768]{3,2,1,0:T(8,128)(2,1)}, u32[]{:S(2)}, u32[]{:S(2)}) async-start(bf16[32,2,16,768]{3,2,1,0:T(8,128)(2,1)} %bitcast.12), calls=%async_computation | async-start | bytes 3145728 | tf_op jit(solution)/shard_map/all_to_all | solution.py:132
  27.4 8.6 %collective-permute-done.2 = bf16[3,64,3072]{2,1,0:T(8,128)(2,1)} collective-permute-done((bf16[3,64,3072]{2,1,0:T(8,128)(2,1)S(1)}, bf16[3,64,3072]{2,1,0:T(8,128)(2,1)}, u32[]{:S(2)}, u32[]{:S(2)}) %collective-permute-start.2) | collective-permute-done | bytes 1179680 | tf_op jit(solution)/shard_map/ppermute | solution.py:18
  36.0 2.1 %fusion.16 = bf16[8,16,3,3072]{3,1,2,0:T(8,128)(2,1)S(1)} fusion(bf16[3,64,3072]{2,1,0:T(8,128)(2,1)} %collective-permute-done.2, s32[8,16]{1,0:T(8,128)S(1)} %select_reduce_fusion, pred[8,16]{1,0:T(8,128)(4,1)S(1)} %fusion.52), kind=kOutput, calls=%fused_computation.36 | convolution fusion | flops 151011328 | bytes 3539584 | tf_op jit(solution)/shard_map/skt,atf->skaf/dot_general | solution.py:148
  38.1 3.0 %reshape.685 = bf16[8,16,3,4,768]{4,3,1,2,0:T(4,128)(2,1)} reshape(bf16[8,16,3,3072]{3,1,2,0:T(8,128)(2,1)S(1)} %fusion.16) | data formatting | bytes 4718592 | tf_op jit(solution)/shard_map/reshape | solution.py:150
  41.1 3.5 %copy.125 = bf16[8,4,3,16,768]{4,3,2,1,0:T(8,128)(2,1)} copy(bf16[8,4,3,16,768]{4,1,3,2,0:T(4,128)(2,1)} %bitcast.179) | data formatting | bytes 4718592 | tf_op jit(solution)/shard_map/transpose | solution.py:151
  44.6 7.5 %all-to-all-start.2 = ((bf16[32,3,16,768]{3,2,1,0:T(8,128)(2,1)}), bf16[32,3,16,768]{3,2,1,0:T(8,128)(2,1)S(1)}, u32[]{:S(2)}, u32[]{:S(2)}) async-start(bf16[32,3,16,768]{3,2,1,0:T(8,128)(2,1)} %bitcast.39), calls=%async_computation.2 | async-start | bytes 4718592 | tf_op jit(solution)/shard_map/all_to_all | solution.py:154
  52.1 2.0 %convolution_bitcast_fusion.5 = bf16[2,256,768]{1,2,0:T(8,128)(2,1)S(1)} fusion(bf16[32,2,16,768]{3,2,1,0:T(8,128)(2,1)} %all-to-all-done, pred[256,16]{0,1:T(8,128)(4,1)S(1)} %copy-done.12, pred[256,32]{0,1:T(8,128)(4,1)S(1)} %iota_compare_fusion.9), kind=kOutput, calls=%fused_computation.27 | convolution fusion | flops 402784256 | bytes 2371584 | tf_op jit(solution)/shard_map/irk,rakf->aif/dot_general | solution.py:136
  54.2 2.7 %fusion.101 = (f32[6,256]{1,0:T(8,128)S(1)}, f32[6,256,256]{1,2,0:T(8,128)}) fusion(bf16[256,6,128]{0,2,1:T(8,128)(2,1)S(1)} %bitcast.197, pred[256,256]{0,1:T(8,128)(4,1)} %fusion.43), kind=kOutput, calls=%fused_computation.183 | convolution fusion | flops 102236416 | bytes 2037760 | tf_op jit(solution)/shard_map/sub | solution.py:36
  56.9 1.7 %convolution_convert_fusion.1 = bf16[6,128,256]{2,1,0:T(8,128)(2,1)S(1)} fusion(bf16[256,6,128]{0,2,1:T(8,128)(2,1)S(1)} %bitcast.196, f32[6,256,256]{1,2,0:T(8,128)} %get-tuple-element.23, f32[6,256]{1,0:T(8,128)S(1)} %get-tuple-element.22), kind=kOutput, calls=%fused_computation.32 | convolution fusion | flops 101646336 | bytes 2365440 | tf_op jit(solution)/shard_map/nhqk,nkhd->nqhd/dot_general | solution.py:42
  59.1 3.6 %collective-permute-start = (bf16[523,768]{1,0:T(8,128)(2,1)S(1)}, bf16[523,768]{1,0:T(8,128)(2,1)}, u32[]{:S(2)}, u32[]{:S(2)}) collective-permute-start(bf16[523,768]{1,0:T(8,128)(2,1)S(1)} %pad_maximum_fusion.2), channel_id=1, source_target_pairs={{0,32},{32,64},{64,96},{96,128},{128,160},{160,192},{192,224},{1,3... | collective-permute-start | bytes 2409992 | tf_op jit(solution)/shard_map/ppermute | solution.py:18
  65.0 16.4 %collective-permute-done = bf16[523,768]{1,0:T(8,128)(2,1)} collective-permute-done((bf16[523,768]{1,0:T(8,128)(2,1)S(1)}, bf16[523,768]{1,0:T(8,128)(2,1)}, u32[]{:S(2)}, u32[]{:S(2)}) %collective-permute-start) | collective-permute-done | bytes 803360 | tf_op jit(solution)/shard_map/ppermute | solution.py:18
  81.4 2.1 %slice.103 = bf16[512,768]{1,0:T(8,128)(2,1)} slice(bf16[523,768]{1,0:T(8,128)(2,1)} %collective-permute-done), slice={[0:512], [0:768]} | slice | bytes 1572864 | tf_op jit(solution)/shard_map/slice | solution.py:169
  83.5 7.4 %all-to-all-start.1 = ((bf16[32,1,16,768]{3,2,1,0:T(8,128)(2,1)}), bf16[32,1,16,768]{3,2,1,0:T(8,128)(2,1)S(1)}, u32[]{:S(2)}, u32[]{:S(2)}) async-start(bf16[32,1,16,768]{3,2,1,0:T(8,128)(2,1)} %bitcast.24), calls=%async_computation.1 | async-start | bytes 1572864 | tf_op jit(solution)/shard_map/all_to_all | solution.py:172
  92.6 1.9 %fusion.102 = (f32[6,256]{1,0:T(8,128)S(1)}, f32[6,256,256]{1,2,0:T(8,128)}) fusion(pred[256,256]{0,1:T(8,128)(4,1)S(1)} %copy-done.5, bf16[256,6,128]{0,2,1:T(8,128)(2,1)S(1)} %bitcast.181), kind=kOutput, calls=%fused_computation.184 | convolution fusion | flops 102236416 | bytes 2037760 | tf_op jit(solution)/shard_map/sub | solution.py:36
  94.4 1.8 %fusion.15 = f32[256,6]{0,1:T(8,128)S(1)} fusion(bf16[256,6,128]{0,2,1:T(8,128)(2,1)S(1)} %bitcast.190, bf16[1,256,6,128]{1,3,2,0:T(8,128)(2,1)S(1)} %bitcast.187, f32[6,256,256]{1,2,0:T(8,128)} %get-tuple-element.25, f32[6,256]{1,0:T(8,128)S(1)} %get-tuple-element.24), kind=kOutput, calls=%fused_computation.33 | convolution fusion | flops 102038016 | bytes 2371584 | tf_op jit(solution)/shard_map/nhqk,nkhd->nqhd/dot_general | solution.py:50
  97.6 1.8 %convolution_convert_fusion = bf16[6,128,256]{2,1,0:T(8,128)(2,1)S(1)} fusion(bf16[256,6,128]{0,2,1:T(8,128)(2,1)S(1)} %bitcast.189, f32[6,256,256]{1,2,0:T(8,128)} %get-tuple-element.25, f32[6,256]{1,0:T(8,128)S(1)} %get-tuple-element.24), kind=kOutput, calls=%fused_computation.31 | convolution fusion | flops 101646336 | bytes 2365440 | tf_op jit(solution)/shard_map/nhqk,nqhd->nkhd/dot_general | solution.py:52
  100.3 2.0 %copy.138 = bf16[32,2,16,768]{3,2,1,0:T(8,128)(2,1)} copy(bf16[32,2,16,768]{3,0,2,1:T(8,128)(2,1)S(1)} %convolution_bitcast_fusion.2) | data formatting | bytes 3145728 | tf_op jit(solution)/shard_map/airk,aif->rakf/transpose | solution.py:140
  102.3 2.8 %all-to-all-done.1 = bf16[32,1,16,768]{3,2,1,0:T(8,128)(2,1)S(1)} async-done(((bf16[32,1,16,768]{3,2,1,0:T(8,128)(2,1)}), bf16[32,1,16,768]{3,2,1,0:T(8,128)(2,1)S(1)}, u32[]{:S(2)}, u32[]{:S(2)}) %all-to-all-start.1) | async-done | bytes 786464 | tf_op jit(solution)/shard_map/all_to_all | solution.py:172
  105.1 4.4 %all-to-all-start.3 = ((bf16[32,2,16,768]{3,2,1,0:T(8,128)(2,1)}), bf16[32,2,16,768]{3,2,1,0:T(8,128)(2,1)S(1)}, u32[]{:S(2)}, u32[]{:S(2)}) async-start(bf16[32,2,16,768]{3,2,1,0:T(8,128)(2,1)} %copy.138), calls=%async_computation.3 | async-start | bytes 3145728 | tf_op jit(solution)/shard_map/all_to_all | solution.py:141
  109.6 1.3 %slice.104 = bf16[11,768]{1,0:T(8,128)(2,1)} slice(bf16[523,768]{1,0:T(8,128)(2,1)} %collective-permute-done), slice={[512:523], [0:768]} | slice | bytes 33792 | tf_op jit(solution)/shard_map/slice | solution.py:166
  112.9 19.1 %all-to-all-done.3 = bf16[32,2,16,768]{3,2,1,0:T(8,128)(2,1)S(1)} async-done(((bf16[32,2,16,768]{3,2,1,0:T(8,128)(2,1)}), bf16[32,2,16,768]{3,2,1,0:T(8,128)(2,1)S(1)}, u32[]{:S(2)}, u32[]{:S(2)}) %all-to-all-start.3) | async-done | bytes 1572896 | tf_op jit(solution)/shard_map/all_to_all | solution.py:141
  (117 shorter events, 24.1 us)
Async XLA Ops:
  0.6 7.8 %copy-start = (bf16[1,64,3072]{2,1,0:T(8,128)(2,1)S(1)}, bf16[1,64,3072]{2,1,0:T(8,128)(2,1)}, u32[]{:S(2)}) copy-start(bf16[1,64,3072]{2,1,0:T(8,128)(2,1)} %param.7) | copy-start | bytes 1179652
  1.5 7.4 %copy-start.2 = (bf16[1,64,3072]{2,1,0:T(8,128)(2,1)S(1)}, bf16[1,64,3072]{2,1,0:T(8,128)(2,1)}, u32[]{:S(2)}) copy-start(bf16[1,64,3072]{2,1,0:T(8,128)(2,1)} %param.6) | copy-start | bytes 1179652
  1.5 22.1 %collective-permute-start.1 = (s32[2048]{0:T(1024)S(1)}, s32[2048]{0:T(1024)S(1)}, u32[]{:S(2)}, u32[]{:S(2)}) collective-permute-start(s32[2048]{0:T(1024)S(1)} %bitcast.205), channel_id=1, source_target_pairs={{32,0},{64,32},{96,64},{128,96},{160,128},{192,160},{224,192},{33,... | collective-permute-start | bytes 24584 | tf_op jit(solution)/shard_map/ppermute | solution.py:18
  5.0 31.0 %collective-permute-start.2 = (bf16[3,64,3072]{2,1,0:T(8,128)(2,1)S(1)}, bf16[3,64,3072]{2,1,0:T(8,128)(2,1)}, u32[]{:S(2)}, u32[]{:S(2)}) collective-permute-start(bf16[3,64,3072]{2,1,0:T(8,128)(2,1)S(1)} %pad_maximum_fusion.1), channel_id=1, source_target_pairs={{32,0},{64,32},{96,64},{128,96},{160,128},{192,160},{224,192},{33,... | collective-permute-start | bytes 3538952 | tf_op jit(solution)/shard_map/ppermute | solution.py:18
  10.9 33.7 %all-to-all-start = ((bf16[32,2,16,768]{3,2,1,0:T(8,128)(2,1)}), bf16[32,2,16,768]{3,2,1,0:T(8,128)(2,1)}, u32[]{:S(2)}, u32[]{:S(2)}) async-start(bf16[32,2,16,768]{3,2,1,0:T(8,128)(2,1)} %bitcast.12), calls=%async_computation | async-start | bytes 3145728 | tf_op jit(solution)/shard_map/all_to_all | solution.py:132
  26.1 1.2 copy-start.10
  26.5 11.6 %copy-start.8 = (pred[8,16]{1,0:T(8,128)(4,1)}, pred[8,16]{1,0:T(8,128)(4,1)S(1)}, u32[]{:S(2)}) copy-start(pred[8,16]{1,0:T(8,128)(4,1)S(1)} %fusion.52) | copy-start | bytes 388
  44.6 7.5 %copy-start.12 = (pred[256,16]{0,1:T(8,128)(4,1)S(1)}, pred[256,16]{0,1:T(8,128)(4,1)}, u32[]{:S(2)}) copy-start(pred[256,16]{0,1:T(8,128)(4,1)} %iota_compare_fusion.12) | copy-start | bytes 12292
  44.6 38.9 %all-to-all-start.2 = ((bf16[32,3,16,768]{3,2,1,0:T(8,128)(2,1)}), bf16[32,3,16,768]{3,2,1,0:T(8,128)(2,1)S(1)}, u32[]{:S(2)}, u32[]{:S(2)}) async-start(bf16[32,3,16,768]{3,2,1,0:T(8,128)(2,1)} %bitcast.39), calls=%async_computation.2 | async-start | bytes 4718592 | tf_op jit(solution)/shard_map/all_to_all | solution.py:154
  56.9 1.8 %copy-start.1 = (pred[32,16,256]{2,1,0:T(8,128)(4,1)S(1)}, pred[32,16,256]{2,1,0:T(8,128)(4,1)}, u32[]{:S(2)}) copy-start(pred[32,16,256]{2,1,0:T(8,128)(4,1)} %broadcast_and_fusion.1) | copy-start | bytes 393220
  56.9 2.2 %copy-start.4 = (bf16[11,768]{1,0:T(8,128)(2,1)S(1)}, bf16[11,768]{1,0:T(8,128)(2,1)}, u32[]{:S(2)}) copy-start(bf16[11,768]{1,0:T(8,128)(2,1)} %reshape.693) | copy-start | bytes 50692
  58.6 4.9 %copy-start.11 = (s32[256]{0:T(256)S(1)}, s32[256]{0:T(256)}, u32[]{:S(2)}) copy-start(s32[256]{0:T(256)} %copy-done.10) | copy-start | bytes 3076
  58.6 5.6 %copy-start.6 = (pred[256,16]{0,1:T(8,128)(4,1)S(1)}, pred[256,16]{0,1:T(8,128)(4,1)}, u32[]{:S(2)}) copy-start(pred[256,16]{0,1:T(8,128)(4,1)} %iota_compare_fusion.11) | copy-start | bytes 12292
  59.1 22.2 %collective-permute-start = (bf16[523,768]{1,0:T(8,128)(2,1)S(1)}, bf16[523,768]{1,0:T(8,128)(2,1)}, u32[]{:S(2)}, u32[]{:S(2)}) collective-permute-start(bf16[523,768]{1,0:T(8,128)(2,1)S(1)} %pad_maximum_fusion.2), channel_id=1, source_target_pairs={{0,32},{32,64},{64,96},{96,128},{128,160},{160,192},{192,224},{1,3... | collective-permute-start | bytes 2409992 | tf_op jit(solution)/shard_map/ppermute | solution.py:18
  65.0 25.9 %copy-start.7 = (pred[256,16]{0,1:T(8,128)(4,1)S(1)}, pred[256,16]{0,1:T(8,128)(4,1)}, u32[]{:S(2)}) copy-start(pred[256,16]{0,1:T(8,128)(4,1)} %iota_compare_fusion.11) | copy-start | bytes 12292
  83.5 21.6 %all-to-all-start.1 = ((bf16[32,1,16,768]{3,2,1,0:T(8,128)(2,1)}), bf16[32,1,16,768]{3,2,1,0:T(8,128)(2,1)S(1)}, u32[]{:S(2)}, u32[]{:S(2)}) async-start(bf16[32,1,16,768]{3,2,1,0:T(8,128)(2,1)} %bitcast.24), calls=%async_computation.1 | async-start | bytes 1572864 | tf_op jit(solution)/shard_map/all_to_all | solution.py:172
  91.7 0.8 copy-start.5
  94.4 1.9 %copy-start.13 = (f32[6,256,256]{1,2,0:T(8,128)S(1)}, f32[6,256,256]{1,2,0:T(8,128)}, u32[]{:S(2)}) copy-start(f32[6,256,256]{1,2,0:T(8,128)} %get-tuple-element.25) | copy-start | bytes 4718596
  97.6 2.0 %copy-start.3 = (pred[1,256,32,16]{1,2,3,0:T(32,128)(4,1)S(1)}, pred[1,256,32,16]{1,2,3,0:T(32,128)(4,1)}, u32[]{:S(2)}) copy-start(pred[1,256,32,16]{1,2,3,0:T(32,128)(4,1)} %broadcast_and_fusion) | copy-start | bytes 393220
  102.3 7.2 %copy-start.9 = (pred[8,16]{1,0:T(8,128)(4,1)S(1)}, pred[8,16]{1,0:T(8,128)(4,1)}, u32[]{:S(2)}) copy-start(pred[8,16]{1,0:T(8,128)(4,1)} %copy-done.8) | copy-start | bytes 388
  105.1 26.9 %all-to-all-start.3 = ((bf16[32,2,16,768]{3,2,1,0:T(8,128)(2,1)}), bf16[32,2,16,768]{3,2,1,0:T(8,128)(2,1)S(1)}, u32[]{:S(2)}, u32[]{:S(2)}) async-start(bf16[32,2,16,768]{3,2,1,0:T(8,128)(2,1)} %copy.138), calls=%async_computation.3 | async-start | bytes 3145728 | tf_op jit(solution)/shard_map/all_to_all | solution.py:141

commit v13 on v11

--- a/solution.py
+++ b/solution.py
@@ -110,8 +110,7 @@
     last_plane = pipe_index == lax.axis_size("pipe") - 1
     order_fwd = cluster_order[0, 0]
     order_next_bwd = shifted(cluster_order[0, 1], "pipe", -1)
-    inputs_b = shifted(jnp.concatenate([shared_bwd, values_bwd, upstream_bwd]), "pipe", -1)
-    shared_bwd, values_bwd, upstream_bwd = inputs_b[0:1], inputs_b[1:2], inputs_b[2:3]
+    shared_bwd, values_bwd, upstream_bwd = shifted((shared_bwd, values_bwd, upstream_bwd), "pipe", -1)
 
     def plan(order):
         return route_plan(order, seq_index, range_here, seq_count, group_count, tok_dev, slot_count)

time: 134 us -> 134 us (level)
  the two profiles are of different devices: /device:TPU:96 before, /device:TPU:224 now
where the time goes in v13:
time: 134 us; the launch traced here: 133 us
  waiting for transfers between devices  52.6 us (39%)
  starting transfers between devices  35.7 us (27%)
  matrix products  17.7 us (13%)
  local copies, waits for them, and re-layouts  14.4 us (11%)
  other arithmetic  11.6 us (9%)
    all_to_all x1, waiting for transfers between devices, give_back(): lax.all_to_all(placed, axes, split_axis=0, concat_axis=0, tiled=True)  21.1 us
    ppermute x5, waiting for transfers between devices, shifted(): return lax.ppermute(block, axis, route)  18.8 us
    ppermute x5, starting transfers between devices, shifted(): return lax.ppermute(block, axis, route)  12.1 us
    all_to_all x2, starting transfers between devices, exchange(): lax.all_to_all(stacked, axes, split_axis=0, concat_axis=0, tiled=True)  11.6 us
    all_to_all x2, waiting for transfers between devices, exchange(): lax.all_to_all(stacked, axes, split_axis=0, concat_axis=0, tiled=True)  9.83 us
    all_to_all x1, starting transfers between devices, per_device(): lax.all_to_all(placed_f, axes, split_axis=0, concat_axis=0, tiled=True)  7.42 us
    sub x2, matrix products, softmax_weights(): exponent = jnp.exp(scores - largest)  4.57 us
    all_to_all x1, starting transfers between devices, give_back(): lax.all_to_all(placed, axes, split_axis=0, concat_axis=0, tiled=True)  4.52 us
  transfers between devices with their start and end apart: 9, of which 4 were waited for; matrix products, arithmetic and copies ran while one was open for 29% of the time, Pallas kernels for 0%

profile of v13, /device:TPU:224, one launch (start us, length us, event | category | flops | bytes accessed | tf_op | source)
XLA Modules:
  0.0 133.3 jit_solution(15920204054841838108)
XLA Ops:
  1.5 2.9 %collective-permute-start.1 = (s32[2048]{0:T(1024)S(1)}, s32[2048]{0:T(1024)S(1)}, u32[]{:S(2)}, u32[]{:S(2)}) collective-permute-start(s32[2048]{0:T(1024)S(1)} %bitcast.209), channel_id=1, source_target_pairs={{32,0},{64,32},{96,64},{128,96},{160,128},{192,160},{224,192},{33,... | collective-permute-start | bytes 24584 | tf_op jit(solution)/shard_map/ppermute | solution.py:18
  4.4 2.9 %collective-permute-start.4 = (bf16[1,64,3072]{2,1,0:T(8,128)(2,1)}, bf16[1,64,3072]{2,1,0:T(8,128)(2,1)S(1)}, u32[]{:S(2)}, u32[]{:S(2)}) collective-permute-start(bf16[1,64,3072]{2,1,0:T(8,128)(2,1)} %param.10), channel_id=1, source_target_pairs={{32,0},{64,32},{96,64},{128,96},{160,128},{192,160},{224,192},{33,... | collective-permute-start | bytes 1179656 | tf_op jit(solution)/shard_map/ppermute | solution.py:18
  7.4 2.9 %collective-permute-start.3 = (bf16[1,64,3072]{2,1,0:T(8,128)(2,1)}, bf16[1,64,3072]{2,1,0:T(8,128)(2,1)S(1)}, u32[]{:S(2)}, u32[]{:S(2)}) collective-permute-start(bf16[1,64,3072]{2,1,0:T(8,128)(2,1)} %param.9), channel_id=1, source_target_pairs={{32,0},{64,32},{96,64},{128,96},{160,128},{192,160},{224,192},{33,... | collective-permute-start | bytes 1179656 | tf_op jit(solution)/shard_map/ppermute | solution.py:18
  10.3 2.0 %collective-permute-start.2 = (bf16[1,64,3072]{2,1,0:T(8,128)(2,1)}, bf16[1,64,3072]{2,1,0:T(8,128)(2,1)S(1)}, u32[]{:S(2)}, u32[]{:S(2)}) collective-permute-start(bf16[1,64,3072]{2,1,0:T(8,128)(2,1)} %param.8), channel_id=1, source_target_pairs={{32,0},{64,32},{96,64},{128,96},{160,128},{192,160},{224,192},{33,... | collective-permute-start | bytes 1179656 | tf_op jit(solution)/shard_map/ppermute | solution.py:18
  14.9 1.3 copy.118
  16.2 7.3 %all-to-all-start = ((bf16[32,2,16,768]{3,2,1,0:T(8,128)(2,1)}), bf16[32,2,16,768]{3,2,1,0:T(8,128)(2,1)S(1)}, u32[]{:S(2)}, u32[]{:S(2)}) async-start(bf16[32,2,16,768]{3,2,1,0:T(8,128)(2,1)} %bitcast.12), calls=%async_computation | async-start | bytes 3145728 | tf_op jit(solution)/shard_map/all_to_all | solution.py:131
  34.6 1.6 %copy.125 = bf16[8,12,16,768]{3,2,1,0:T(8,128)(2,1)} copy(bf16[8,12,16,768]{3,2,0,1:T(8,128)(2,1)S(1)} %pad_maximum_fusion.1) | data formatting | bytes 4718592 | tf_op jit(solution)/shard_map/concatenate.2
  36.2 9.8 %all-to-all-done = bf16[32,2,16,768]{3,2,1,0:T(8,128)(2,1)S(1)} async-done(((bf16[32,2,16,768]{3,2,1,0:T(8,128)(2,1)}), bf16[32,2,16,768]{3,2,1,0:T(8,128)(2,1)S(1)}, u32[]{:S(2)}, u32[]{:S(2)}) %all-to-all-start) | async-done | bytes 1572896 | tf_op jit(solution)/shard_map/all_to_all | solution.py:131
  46.0 1.2 copy-done.1
  47.2 4.3 %all-to-all-start.2 = ((bf16[32,3,16,768]{3,2,1,0:T(8,128)(2,1)}), bf16[32,3,16,768]{3,2,1,0:T(8,128)(2,1)S(1)}, u32[]{:S(2)}, u32[]{:S(2)}) async-start(bf16[32,3,16,768]{3,2,1,0:T(8,128)(2,1)} %bitcast.44), calls=%async_computation.2 | async-start | bytes 4718592 | tf_op jit(solution)/shard_map/all_to_all | solution.py:131
  51.5 2.0 %convolution_bitcast_fusion.8 = bf16[2,256,768]{1,2,0:T(8,128)(2,1)S(1)} fusion(bf16[32,2,16,768]{3,2,1,0:T(8,128)(2,1)} %copy-done.1, pred[256,16]{0,1:T(8,128)(4,1)} %iota_compare_fusion.12, pred[256,32]{0,1:T(8,128)(4,1)S(1)} %iota_compare_fusion.9), kind=kOutput, calls=%fused_computation.32 | convolution fusion | flops 402784256 | bytes 2371584 | tf_op jit(solution)/shard_map/irk,rakf->aif/dot_general | solution.py:135
  53.7 2.7 %fusion.108 = (f32[6,256]{1,0:T(8,128)S(1)}, f32[6,256,256]{1,2,0:T(8,128)}) fusion(bf16[256,6,128]{0,2,1:T(8,128)(2,1)S(1)} %bitcast.201, pred[256,256]{0,1:T(8,128)(4,1)} %fusion.44), kind=kOutput, calls=%fused_computation.192 | convolution fusion | flops 102236416 | bytes 2037760 | tf_op jit(solution)/shard_map/sub | solution.py:36
  56.4 1.7 %convolution_convert_fusion.1 = bf16[6,128,256]{2,1,0:T(8,128)(2,1)S(1)} fusion(bf16[256,6,128]{0,2,1:T(8,128)(2,1)S(1)} %bitcast.200, f32[6,256,256]{1,2,0:T(8,128)} %get-tuple-element.27, f32[6,256]{1,0:T(8,128)S(1)} %get-tuple-element.26), kind=kOutput, calls=%fused_computation.37 | convolution fusion | flops 101646336 | bytes 2365440 | tf_op jit(solution)/shard_map/nhqk,nkhd->nqhd/dot_general | solution.py:42
  58.6 1.3 collective-permute-start
  62.0 18.8 %collective-permute-done = bf16[523,768]{1,0:T(8,128)(2,1)S(1)} collective-permute-done((bf16[523,768]{1,0:T(8,128)(2,1)S(1)}, bf16[523,768]{1,0:T(8,128)(2,1)S(1)}, u32[]{:S(2)}, u32[]{:S(2)}) %collective-permute-start) | collective-permute-done | bytes 803360 | tf_op jit(solution)/shard_map/ppermute | solution.py:18
  81.7 0.9 slice.119
  82.6 7.4 %all-to-all-start.1 = ((bf16[32,1,16,768]{3,2,1,0:T(8,128)(2,1)}), bf16[32,1,16,768]{3,2,1,0:T(8,128)(2,1)S(1)}, u32[]{:S(2)}, u32[]{:S(2)}) async-start(bf16[32,1,16,768]{3,2,1,0:T(8,128)(2,1)} %bitcast.24), calls=%async_computation.1 | async-start | bytes 1572864 | tf_op jit(solution)/shard_map/all_to_all | solution.py:165
  91.7 1.9 %fusion.109 = (f32[6,256]{1,0:T(8,128)S(1)}, f32[6,256,256]{1,2,0:T(8,128)}) fusion(pred[256,256]{0,1:T(8,128)(4,1)S(1)} %copy-done.7, bf16[256,6,128]{0,2,1:T(8,128)(2,1)S(1)} %bitcast.185), kind=kOutput, calls=%fused_computation.193 | convolution fusion | flops 102236416 | bytes 2037760 | tf_op jit(solution)/shard_map/sub | solution.py:36
  93.6 1.8 %fusion.15 = f32[256,6]{0,1:T(8,128)S(1)} fusion(bf16[256,6,128]{0,2,1:T(8,128)(2,1)S(1)} %bitcast.194, bf16[1,256,6,128]{1,3,2,0:T(8,128)(2,1)S(1)} %bitcast.191, f32[6,256,256]{1,2,0:T(8,128)} %get-tuple-element.29, f32[6,256]{1,0:T(8,128)S(1)} %get-tuple-element.28), kind=kOutput, calls=%fused_computation.38 | convolution fusion | flops 102038016 | bytes 2371584 | tf_op jit(solution)/shard_map/nhqk,nkhd->nqhd/dot_general | solution.py:50
  96.8 1.8 %convolution_convert_fusion = bf16[6,128,256]{2,1,0:T(8,128)(2,1)S(1)} fusion(bf16[256,6,128]{0,2,1:T(8,128)(2,1)S(1)} %bitcast.193, f32[6,256,256]{1,2,0:T(8,128)} %get-tuple-element.29, f32[6,256]{1,0:T(8,128)S(1)} %get-tuple-element.28), kind=kOutput, calls=%fused_computation.36 | convolution fusion | flops 101646336 | bytes 2365440 | tf_op jit(solution)/shard_map/nhqk,nqhd->nkhd/dot_general | solution.py:52
  99.4 2.0 %copy.138 = bf16[32,2,16,768]{3,2,1,0:T(8,128)(2,1)} copy(bf16[32,2,16,768]{3,0,2,1:T(8,128)(2,1)S(1)} %convolution_bitcast_fusion.5) | data formatting | bytes 3145728 | tf_op jit(solution)/shard_map/airk,aif->rakf/transpose | solution.py:139
  101.4 2.8 %all-to-all-done.1 = bf16[32,1,16,768]{3,2,1,0:T(8,128)(2,1)S(1)} async-done(((bf16[32,1,16,768]{3,2,1,0:T(8,128)(2,1)}), bf16[32,1,16,768]{3,2,1,0:T(8,128)(2,1)S(1)}, u32[]{:S(2)}, u32[]{:S(2)}) %all-to-all-start.1) | async-done | bytes 786464 | tf_op jit(solution)/shard_map/all_to_all | solution.py:165
  104.2 4.5 %all-to-all-start.3 = ((bf16[32,2,16,768]{3,2,1,0:T(8,128)(2,1)}), bf16[32,2,16,768]{3,2,1,0:T(8,128)(2,1)S(1)}, u32[]{:S(2)}, u32[]{:S(2)}) async-start(bf16[32,2,16,768]{3,2,1,0:T(8,128)(2,1)} %copy.138), calls=%async_computation.3 | async-start | bytes 3145728 | tf_op jit(solution)/shard_map/all_to_all | solution.py:140
  110.1 21.1 %all-to-all-done.3 = bf16[32,2,16,768]{3,2,1,0:T(8,128)(2,1)S(1)} async-done(((bf16[32,2,16,768]{3,2,1,0:T(8,128)(2,1)}), bf16[32,2,16,768]{3,2,1,0:T(8,128)(2,1)S(1)}, u32[]{:S(2)}, u32[]{:S(2)}) %all-to-all-start.3) | async-done | bytes 1572896 | tf_op jit(solution)/shard_map/all_to_all | solution.py:140
  (127 shorter events, 24.8 us)
Async XLA Ops:
  0.6 13.1 %copy-start = (bf16[1,64,3072]{2,1,0:T(8,128)(2,1)S(1)}, bf16[1,64,3072]{2,1,0:T(8,128)(2,1)}, u32[]{:S(2)}) copy-start(bf16[1,64,3072]{2,1,0:T(8,128)(2,1)} %param.7) | copy-start | bytes 1179652
  0.6 13.5 %copy-start.4 = (bf16[1,64,3072]{2,1,0:T(8,128)(2,1)S(1)}, bf16[1,64,3072]{2,1,0:T(8,128)(2,1)}, u32[]{:S(2)}) copy-start(bf16[1,64,3072]{2,1,0:T(8,128)(2,1)} %param.6) | copy-start | bytes 1179652
  1.5 27.2 %collective-permute-start.1 = (s32[2048]{0:T(1024)S(1)}, s32[2048]{0:T(1024)S(1)}, u32[]{:S(2)}, u32[]{:S(2)}) collective-permute-start(s32[2048]{0:T(1024)S(1)} %bitcast.209), channel_id=1, source_target_pairs={{32,0},{64,32},{96,64},{128,96},{160,128},{192,160},{224,192},{33,... | collective-permute-start | bytes 24584 | tf_op jit(solution)/shard_map/ppermute | solution.py:18
  4.4 28.1 %collective-permute-start.4 = (bf16[1,64,3072]{2,1,0:T(8,128)(2,1)}, bf16[1,64,3072]{2,1,0:T(8,128)(2,1)S(1)}, u32[]{:S(2)}, u32[]{:S(2)}) collective-permute-start(bf16[1,64,3072]{2,1,0:T(8,128)(2,1)} %param.10), channel_id=1, source_target_pairs={{32,0},{64,32},{96,64},{128,96},{160,128},{192,160},{224,192},{33,... | collective-permute-start | bytes 1179656 | tf_op jit(solution)/shard_map/ppermute | solution.py:18
  7.4 25.5 %collective-permute-start.3 = (bf16[1,64,3072]{2,1,0:T(8,128)(2,1)}, bf16[1,64,3072]{2,1,0:T(8,128)(2,1)S(1)}, u32[]{:S(2)}, u32[]{:S(2)}) collective-permute-start(bf16[1,64,3072]{2,1,0:T(8,128)(2,1)} %param.9), channel_id=1, source_target_pairs={{32,0},{64,32},{96,64},{128,96},{160,128},{192,160},{224,192},{33,... | collective-permute-start | bytes 1179656 | tf_op jit(solution)/shard_map/ppermute | solution.py:18
  10.3 23.0 %collective-permute-start.2 = (bf16[1,64,3072]{2,1,0:T(8,128)(2,1)}, bf16[1,64,3072]{2,1,0:T(8,128)(2,1)S(1)}, u32[]{:S(2)}, u32[]{:S(2)}) collective-permute-start(bf16[1,64,3072]{2,1,0:T(8,128)(2,1)} %param.8), channel_id=1, source_target_pairs={{32,0},{64,32},{96,64},{128,96},{160,128},{192,160},{224,192},{33,... | collective-permute-start | bytes 1179656 | tf_op jit(solution)/shard_map/ppermute | solution.py:18
  16.2 29.8 %all-to-all-start = ((bf16[32,2,16,768]{3,2,1,0:T(8,128)(2,1)}), bf16[32,2,16,768]{3,2,1,0:T(8,128)(2,1)S(1)}, u32[]{:S(2)}, u32[]{:S(2)}) async-start(bf16[32,2,16,768]{3,2,1,0:T(8,128)(2,1)} %bitcast.12), calls=%async_computation | async-start | bytes 3145728 | tf_op jit(solution)/shard_map/all_to_all | solution.py:131
  29.5 1.9 %copy-start.12 = (s32[256]{0:T(256)}, s32[256]{0:T(256)S(1)}, u32[]{:S(2)}) copy-start(s32[256]{0:T(256)S(1)} %and_select_fusion) | copy-start | bytes 3076
  32.2 1.5 %copy-start.8 = (pred[8,16]{1,0:T(8,128)(4,1)}, pred[8,16]{1,0:T(8,128)(4,1)S(1)}, u32[]{:S(2)}) copy-start(pred[8,16]{1,0:T(8,128)(4,1)S(1)} %fusion.53) | copy-start | bytes 388
  46.0 1.2 copy-start.1
  47.2 35.4 %all-to-all-start.2 = ((bf16[32,3,16,768]{3,2,1,0:T(8,128)(2,1)}), bf16[32,3,16,768]{3,2,1,0:T(8,128)(2,1)S(1)}, u32[]{:S(2)}, u32[]{:S(2)}) async-start(bf16[32,3,16,768]{3,2,1,0:T(8,128)(2,1)} %bitcast.44), calls=%async_computation.2 | async-start | bytes 4718592 | tf_op jit(solution)/shard_map/all_to_all | solution.py:131
  56.4 1.8 %copy-start.3 = (pred[32,16,256]{2,1,0:T(8,128)(4,1)S(1)}, pred[32,16,256]{2,1,0:T(8,128)(4,1)}, u32[]{:S(2)}) copy-start(pred[32,16,256]{2,1,0:T(8,128)(4,1)} %broadcast_and_fusion.1) | copy-start | bytes 393220
  56.4 2.2 %copy-start.6 = (bf16[11,768]{1,0:T(8,128)(2,1)S(1)}, bf16[11,768]{1,0:T(8,128)(2,1)}, u32[]{:S(2)}) copy-start(bf16[11,768]{1,0:T(8,128)(2,1)} %reshape.690) | copy-start | bytes 50692
  58.1 2.4 %copy-start.13 = (s32[256]{0:T(256)S(1)}, s32[256]{0:T(256)}, u32[]{:S(2)}) copy-start(s32[256]{0:T(256)} %copy-done.12) | copy-start | bytes 3076
  58.1 3.1 %copy-start.10 = (pred[256,16]{0,1:T(8,128)(4,1)S(1)}, pred[256,16]{0,1:T(8,128)(4,1)}, u32[]{:S(2)}) copy-start(pred[256,16]{0,1:T(8,128)(4,1)} %iota_compare_fusion.11) | copy-start | bytes 12292
  58.6 22.1 %collective-permute-start = (bf16[523,768]{1,0:T(8,128)(2,1)S(1)}, bf16[523,768]{1,0:T(8,128)(2,1)S(1)}, u32[]{:S(2)}, u32[]{:S(2)}) collective-permute-start(bf16[523,768]{1,0:T(8,128)(2,1)S(1)} %pad_maximum_fusion.3), channel_id=1, source_target_pairs={{0,32},{32,64},{64,96},{96,128},{128,160},{160,192},{192,224},{1,3... | collective-permute-start | bytes 2409992 | tf_op jit(solution)/shard_map/ppermute | solution.py:18
  62.0 28.0 %copy-start.11 = (pred[256,16]{0,1:T(8,128)(4,1)S(1)}, pred[256,16]{0,1:T(8,128)(4,1)}, u32[]{:S(2)}) copy-start(pred[256,16]{0,1:T(8,128)(4,1)} %iota_compare_fusion.11) | copy-start | bytes 12292
  80.8 0.9 copy-start.2
  82.6 21.7 %all-to-all-start.1 = ((bf16[32,1,16,768]{3,2,1,0:T(8,128)(2,1)}), bf16[32,1,16,768]{3,2,1,0:T(8,128)(2,1)S(1)}, u32[]{:S(2)}, u32[]{:S(2)}) async-start(bf16[32,1,16,768]{3,2,1,0:T(8,128)(2,1)} %bitcast.24), calls=%async_computation.1 | async-start | bytes 1572864 | tf_op jit(solution)/shard_map/all_to_all | solution.py:165
  93.6 1.9 %copy-start.14 = (f32[6,256,256]{1,2,0:T(8,128)S(1)}, f32[6,256,256]{1,2,0:T(8,128)}, u32[]{:S(2)}) copy-start(f32[6,256,256]{1,2,0:T(8,128)} %get-tuple-element.29) | copy-start | bytes 4718596
  96.8 2.0 %copy-start.5 = (pred[1,256,32,16]{1,2,3,0:T(32,128)(4,1)S(1)}, pred[1,256,32,16]{1,2,3,0:T(32,128)(4,1)}, u32[]{:S(2)}) copy-start(pred[1,256,32,16]{1,2,3,0:T(32,128)(4,1)} %broadcast_and_fusion) | copy-start | bytes 393220
  101.4 7.3 %copy-start.9 = (pred[8,16]{1,0:T(8,128)(4,1)S(1)}, pred[8,16]{1,0:T(8,128)(4,1)}, u32[]{:S(2)}) copy-start(pred[8,16]{1,0:T(8,128)(4,1)} %copy-done.8) | copy-start | bytes 388
  101.4 7.5 %slice-start = ((bf16[523,768]{1,0:T(8,128)(2,1)}), bf16[11,768]{1,0:T(8,128)(2,1)S(1)}, s32[]{:S(2)}) async-start(bf16[523,768]{1,0:T(8,128)(2,1)} %copy-done.2), calls=%async_computation.4 | async-start | bytes 49152 | tf_op jit(solution)/shard_map/slice | solution.py:159
  104.2 27.0 %all-to-all-start.3 = ((bf16[32,2,16,768]{3,2,1,0:T(8,128)(2,1)}), bf16[32,2,16,768]{3,2,1,0:T(8,128)(2,1)S(1)}, u32[]{:S(2)}, u32[]{:S(2)}) async-start(bf16[32,2,16,768]{3,2,1,0:T(8,128)(2,1)} %copy.138), calls=%async_computation.3 | async-start | bytes 3145728 | tf_op jit(solution)/shard_map/all_to_all | solution.py:140
  (1 other events, 0.8 us)
